TPU v7x, 32 devices: a whole 2x2x4 slice. The times are simulated.
32 devices in a mesh: groups: 2 (over y), owner: 4 (over x, core), loop: 4 (over z).
Axes of the slice: x: 2, y: 2, z: 4, core: 2. Of those that a mesh axis runs over, the one named last changes fastest.
Arguments:
- emb: bfloat16 [8192, 1024], P(('groups', 'owner', 'loop')), parts along dimension 0, may hold values from -30 to 30
- row_owner: int32 [8192], P(('groups', 'owner', 'loop')), parts along dimension 0, may hold values from 0 to 3, as said below
- row_sub: int32 [8192], P(('groups', 'owner', 'loop')), parts along dimension 0, may hold values from 0 to 15, as said below
- cand: int32 [64, 32], P('groups'), parts along dimension 0, may hold values from 0 to 1, as said below
Outputs:
- dedup: bfloat16 [8192, 1024], P(('groups', 'owner', 'loop')), parts along dimension 0
There are 2 independent parts, one for each index of `groups`. A program takes and returns all parts, laid end to end along the dimension named above; each array names one. Nothing has to cross between parts.
Inputs may be any that keep to these rules, and one draw needn't show every extreme that they name: `row_owner`: among the documents of one device no owner appears more than 128 times, and on every device some owner appears exactly 128 times. Documents 2k and 2k + 1 have the same owner and cluster. Documents 2k and 2k + 1 have the same cluster. Among the documents of one device with one owner, no more than 32 have a row_sub of one value modulo 4, and on every device some owner and residue have exactly 32. cand is 1 on its diagonal.
All inputs are finite; a program needn't handle non-finite values.
Results may differ from a plain program's by a relative error of at most 0.0017.
Values may be sent and summed in bfloat16 or wider, within the bound.
No kernel may reach another device: no remote copies, remote signals or barrier semaphores. Data moves between devices by JAX's collectives and lax.ppermute only.
A program may use at most 64 MiB of HBM per device.

v0:
```python
import jax
import jax.numpy as jnp
from jax import lax
from jax.sharding import PartitionSpec as P

BLOCK = 128


def from_behind(x, axis, by):
    count = lax.axis_size(axis)
    return lax.ppermute(x, axis, [(i, (i + by) % count) for i in range(count)])


def describe(labels, position, slots, capacity, loop_count, local_blocks):
    local_block = labels[:, 0].astype(jnp.int32)
    cluster_sub = labels[:, 1].astype(jnp.int32)
    source_loop = position // slots
    source_owner = position % slots // capacity
    global_block = (source_owner * loop_count + source_loop) * local_blocks + local_block
    return (global_block, cluster_sub)


def candidate_rows(cand, global_block):
    clipped = jnp.clip(global_block, 0, cand.shape[0] - 1)
    return jnp.take(cand, clipped, axis=0).astype(jnp.bfloat16)


def contribute(
    carry, query_emb, query_rows, query_sub, query_pos, key_emb, key_block, key_sub, key_pos
):
    running_max, total, summed = carry
    scale = 4.0 / query_emb.shape[1]
    scores = scale * lax.dot_general(
        query_emb, key_emb, (((1,), (1,)), ((), ())), preferred_element_type=jnp.float32
    )
    key_onehot = (
        key_block[None, :] == jnp.arange(query_rows.shape[1], dtype=jnp.int32)[:, None]
    ).astype(jnp.bfloat16)
    near = jnp.dot(query_rows, key_onehot, preferred_element_type=jnp.float32) > 0.5
    present = (query_sub >= 0)[:, None] & (key_sub >= 0)[None, :]
    same = (query_pos[:, None] == key_pos[None, :]) | (
        query_sub[:, None] == key_sub[None, :]
    ) & near
    allowed = present & same
    top = jnp.max(jnp.where(allowed, scores, jnp.float32(-1e30)), axis=1)
    new_max = jnp.maximum(running_max, top)
    weights = jnp.where(allowed, jnp.exp(scores - new_max[:, None]), jnp.float32(0.0))
    rescale = jnp.exp(running_max - new_max)
    total = total * rescale + jnp.sum(weights, axis=1)
    summed = summed * rescale[:, None] + jnp.dot(
        weights.astype(jnp.bfloat16), key_emb, preferred_element_type=jnp.float32
    )
    return (new_max, total, summed)


def finish(summed, total):
    return (summed / jnp.where(total > 0.0, total, 1.0)[:, None]).astype(jnp.bfloat16)


def body(emb, row_owner, row_sub, cand):
    local_rows = emb.shape[0]
    owner_count = lax.axis_size("owner")
    loop_count = lax.axis_size("loop")
    loop_index = lax.axis_index("loop")
    capacity = 2 * local_rows // owner_count
    slots = owner_count * capacity
    local_blocks = local_rows // BLOCK
    dest_onehot = (row_owner[:, None] == jnp.arange(owner_count, dtype=jnp.int32)[None, :]).astype(
        jnp.int32
    )
    earlier = jnp.cumsum(dest_onehot, axis=0) - dest_onehot
    within = jnp.sum(earlier * dest_onehot, axis=1)
    slot_of_row = row_owner * capacity + within
    placing = (jnp.arange(slots, dtype=jnp.int32)[:, None] == slot_of_row[None, :]).astype(
        jnp.bfloat16
    )
    send_emb = jnp.dot(placing, emb, preferred_element_type=jnp.float32).astype(jnp.bfloat16)
    row_labels = jnp.stack(
        [jnp.arange(local_rows, dtype=jnp.int32) // BLOCK, row_sub + 1], axis=1
    ).astype(jnp.bfloat16)
    send_labels = (
        jnp.dot(placing, row_labels, preferred_element_type=jnp.float32)
        - jnp.array([0.0, 1.0], jnp.float32)[None, :]
    )
    send_labels = send_labels.astype(jnp.bfloat16)
    owned_emb, owned_labels = (
        lax.all_to_all(send_emb, "owner", split_axis=0, concat_axis=0, tiled=True),
        lax.all_to_all(send_labels, "owner", split_axis=0, concat_axis=0, tiled=True),
    )
    home_pos = loop_index * slots + jnp.arange(slots, dtype=jnp.int32)
    home_block, home_sub = describe(
        owned_labels, home_pos, slots, capacity, loop_count, local_blocks
    )
    width = emb.shape[1]

    def one_turn(turn, state):
        visit_emb, visit_labels, running_max, total, summed = state
        anchor = (loop_index - turn) % loop_count
        visit_pos = anchor * slots + jnp.arange(slots, dtype=jnp.int32)
        visit_block, visit_sub = describe(
            visit_labels, visit_pos, slots, capacity, loop_count, local_blocks
        )
        visit_rows = candidate_rows(cand, visit_block)
        running_max, total, summed = contribute(
            (running_max, total, summed),
            visit_emb,
            visit_rows,
            visit_sub,
            visit_pos,
            owned_emb,
            home_block,
            home_sub,
            home_pos,
        )
        visit_emb, visit_labels = from_behind((visit_emb, visit_labels), "loop", 1)
        running_max, total, summed = from_behind((running_max, total, summed), "loop", 1)
        return (visit_emb, visit_labels, running_max, total, summed)

    final = lax.fori_loop(
        0,
        loop_count,
        one_turn,
        (owned_emb, owned_labels)
        + (
            jnp.full((slots,), -1e30, jnp.float32),
            jnp.zeros((slots,), jnp.float32),
            jnp.zeros((slots, width), jnp.float32),
        ),
    )
    averaged = finish(final[4], final[3])
    returned = lax.all_to_all(averaged, "owner", split_axis=0, concat_axis=0, tiled=True)
    result = lax.dot_general(
        placing, returned, (((0,), (0,)), ((), ())), preferred_element_type=jnp.float32
    )
    return result.astype(jnp.bfloat16)


def solution(mesh):
    return jax.shard_map(
        body,
        mesh=mesh,
        in_specs=(
            P(("groups", "owner", "loop"), None),
            P(("groups", "owner", "loop")),
            P(("groups", "owner", "loop")),
            P("groups", None),
        ),
        out_specs=P(("groups", "owner", "loop"), None),
        check_vma=False,
    )
```

profile of v0, /device:TPU:1, one launch (start us, length us, event | category | flops | bytes accessed | tf_op | source)
XLA Modules:
  0.0 370.4 jit_solution(17943713336354084027)
XLA Ops:
  5.2 4.3 %all-to-all-start.1 = ((bf16[4,128,2]{1,2,0:T(2,128)(2,1)}), bf16[4,128,2]{1,2,0:T(2,128)(2,1)S(1)}, u32[]{:S(2)}, u32[]{:S(2)}) async-start(bf16[4,128,2]{1,2,0:T(2,128)(2,1)} %fusion.16), calls=%async_computation.1 | async-start | bytes 4096 | tf_op jit(solution)/shard_map/all_to_all | solution.py:88
  9.5 1.4 convolution_convert_fusion
  10.9 1.6 all-to-all-done.1
  12.5 4.2 %all-to-all-start = ((bf16[4,128,1024]{2,1,0:T(8,128)(2,1)}), bf16[4,128,1024]{2,1,0:T(8,128)(2,1)S(1)}, u32[]{:S(2)}, u32[]{:S(2)}) async-start(bf16[4,128,1024]{2,1,0:T(8,128)(2,1)} %bitcast.3), calls=%async_computation | async-start | bytes 2097152 | tf_op jit(solution)/shard_map/all_to_all | solution.py:87
  16.7 13.4 %all-to-all-done = bf16[4,128,1024]{2,1,0:T(8,128)(2,1)S(1)} async-done(((bf16[4,128,1024]{2,1,0:T(8,128)(2,1)}), bf16[4,128,1024]{2,1,0:T(8,128)(2,1)S(1)}, u32[]{:S(2)}, u32[]{:S(2)}) %all-to-all-start) | async-done | bytes 1048608 | tf_op jit(solution)/shard_map/all_to_all | solution.py:87
  31.7 316.7 %while.25 = (s32[]{:T(128)}, bf16[512,1024]{1,0:T(8,128)(2,1)}, bf16[512,2]{0,1:T(2,128)(2,1)S(1)}, f32[512]{0:T(512)S(1)}, f32[512]{0:T(512)S(1)}, /*index=5*/f...) while((s32[]{:T(128)}, bf16[512,1024]{1,0:T(8,128)(2,1)}, ...), condition=%wide.region_6.7_spmd.clone, body=%wide.region_3.6_spmd.clone.sunk | while | flops 1095840256 | bytes 31484432 | solution.py:119
  31.9 2.3 copy.22
  35.2 2.3 convolution_multiply_fusion.2
  38.7 2.1 multiply_add_fusion.6
  40.9 1.7 collective-permute-start.4
  42.6 1.3 collective-permute-start
  43.9 1.3 collective-permute-start.2
  45.2 1.2 collective-permute-start.1
  46.4 66.0 %collective-permute-done.2 = f32[512]{0:T(512)S(1)} collective-permute-done((f32[512]{0:T(512)S(1)}, f32[512]{0:T(512)S(1)}, u32[]{:S(2)}, u32[]{:S(2)}) %collective-permute-start.2) | collective-permute-done | bytes 2080 | tf_op jit(solution)/shard_map/while/body/eval_jaxpr/ppermute | solution.py:11
  112.7 2.3 copy.22
  116.0 2.3 convolution_multiply_fusion.2
  119.6 2.1 multiply_add_fusion.6
  122.1 1.3 collective-permute-start.2
  123.4 2.1 collective-permute-start.3
  125.5 66.4 %collective-permute-done.2 = f32[512]{0:T(512)S(1)} collective-permute-done((f32[512]{0:T(512)S(1)}, f32[512]{0:T(512)S(1)}, u32[]{:S(2)}, u32[]{:S(2)}) %collective-permute-start.2) | collective-permute-done | bytes 2080 | tf_op jit(solution)/shard_map/while/body/eval_jaxpr/ppermute | solution.py:11
  192.2 2.3 copy.22
  195.5 2.3 convolution_multiply_fusion.2
  199.0 2.1 multiply_add_fusion.6
  201.2 3.8 %collective-permute-start.3 = (f32[512]{0:T(512)S(1)}, f32[512]{0:T(512)S(1)}, u32[]{:S(2)}, u32[]{:S(2)}) collective-permute-start(f32[512]{0:T(512)S(1)} %get-tuple-element.487), channel_id=1, source_target_pairs={{0,1},{1,2},{2,3},{3,0},{4,5},{5,6},{6,7},{7,4},{8,9},{9,10},{10,1... | collective-permute-start | bytes 6152 | tf_op jit(solution)/shard_map/while/body/eval_jaxpr/ppermute | solution.py:11
  205.0 65.6 %collective-permute-done.2 = f32[512]{0:T(512)S(1)} collective-permute-done((f32[512]{0:T(512)S(1)}, f32[512]{0:T(512)S(1)}, u32[]{:S(2)}, u32[]{:S(2)}) %collective-permute-start.2) | collective-permute-done | bytes 2080 | tf_op jit(solution)/shard_map/while/body/eval_jaxpr/ppermute | solution.py:11
  270.8 2.3 copy.22
  274.1 2.3 convolution_multiply_fusion.2
  277.7 2.1 multiply_add_fusion.6
  279.8 3.8 %collective-permute-start.3 = (f32[512]{0:T(512)S(1)}, f32[512]{0:T(512)S(1)}, u32[]{:S(2)}, u32[]{:S(2)}) collective-permute-start(f32[512]{0:T(512)S(1)} %get-tuple-element.487), channel_id=1, source_target_pairs={{0,1},{1,2},{2,3},{3,0},{4,5},{5,6},{6,7},{7,4},{8,9},{9,10},{10,1... | collective-permute-start | bytes 6152 | tf_op jit(solution)/shard_map/while/body/eval_jaxpr/ppermute | solution.py:11
  283.6 64.7 %collective-permute-done.2 = f32[512]{0:T(512)S(1)} collective-permute-done((f32[512]{0:T(512)S(1)}, f32[512]{0:T(512)S(1)}, u32[]{:S(2)}, u32[]{:S(2)}) %collective-permute-start.2) | collective-permute-done | bytes 2080 | tf_op jit(solution)/shard_map/while/body/eval_jaxpr/ppermute | solution.py:11
  348.8 20.4 %all_to_all.36 = bf16[4,128,1024]{2,1,0:T(8,128)(2,1)S(1)} all-to-all(bf16[4,128,1024]{2,1,0:T(8,128)(2,1)S(1)} %bitcast.49), channel_id=1, replica_groups=mesh['groups'=2,'owner'=4,'loop'=4] {'owner'}, dimensions={0} | all-to-all | bytes 2097152 | tf_op jit(solution)/shard_map/all_to_all | solution.py:131
  369.1 1.3 convolution_convert_fusion.1
  (112 shorter events, 17.4 us)
Async XLA Ops:
  0.0 9.5 %copy-start = (bf16[256,1024]{1,0:T(8,128)(2,1)S(1)}, bf16[256,1024]{1,0:T(8,128)(2,1)}, u32[]{:S(2)}) copy-start(bf16[256,1024]{1,0:T(8,128)(2,1)} %param.7) | copy-start | bytes 1572868
  5.2 7.3 %all-to-all-start.1 = ((bf16[4,128,2]{1,2,0:T(2,128)(2,1)}), bf16[4,128,2]{1,2,0:T(2,128)(2,1)S(1)}, u32[]{:S(2)}, u32[]{:S(2)}) async-start(bf16[4,128,2]{1,2,0:T(2,128)(2,1)} %fusion.16), calls=%async_computation.1 | async-start | bytes 4096 | tf_op jit(solution)/shard_map/all_to_all | solution.py:88
  12.5 17.6 %all-to-all-start = ((bf16[4,128,1024]{2,1,0:T(8,128)(2,1)}), bf16[4,128,1024]{2,1,0:T(8,128)(2,1)S(1)}, u32[]{:S(2)}, u32[]{:S(2)}) async-start(bf16[4,128,1024]{2,1,0:T(8,128)(2,1)} %bitcast.3), calls=%async_computation | async-start | bytes 2097152 | tf_op jit(solution)/shard_map/all_to_all | solution.py:87
  30.1 1.3 copy-start.2
  30.1 1.6 copy-start.1
  37.5 1.2 copy-start.3
  40.9 71.7 %collective-permute-start.4 = (f32[512,1024]{1,0:T(8,128)}, f32[512,1024]{1,0:T(8,128)S(1)}, u32[]{:S(2)}, u32[]{:S(2)}) collective-permute-start(f32[512,1024]{1,0:T(8,128)} %multiply_add_fusion.6), channel_id=1, source_target_pairs={{0,1},{1,2},{2,3},{3,0},{4,5},{5,6},{6,7},{7,4},{8,9},{9,10},{10,1... | collective-permute-start | bytes 6291464 | tf_op jit(solution)/shard_map/while/body/eval_jaxpr/ppermute | solution.py:11
  42.6 70.0 %collective-permute-start = (bf16[512,1024]{1,0:T(8,128)(2,1)}, bf16[512,1024]{1,0:T(8,128)(2,1)}, u32[]{:S(2)}, u32[]{:S(2)}) collective-permute-start(bf16[512,1024]{1,0:T(8,128)(2,1)} %copy.22), channel_id=1, source_target_pairs={{0,1},{1,2},{2,3},{3,0},{4,5},{5,6},{6,7},{7,4},{8,9},{9,10},{10,1... | collective-permute-start | bytes 3145736 | tf_op jit(solution)/shard_map/while/body/eval_jaxpr/ppermute | solution.py:11
  43.9 68.6 %collective-permute-start.2 = (f32[512]{0:T(512)S(1)}, f32[512]{0:T(512)S(1)}, u32[]{:S(2)}, u32[]{:S(2)}) collective-permute-start(f32[512]{0:T(512)S(1)} %max.19), channel_id=1, source_target_pairs={{0,1},{1,2},{2,3},{3,0},{4,5},{5,6},{6,7},{7,4},{8,9},{9,10},{10,1... | collective-permute-start | bytes 6152 | tf_op jit(solution)/shard_map/while/body/eval_jaxpr/ppermute | solution.py:11
  45.2 67.3 %collective-permute-start.3 = (f32[512]{0:T(512)S(1)}, f32[512]{0:T(512)S(1)}, u32[]{:S(2)}, u32[]{:S(2)}) collective-permute-start(f32[512]{0:T(512)S(1)} %get-tuple-element.487), channel_id=1, source_target_pairs={{0,1},{1,2},{2,3},{3,0},{4,5},{5,6},{6,7},{7,4},{8,9},{9,10},{10,1... | collective-permute-start | bytes 6152 | tf_op jit(solution)/shard_map/while/body/eval_jaxpr/ppermute | solution.py:11
  45.2 67.4 %collective-permute-start.1 = (bf16[512,2]{0,1:T(2,128)(2,1)S(1)}, bf16[512,2]{0,1:T(2,128)(2,1)S(1)}, u32[]{:S(2)}, u32[]{:S(2)}) collective-permute-start(bf16[512,2]{0,1:T(2,128)(2,1)S(1)} %copy.23), channel_id=1, source_target_pairs={{0,1},{1,2},{2,3},{3,0},{4,5},{5,6},{6,7},{7,4},{8,9},{9,10},{10,1... | collective-permute-start | bytes 6152 | tf_op jit(solution)/shard_map/while/body/eval_jaxpr/ppermute | solution.py:11
  118.3 1.2 copy-start.3
  121.7 70.4 %collective-permute-start.4 = (f32[512,1024]{1,0:T(8,128)}, f32[512,1024]{1,0:T(8,128)S(1)}, u32[]{:S(2)}, u32[]{:S(2)}) collective-permute-start(f32[512,1024]{1,0:T(8,128)} %multiply_add_fusion.6), channel_id=1, source_target_pairs={{0,1},{1,2},{2,3},{3,0},{4,5},{5,6},{6,7},{7,4},{8,9},{9,10},{10,1... | collective-permute-start | bytes 6291464 | tf_op jit(solution)/shard_map/while/body/eval_jaxpr/ppermute | solution.py:11
  121.7 70.4 %collective-permute-start = (bf16[512,1024]{1,0:T(8,128)(2,1)}, bf16[512,1024]{1,0:T(8,128)(2,1)}, u32[]{:S(2)}, u32[]{:S(2)}) collective-permute-start(bf16[512,1024]{1,0:T(8,128)(2,1)} %copy.22), channel_id=1, source_target_pairs={{0,1},{1,2},{2,3},{3,0},{4,5},{5,6},{6,7},{7,4},{8,9},{9,10},{10,1... | collective-permute-start | bytes 3145736 | tf_op jit(solution)/shard_map/while/body/eval_jaxpr/ppermute | solution.py:11
  122.1 69.8 %collective-permute-start.2 = (f32[512]{0:T(512)S(1)}, f32[512]{0:T(512)S(1)}, u32[]{:S(2)}, u32[]{:S(2)}) collective-permute-start(f32[512]{0:T(512)S(1)} %max.19), channel_id=1, source_target_pairs={{0,1},{1,2},{2,3},{3,0},{4,5},{5,6},{6,7},{7,4},{8,9},{9,10},{10,1... | collective-permute-start | bytes 6152 | tf_op jit(solution)/shard_map/while/body/eval_jaxpr/ppermute | solution.py:11
  123.4 68.6 %collective-permute-start.3 = (f32[512]{0:T(512)S(1)}, f32[512]{0:T(512)S(1)}, u32[]{:S(2)}, u32[]{:S(2)}) collective-permute-start(f32[512]{0:T(512)S(1)} %get-tuple-element.487), channel_id=1, source_target_pairs={{0,1},{1,2},{2,3},{3,0},{4,5},{5,6},{6,7},{7,4},{8,9},{9,10},{10,1... | collective-permute-start | bytes 6152 | tf_op jit(solution)/shard_map/while/body/eval_jaxpr/ppermute | solution.py:11
  125.5 66.5 %collective-permute-start.1 = (bf16[512,2]{0,1:T(2,128)(2,1)S(1)}, bf16[512,2]{0,1:T(2,128)(2,1)S(1)}, u32[]{:S(2)}, u32[]{:S(2)}) collective-permute-start(bf16[512,2]{0,1:T(2,128)(2,1)S(1)} %copy.23), channel_id=1, source_target_pairs={{0,1},{1,2},{2,3},{3,0},{4,5},{5,6},{6,7},{7,4},{8,9},{9,10},{10,1... | collective-permute-start | bytes 6152 | tf_op jit(solution)/shard_map/while/body/eval_jaxpr/ppermute | solution.py:11
  197.8 1.2 copy-start.3
  201.2 69.5 %collective-permute-start.4 = (f32[512,1024]{1,0:T(8,128)}, f32[512,1024]{1,0:T(8,128)S(1)}, u32[]{:S(2)}, u32[]{:S(2)}) collective-permute-start(f32[512,1024]{1,0:T(8,128)} %multiply_add_fusion.6), channel_id=1, source_target_pairs={{0,1},{1,2},{2,3},{3,0},{4,5},{5,6},{6,7},{7,4},{8,9},{9,10},{10,1... | collective-permute-start | bytes 6291464 | tf_op jit(solution)/shard_map/while/body/eval_jaxpr/ppermute | solution.py:11
  201.2 69.5 %collective-permute-start = (bf16[512,1024]{1,0:T(8,128)(2,1)}, bf16[512,1024]{1,0:T(8,128)(2,1)}, u32[]{:S(2)}, u32[]{:S(2)}) collective-permute-start(bf16[512,1024]{1,0:T(8,128)(2,1)} %copy.22), channel_id=1, source_target_pairs={{0,1},{1,2},{2,3},{3,0},{4,5},{5,6},{6,7},{7,4},{8,9},{9,10},{10,1... | collective-permute-start | bytes 3145736 | tf_op jit(solution)/shard_map/while/body/eval_jaxpr/ppermute | solution.py:11
  201.2 69.4 %collective-permute-start.2 = (f32[512]{0:T(512)S(1)}, f32[512]{0:T(512)S(1)}, u32[]{:S(2)}, u32[]{:S(2)}) collective-permute-start(f32[512]{0:T(512)S(1)} %max.19), channel_id=1, source_target_pairs={{0,1},{1,2},{2,3},{3,0},{4,5},{5,6},{6,7},{7,4},{8,9},{9,10},{10,1... | collective-permute-start | bytes 6152 | tf_op jit(solution)/shard_map/while/body/eval_jaxpr/ppermute | solution.py:11
  201.2 69.5 %collective-permute-start.3 = (f32[512]{0:T(512)S(1)}, f32[512]{0:T(512)S(1)}, u32[]{:S(2)}, u32[]{:S(2)}) collective-permute-start(f32[512]{0:T(512)S(1)} %get-tuple-element.487), channel_id=1, source_target_pairs={{0,1},{1,2},{2,3},{3,0},{4,5},{5,6},{6,7},{7,4},{8,9},{9,10},{10,1... | collective-permute-start | bytes 6152 | tf_op jit(solution)/shard_map/while/body/eval_jaxpr/ppermute | solution.py:11
  205.0 65.7 %collective-permute-start.1 = (bf16[512,2]{0,1:T(2,128)(2,1)S(1)}, bf16[512,2]{0,1:T(2,128)(2,1)S(1)}, u32[]{:S(2)}, u32[]{:S(2)}) collective-permute-start(bf16[512,2]{0,1:T(2,128)(2,1)S(1)} %copy.23), channel_id=1, source_target_pairs={{0,1},{1,2},{2,3},{3,0},{4,5},{5,6},{6,7},{7,4},{8,9},{9,10},{10,1... | collective-permute-start | bytes 6152 | tf_op jit(solution)/shard_map/while/body/eval_jaxpr/ppermute | solution.py:11
  276.4 1.2 copy-start.3
  279.8 68.7 %collective-permute-start.4 = (f32[512,1024]{1,0:T(8,128)}, f32[512,1024]{1,0:T(8,128)S(1)}, u32[]{:S(2)}, u32[]{:S(2)}) collective-permute-start(f32[512,1024]{1,0:T(8,128)} %multiply_add_fusion.6), channel_id=1, source_target_pairs={{0,1},{1,2},{2,3},{3,0},{4,5},{5,6},{6,7},{7,4},{8,9},{9,10},{10,1... | collective-permute-start | bytes 6291464 | tf_op jit(solution)/shard_map/while/body/eval_jaxpr/ppermute | solution.py:11
  279.8 68.7 %collective-permute-start = (bf16[512,1024]{1,0:T(8,128)(2,1)}, bf16[512,1024]{1,0:T(8,128)(2,1)}, u32[]{:S(2)}, u32[]{:S(2)}) collective-permute-start(bf16[512,1024]{1,0:T(8,128)(2,1)} %copy.22), channel_id=1, source_target_pairs={{0,1},{1,2},{2,3},{3,0},{4,5},{5,6},{6,7},{7,4},{8,9},{9,10},{10,1... | collective-permute-start | bytes 3145736 | tf_op jit(solution)/shard_map/while/body/eval_jaxpr/ppermute | solution.py:11
  279.8 68.6 %collective-permute-start.2 = (f32[512]{0:T(512)S(1)}, f32[512]{0:T(512)S(1)}, u32[]{:S(2)}, u32[]{:S(2)}) collective-permute-start(f32[512]{0:T(512)S(1)} %max.19), channel_id=1, source_target_pairs={{0,1},{1,2},{2,3},{3,0},{4,5},{5,6},{6,7},{7,4},{8,9},{9,10},{10,1... | collective-permute-start | bytes 6152 | tf_op jit(solution)/shard_map/while/body/eval_jaxpr/ppermute | solution.py:11
  279.8 68.6 %collective-permute-start.3 = (f32[512]{0:T(512)S(1)}, f32[512]{0:T(512)S(1)}, u32[]{:S(2)}, u32[]{:S(2)}) collective-permute-start(f32[512]{0:T(512)S(1)} %get-tuple-element.487), channel_id=1, source_target_pairs={{0,1},{1,2},{2,3},{3,0},{4,5},{5,6},{6,7},{7,4},{8,9},{9,10},{10,1... | collective-permute-start | bytes 6152 | tf_op jit(solution)/shard_map/while/body/eval_jaxpr/ppermute | solution.py:11
  283.6 64.8 %collective-permute-start.1 = (bf16[512,2]{0,1:T(2,128)(2,1)S(1)}, bf16[512,2]{0,1:T(2,128)(2,1)S(1)}, u32[]{:S(2)}, u32[]{:S(2)}) collective-permute-start(bf16[512,2]{0,1:T(2,128)(2,1)S(1)} %copy.23), channel_id=1, source_target_pairs={{0,1},{1,2},{2,3},{3,0},{4,5},{5,6},{6,7},{7,4},{8,9},{9,10},{10,1... | collective-permute-start | bytes 6152 | tf_op jit(solution)/shard_map/while/body/eval_jaxpr/ppermute | solution.py:11
where the time goes:
time: 372 us; the launch traced here: 370 us
  waiting for transfers between devices  278 us (75%)
  starting transfers between devices  25.5 us (7%)
  matrix products  24 us (6%)
  blocking collectives  20.4 us (5%)
  local copies, waits for them, and re-layouts  16 us (4%)
  other arithmetic  5.98 us (2%)
    ppermute x20, waiting for transfers between devices, from_behind(): return lax.ppermute(x, axis, [(i, (i + by) % count) for i in range(count)])  263 us
    all_to_all x1, blocking collectives, body(): lax.all_to_all(averaged, 'owner', split_axis=0, concat_axis=0, tiled=True)  20.4 us
    ppermute x20, starting transfers between devices, from_behind(): return lax.ppermute(x, axis, [(i, (i + by) % count) for i in range(count)])  17.1 us
    all_to_all x1, waiting for transfers between devices, body(): lax.all_to_all(send_emb, 'owner', split_axis=0, concat_axis=0, tiled=True)  13.4 us
    while x16, local copies, waits for them, and re-layouts  10 us
    dot_general x4, matrix products, contribute(): lax.dot_general(query_emb, key_emb, (((1,), (1,)), ((), ())), preferred_e...  9.13 us
    dot_general x4, matrix products, contribute(): jnp.dot(weights.astype(jnp.bfloat16), key_emb, preferred_element_type=jnp...  8.5 us
  transfers between devices with their start and end apart: 22, of which 6 were waited for; matrix products, arithmetic and copies ran while one was open for 0% of the time, Pallas kernels for 0%

commit v1 on v0

v1 whole, which is shorter than its diff:
```python
import jax
import jax.numpy as jnp
from jax import lax
from jax.sharding import PartitionSpec as P

BLOCK = 128
SUB = 16


def route(row_owner, row_sub, loop_count, capacity):
    devices = lax.axis_size("owner") * loop_count
    dest = row_owner * loop_count + row_sub % loop_count
    onehot = (dest[:, None] == jnp.arange(devices, dtype=jnp.int32)[None, :]).astype(jnp.bfloat16)
    rows = row_owner.shape[0]
    lower = (
        jnp.arange(rows, dtype=jnp.int32)[:, None] > jnp.arange(rows, dtype=jnp.int32)[None, :]
    ).astype(jnp.bfloat16)
    earlier = jnp.dot(lower, onehot, preferred_element_type=jnp.float32)
    within = jnp.sum(earlier * onehot.astype(jnp.float32), axis=1).astype(jnp.int32)
    return dest * capacity + within


def attend(keys, near, sub):
    slots = keys.shape[0]
    scale = 4.0 / keys.shape[1]
    scores = scale * lax.dot_general(
        keys, keys, (((1,), (1,)), ((), ())), preferred_element_type=jnp.float32
    )
    index = jnp.arange(slots, dtype=jnp.int32)
    same = (index[:, None] == index[None, :]) | (
        (sub[:, None] == sub[None, :]) & near
    )
    top = jnp.max(jnp.where(same, scores, jnp.float32(-1e30)), axis=1)
    weights = jnp.where(same, jnp.exp(scores - top[:, None]), jnp.float32(0.0))
    total = jnp.sum(weights, axis=1)
    summed = jnp.dot(weights.astype(jnp.bfloat16), keys, preferred_element_type=jnp.float32)
    return (summed / total[:, None]).astype(jnp.bfloat16)


def body(emb, row_owner, row_sub, cand):
    rows = emb.shape[0]
    owner_count = lax.axis_size("owner")
    loop_count = lax.axis_size("loop")
    devices = owner_count * loop_count
    capacity = 2 * rows // owner_count // loop_count
    slots = devices * capacity
    local_blocks = rows // BLOCK
    axes = ("owner", "loop")

    slot_of_row = route(row_owner, row_sub, loop_count, capacity)
    placing = (jnp.arange(slots, dtype=jnp.int32)[:, None] == slot_of_row[None, :]).astype(
        jnp.bfloat16
    )
    send_emb = jnp.dot(placing, emb, preferred_element_type=jnp.float32).astype(jnp.bfloat16)
    row_labels = jnp.stack(
        [jnp.arange(rows, dtype=jnp.int32) // BLOCK + 1, row_sub + 1], axis=1
    ).astype(jnp.bfloat16)
    send_labels = jnp.dot(placing, row_labels, preferred_element_type=jnp.float32).astype(
        jnp.int32
    )
    held_emb = lax.all_to_all(send_emb, axes, split_axis=0, concat_axis=0, tiled=True)
    held_labels = lax.all_to_all(send_labels, axes, split_axis=0, concat_axis=0, tiled=True)

    index = jnp.arange(slots, dtype=jnp.int32)
    present = held_labels[:, 0] > 0
    source = index // capacity
    global_block = source * local_blocks + held_labels[:, 0] - 1
    global_block = jnp.where(present, global_block, 0)
    sub = jnp.where(present, held_labels[:, 1] - 1, -1 - index)
    block_count = cand.shape[1]
    block_onehot = (
        global_block[:, None] == jnp.arange(block_count, dtype=jnp.int32)[None, :]
    ).astype(jnp.bfloat16)
    cand_rows = jnp.dot(block_onehot, cand.astype(jnp.bfloat16), preferred_element_type=jnp.float32)
    near = (
        lax.dot_general(
            cand_rows.astype(jnp.bfloat16),
            block_onehot,
            (((1,), (1,)), ((), ())),
            preferred_element_type=jnp.float32,
        )
        > 0.5
    )
    averaged = attend(held_emb, near, sub)
    returned = lax.all_to_all(averaged, axes, split_axis=0, concat_axis=0, tiled=True)
    result = lax.dot_general(
        placing, returned, (((0,), (0,)), ((), ())), preferred_element_type=jnp.float32
    )
    return result.astype(jnp.bfloat16)


def solution(mesh):
    return jax.shard_map(
        body,
        mesh=mesh,
        in_specs=(
            P(("groups", "owner", "loop"), None),
            P(("groups", "owner", "loop")),
            P(("groups", "owner", "loop")),
            P("groups", None),
        ),
        out_specs=P(("groups", "owner", "loop"), None),
        check_vma=False,
    )
```

time: 372 us -> 80.3 us (0.22)
  waiting for transfers between devices: 278 us -> 30.8 us
  matrix products: 24 us -> 5.33 us
  local copies, waits for them, and re-layouts: 16 us -> 0.8 us
  starting transfers between devices: 25.5 us -> 11.2 us
  blocking collectives: 20.4 us -> 30.1 us
  other arithmetic: 5.98 us -> 1.09 us
    ppermute x20 -> x0, waiting for transfers between devices: 263 us -> none  [from_behind(): return lax.ppermute(x, axis, [(i, (i + by) % count) for i in range(count)])]
    dot_general x12 -> x4, matrix products: 20.5 us -> 2.4 us  [the longest x1 0.77 us: attend(): jnp.dot(weights.astype(jnp.bfloat16), keys, preferred_element_type=jnp.fl...]
    ppermute x20 -> x0, starting transfers between devices: 17.1 us -> none  [from_behind(): return lax.ppermute(x, axis, [(i, (i + by) % count) for i in range(count)])]
    all_to_all x2, waiting for transfers between devices: 15 us -> 30.8 us  [the longest x1 26.1 us: body(): lax.all_to_all(send_emb, axes, split_axis=0, concat_axis=0, tiled=True)]
    while x16 -> x0, local copies, waits for them, and re-layouts: 10 us -> none
    all_to_all x1, blocking collectives: 20.4 us -> 30.1 us  [body(): lax.all_to_all(averaged, axes, split_axis=0, concat_axis=0, tiled=True)]
    gather x4 -> x0, local copies, waits for them, and re-layouts: 4.15 us -> none  [candidate_rows(): return jnp.take(cand, clipped, axis=0).astype(jnp.bfloat16)]
  transfers between devices with their start and end apart: 22 -> 2, of which waited for: 6 -> 2; matrix products, arithmetic and copies ran while one was open for 0% -> 2% of each run, Pallas kernels for 0% -> 0%
where the time goes in v1:
time: 80.3 us; the launch traced here: 79.3 us
  waiting for transfers between devices  30.8 us (38%)
  blocking collectives  30.1 us (37%)
  starting transfers between devices  11.2 us (14%)
  matrix products  5.33 us (7%)
  other arithmetic  1.09 us (1%)
    all_to_all x1, blocking collectives, body(): lax.all_to_all(averaged, axes, split_axis=0, concat_axis=0, tiled=True)  30.1 us
    all_to_all x1, waiting for transfers between devices, body(): lax.all_to_all(send_emb, axes, split_axis=0, concat_axis=0, tiled=True)  26.1 us
    all_to_all x1, starting transfers between devices, body(): lax.all_to_all(send_labels, axes, split_axis=0, concat_axis=0, tiled=True)  7.31 us
    all_to_all x1, waiting for transfers between devices, body(): lax.all_to_all(send_labels, axes, split_axis=0, concat_axis=0, tiled=True)  4.7 us
    all_to_all x1, starting transfers between devices, body(): lax.all_to_all(send_emb, axes, split_axis=0, concat_axis=0, tiled=True)  3.86 us
  transfers between devices with their start and end apart: 2, of which 2 were waited for; matrix products, arithmetic and copies ran while one was open for 2% of the time, Pallas kernels for 0%

profile of v1, /device:TPU:1, one launch (start us, length us, event | category | flops | bytes accessed | tf_op | source)
XLA Modules:
  0.0 79.3 jit_solution(15037593979401842642)
XLA Ops:
  0.0 0.0 copy-start
  0.0 0.8 add_convert_fusion
  0.8 0.2 fusion.2
  1.0 0.2 convolution_convert_fusion.3
  1.2 0.1 all_to_all.24
  1.3 0.6 copy.6
  1.9 7.3 %all-to-all-start = ((s32[16,32,2]{1,2,0:T(2,128)}), s32[16,32,2]{1,2,0:T(2,128)S(1)}, u32[]{:S(2)}, u32[]{:S(2)}) async-start(s32[16,32,2]{1,2,0:T(2,128)} %copy.6), calls=%async_computation | async-start | bytes 32768 | tf_op jit(solution)/shard_map/all_to_all | solution.py:62
  9.2 0.0 copy-done
  9.2 1.4 %convolution_convert_fusion = bf16[512,1024]{1,0:T(8,128)(2,1)} fusion(bf16[256,1024]{1,0:T(8,128)(2,1)S(1)} %copy-done, s32[256]{0:T(256)S(1)} %convert_add_fusion), kind=kOutput, calls=%fused_computation.1 | convolution fusion | flops 269090816 | bytes 1573888 | tf_op jit(solution)/shard_map/dot_general | solution.py:54
  10.7 4.7 %all-to-all-done = s32[16,32,2]{1,2,0:T(2,128)S(1)} async-done(((s32[16,32,2]{1,2,0:T(2,128)}), s32[16,32,2]{1,2,0:T(2,128)S(1)}, u32[]{:S(2)}, u32[]{:S(2)}) %all-to-all-start) | async-done | bytes 4128 | tf_op jit(solution)/shard_map/all_to_all | solution.py:62
  15.4 3.9 %all-to-all-start.1 = ((bf16[16,32,1024]{2,1,0:T(8,128)(2,1)}), bf16[16,32,1024]{2,1,0:T(8,128)(2,1)S(1)}, u32[]{:S(2)}, u32[]{:S(2)}) async-start(bf16[16,32,1024]{2,1,0:T(8,128)(2,1)} %bitcast.3), calls=%async_computation.1 | async-start | bytes 2097152 | tf_op jit(solution)/shard_map/all_to_all | solution.py:61
  19.2 0.1 all_to_all.26
  19.4 26.1 %all-to-all-done.1 = bf16[16,32,1024]{2,1,0:T(8,128)(2,1)S(1)} async-done(((bf16[16,32,1024]{2,1,0:T(8,128)(2,1)}), bf16[16,32,1024]{2,1,0:T(8,128)(2,1)S(1)}, u32[]{:S(2)}, u32[]{:S(2)}) %all-to-all-start.1) | async-done | bytes 1048608 | tf_op jit(solution)/shard_map/all_to_all | solution.py:61
  45.4 0.0 copy-start.1
  45.4 0.7 convolution_multiply_fusion
  46.2 0.0 copy-done.1
  46.2 0.7 select_reduce_fusion
  46.9 0.3 fusion.3
  47.2 0.8 divide_convert_fusion
  47.9 30.1 %all_to_all.36 = bf16[16,32,1024]{2,1,0:T(8,128)(2,1)S(1)} all-to-all(bf16[16,32,1024]{2,1,0:T(8,128)(2,1)S(1)} %bitcast.19), channel_id=1, replica_groups=mesh['groups'=2,'owner'=4,'loop'=4] {'owner','loop'}, dimensions={0} | all-to-all | bytes 2097152 | tf_op jit(solution)/shard_map/all_to_all | solution.py:85
  78.0 1.3 %convolution_convert_fusion.1 = bf16[256,1024]{1,0:T(8,128)(2,1)} fusion(bf16[512,1024]{1,0:T(8,128)(2,1)S(1)} %bitcast.16, s32[256]{0:T(256)S(1)} %convert_add_fusion), kind=kOutput, calls=%fused_computation.3 | convolution fusion | flops 268828672 | bytes 1573888 | tf_op jit(solution)/shard_map/dot_general | solution.py:86
  (7 shorter events, 0.1 us)
Async XLA Ops:
  0.0 9.2 %copy-start = (bf16[256,1024]{1,0:T(8,128)(2,1)S(1)}, bf16[256,1024]{1,0:T(8,128)(2,1)}, u32[]{:S(2)}) copy-start(bf16[256,1024]{1,0:T(8,128)(2,1)} %param.4) | copy-start | bytes 1572868
  1.9 13.5 %all-to-all-start = ((s32[16,32,2]{1,2,0:T(2,128)}), s32[16,32,2]{1,2,0:T(2,128)S(1)}, u32[]{:S(2)}, u32[]{:S(2)}) async-start(s32[16,32,2]{1,2,0:T(2,128)} %copy.6), calls=%async_computation | async-start | bytes 32768 | tf_op jit(solution)/shard_map/all_to_all | solution.py:62
  15.4 30.1 %all-to-all-start.1 = ((bf16[16,32,1024]{2,1,0:T(8,128)(2,1)}), bf16[16,32,1024]{2,1,0:T(8,128)(2,1)S(1)}, u32[]{:S(2)}, u32[]{:S(2)}) async-start(bf16[16,32,1024]{2,1,0:T(8,128)(2,1)} %bitcast.3), calls=%async_computation.1 | async-start | bytes 2097152 | tf_op jit(solution)/shard_map/all_to_all | solution.py:61
  45.4 0.8 copy-start.1

commit v2 on v1

--- a/solution.py
+++ b/solution.py
@@ -18,6 +18,30 @@
     earlier = jnp.dot(lower, onehot, preferred_element_type=jnp.float32)
     within = jnp.sum(earlier * onehot.astype(jnp.float32), axis=1).astype(jnp.int32)
     return dest * capacity + within
+
+
+def arrivals(row_owner, row_sub, axes, loop_count, capacity):
+    rows = row_owner.shape[0]
+    packed = (row_owner * loop_count + row_sub % loop_count) * 1024 + row_sub
+    every = lax.all_gather(packed, axes, axis=0, tiled=False)
+    sources = every.shape[0]
+    me = lax.axis_index("owner") * loop_count + lax.axis_index("loop")
+    mine = every // 1024 == me
+    upper = (
+        jnp.arange(rows, dtype=jnp.int32)[:, None] < jnp.arange(rows, dtype=jnp.int32)[None, :]
+    ).astype(jnp.bfloat16)
+    within = jnp.dot(mine.astype(jnp.bfloat16), upper, preferred_element_type=jnp.float32)
+    within = within.astype(jnp.int32)
+    match = mine[:, None, :] & (
+        within[:, None, :] == jnp.arange(capacity, dtype=jnp.int32)[None, :, None]
+    )
+    local_block = (jnp.arange(rows, dtype=jnp.int32) // BLOCK)[None, None, :]
+    present = jnp.any(match, axis=2).reshape(sources * capacity)
+    held_block = jnp.sum(jnp.where(match, local_block, 0), axis=2).reshape(sources * capacity)
+    held_sub = jnp.sum(jnp.where(match, every[:, None, :] % 1024, 0), axis=2)
+    held_sub = held_sub.reshape(sources * capacity)
+    index = jnp.arange(sources * capacity, dtype=jnp.int32)
+    return held_block, jnp.where(present, held_sub, -1 - index)
 
 
 def attend(keys, near, sub):
@@ -52,21 +76,10 @@
         jnp.bfloat16
     )
     send_emb = jnp.dot(placing, emb, preferred_element_type=jnp.float32).astype(jnp.bfloat16)
-    row_labels = jnp.stack(
-        [jnp.arange(rows, dtype=jnp.int32) // BLOCK + 1, row_sub + 1], axis=1
-    ).astype(jnp.bfloat16)
-    send_labels = jnp.dot(placing, row_labels, preferred_element_type=jnp.float32).astype(
-        jnp.int32
-    )
     held_emb = lax.all_to_all(send_emb, axes, split_axis=0, concat_axis=0, tiled=True)
-    held_labels = lax.all_to_all(send_labels, axes, split_axis=0, concat_axis=0, tiled=True)
 
-    index = jnp.arange(slots, dtype=jnp.int32)
-    present = held_labels[:, 0] > 0
-    source = index // capacity
-    global_block = source * local_blocks + held_labels[:, 0] - 1
-    global_block = jnp.where(present, global_block, 0)
-    sub = jnp.where(present, held_labels[:, 1] - 1, -1 - index)
+    held_block, sub = arrivals(row_owner, row_sub, axes, loop_count, capacity)
+    global_block = jnp.arange(slots, dtype=jnp.int32) // capacity * local_blocks + held_block
     block_count = cand.shape[1]
     block_onehot = (
         global_block[:, None] == jnp.arange(block_count, dtype=jnp.int32)[None, :]

time: 80.3 us -> 94.5 us (1.18)
  blocking collectives: 30.1 us -> 78.4 us
  waiting for transfers between devices: 30.8 us -> 0.01 us
  starting transfers between devices: 11.2 us -> 7.31 us
  other arithmetic: 1.09 us -> 2.08 us
    all_gather x0 -> x1, blocking collectives: none -> 46.2 us  [arrivals(): every = lax.all_gather(packed, axes, axis=0, tiled=False)]
    all_to_all x1, waiting for transfers between devices: 26.1 us -> 0.01 us  [body(): lax.all_to_all(send_emb, axes, split_axis=0, concat_axis=0, tiled=True)]
    all_to_all x1 -> x0, starting transfers between devices: 7.31 us -> none  [body(): lax.all_to_all(send_labels, axes, split_axis=0, concat_axis=0, tiled=True)]
    all_to_all x1 -> x0, waiting for transfers between devices: 4.7 us -> none  [body(): lax.all_to_all(send_labels, axes, split_axis=0, concat_axis=0, tiled=True)]
    all_to_all x1, starting transfers between devices: 3.86 us -> 7.31 us  [body(): lax.all_to_all(send_emb, axes, split_axis=0, concat_axis=0, tiled=True)]
    all_to_all x1, blocking collectives: 30.1 us -> 32.2 us  [body(): lax.all_to_all(averaged, axes, split_axis=0, concat_axis=0, tiled=True)]
  transfers between devices with their start and end apart: 2 -> 1, of which waited for: 2 -> 0; matrix products, arithmetic and copies ran while one was open for 2% -> 2% of each run, Pallas kernels for 0% -> 0%
where the time goes in v2:
time: 94.5 us; the launch traced here: 93.5 us
  blocking collectives  78.4 us (83%)
  starting transfers between devices  7.31 us (8%)
  matrix products  5.27 us (6%)
  other arithmetic  2.08 us (2%)
    all_gather x1, blocking collectives, arrivals(): every = lax.all_gather(packed, axes, axis=0, tiled=False)  46.2 us
    all_to_all x1, blocking collectives, body(): lax.all_to_all(averaged, axes, split_axis=0, concat_axis=0, tiled=True)  32.2 us
    all_to_all x1, starting transfers between devices, body(): lax.all_to_all(send_emb, axes, split_axis=0, concat_axis=0, tiled=True)  7.31 us
  transfers between devices with their start and end apart: 1, of which 0 were waited for; matrix products, arithmetic and copies ran while one was open for 2% of the time, Pallas kernels for 0%

profile of v2, /device:TPU:1, one launch (start us, length us, event | category | flops | bytes accessed | tf_op | source)
XLA Modules:
  0.0 93.5 jit_solution(17175812813753035231)
XLA Ops:
  0.0 0.0 copy-start
  0.0 0.8 multiply_add_fusion
  0.8 0.2 fusion.2
  1.0 0.1 copy-done
  1.1 1.4 %convolution_convert_fusion = bf16[512,1024]{1,0:T(8,128)(2,1)} fusion(bf16[256,1024]{1,0:T(8,128)(2,1)S(1)} %copy-done, s32[256]{0:T(256)S(1)} %convert_add_fusion), kind=kOutput, calls=%fused_computation.1 | convolution fusion | flops 269090816 | bytes 1573888 | tf_op jit(solution)/shard_map/dot_general | solution.py:78
  2.5 7.3 %all-to-all-start = ((bf16[16,32,1024]{2,1,0:T(8,128)(2,1)}), bf16[16,32,1024]{2,1,0:T(8,128)(2,1)S(1)}, u32[]{:S(2)}, u32[]{:S(2)}) async-start(bf16[16,32,1024]{2,1,0:T(8,128)(2,1)} %bitcast.1), calls=%async_computation | async-start | bytes 2097152 | tf_op jit(solution)/shard_map/all_to_all | solution.py:79
  9.8 46.2 %all-gather.1 = s32[16,1,256]{2,1,0:T(1,128)S(1)} all-gather(s32[1,1,256]{2,1,0:T(1,128)S(1)} %bitcast.41), channel_id=2, replica_groups=mesh['groups'=2,'owner'=4,'loop'=4] {'owner','loop'}, dimensions={0}, use_global_device_ids=true | all-gather | bytes 17408 | tf_op jit(solution)/shard_map/all_gather | solution.py:26
  56.1 0.2 convolution_convert_fusion.3
  56.2 0.4 fusion.9
  56.6 0.1 reshape.84
  56.7 0.6 select_reduce_fusion.1
  57.4 0.1 reshape.86
  57.4 0.1 reshape.85
  57.5 0.0 all-to-all-done
  57.5 0.0 copy-start.1
  57.5 0.7 convolution_multiply_fusion
  58.3 0.0 copy-done.1
  58.3 0.7 select_reduce_fusion
  59.0 0.3 fusion.3
  59.2 0.8 divide_convert_fusion
  60.0 32.2 %all_to_all.24 = bf16[16,32,1024]{2,1,0:T(8,128)(2,1)S(1)} all-to-all(bf16[16,32,1024]{2,1,0:T(8,128)(2,1)S(1)} %bitcast.40), channel_id=1, replica_groups=mesh['groups'=2,'owner'=4,'loop'=4] {'owner','loop'}, dimensions={0} | all-to-all | bytes 2097152 | tf_op jit(solution)/shard_map/all_to_all | solution.py:98
  92.2 1.3 %convolution_convert_fusion.1 = bf16[256,1024]{1,0:T(8,128)(2,1)} fusion(bf16[512,1024]{1,0:T(8,128)(2,1)S(1)} %bitcast.37, s32[256]{0:T(256)S(1)} %convert_add_fusion), kind=kOutput, calls=%fused_computation.3 | convolution fusion | flops 268828672 | bytes 1573888 | tf_op jit(solution)/shard_map/dot_general | solution.py:99
  (5 shorter events, 0.0 us)
Async XLA Ops:
  0.0 1.1 %copy-start = (bf16[256,1024]{1,0:T(8,128)(2,1)S(1)}, bf16[256,1024]{1,0:T(8,128)(2,1)}, u32[]{:S(2)}) copy-start(bf16[256,1024]{1,0:T(8,128)(2,1)} %param.4) | copy-start | bytes 1572868
  2.5 55.0 %all-to-all-start = ((bf16[16,32,1024]{2,1,0:T(8,128)(2,1)}), bf16[16,32,1024]{2,1,0:T(8,128)(2,1)S(1)}, u32[]{:S(2)}, u32[]{:S(2)}) async-start(bf16[16,32,1024]{2,1,0:T(8,128)(2,1)} %bitcast.1), calls=%async_computation | async-start | bytes 2097152 | tf_op jit(solution)/shard_map/all_to_all | solution.py:79
  57.5 0.8 copy-start.1

commit v3 on v1

--- a/solution.py
+++ b/solution.py
@@ -5,6 +5,7 @@
 
 BLOCK = 128
 SUB = 16
+LABEL_COLUMNS = 128
 
 
 def route(row_owner, row_sub, loop_count, capacity):
@@ -51,15 +52,17 @@
     placing = (jnp.arange(slots, dtype=jnp.int32)[:, None] == slot_of_row[None, :]).astype(
         jnp.bfloat16
     )
-    send_emb = jnp.dot(placing, emb, preferred_element_type=jnp.float32).astype(jnp.bfloat16)
+    width = emb.shape[1]
     row_labels = jnp.stack(
         [jnp.arange(rows, dtype=jnp.int32) // BLOCK + 1, row_sub + 1], axis=1
     ).astype(jnp.bfloat16)
-    send_labels = jnp.dot(placing, row_labels, preferred_element_type=jnp.float32).astype(
-        jnp.int32
+    labelled = jnp.concatenate(
+        [emb, jnp.pad(row_labels, ((0, 0), (0, LABEL_COLUMNS - 2)))], axis=1
     )
-    held_emb = lax.all_to_all(send_emb, axes, split_axis=0, concat_axis=0, tiled=True)
-    held_labels = lax.all_to_all(send_labels, axes, split_axis=0, concat_axis=0, tiled=True)
+    send = jnp.dot(placing, labelled, preferred_element_type=jnp.float32).astype(jnp.bfloat16)
+    held = lax.all_to_all(send, axes, split_axis=0, concat_axis=0, tiled=True)
+    held_emb = held[:, :width]
+    held_labels = held[:, width : width + 2].astype(jnp.int32)
 
     index = jnp.arange(slots, dtype=jnp.int32)
     present = held_labels[:, 0] > 0

time: 80.3 us -> 74.1 us (0.923)
  blocking collectives: 30.1 us -> 66.2 us
  waiting for transfers between devices: 30.8 us -> 0 us
  starting transfers between devices: 11.2 us -> 0 us
    all_to_all x0 -> x1, blocking collectives: none -> 36.5 us  [body(): held = lax.all_to_all(send, axes, split_axis=0, concat_axis=0, tiled=True)]
    all_to_all x2 -> x0, waiting for transfers between devices: 30.8 us -> none  [the longest x1 26.1 us: body(): lax.all_to_all(send_emb, axes, split_axis=0, concat_axis=0, tiled=True)]
    all_to_all x2 -> x0, starting transfers between devices: 11.2 us -> none  [the longest x1 7.31 us: body(): lax.all_to_all(send_labels, axes, split_axis=0, concat_axis=0, tiled=True)]
    dot_general x2 -> x1, matrix products: 1.64 us -> 1.55 us  [body(): jnp.dot(placing, labelled, preferred_element_type=jnp.float32)]
  transfers between devices with their start and end apart: 2 -> 0, of which waited for: 2 -> 0; matrix products, arithmetic and copies ran while one was open for 2% -> 0% of each run, Pallas kernels for 0% -> 0%
where the time goes in v3:
time: 74.1 us; the launch traced here: 73.2 us
  blocking collectives  66.2 us (89%)
  matrix products  5.22 us (7%)
  other arithmetic  1.57 us (2%)
    all_to_all x1, blocking collectives, body(): held = lax.all_to_all(send, axes, split_axis=0, concat_axis=0, tiled=True)  36.5 us
    all_to_all x1, blocking collectives, body(): lax.all_to_all(averaged, axes, split_axis=0, concat_axis=0, tiled=True)  29.7 us
    dot_general x1, matrix products, body(): jnp.dot(placing, labelled, preferred_element_type=jnp.float32)  1.55 us

profile of v3, /device:TPU:1, one launch (start us, length us, event | category | flops | bytes accessed | tf_op | source)
XLA Modules:
  0.0 73.2 jit_solution(1754709702645708677)
XLA Ops:
  0.0 0.7 fusion.34
  0.7 0.2 fusion.3
  1.0 0.1 copy.8
  1.1 1.6 %convolution_convert_fusion = bf16[512,1152]{1,0:T(8,128)(2,1)S(1)} fusion(bf16[256,2]{1,0:T(8,128)(2,1)S(1)} %copy.8, bf16[256,1024]{1,0:T(8,128)(2,1)} %param.4, s32[256]{0:T(256)S(1)} %convert_add_fusion), kind=kOutput, calls=%fused_computation | convolution fusion | flops 304480256 | bytes 1705984 | tf_op jit(solution)/shard_map/dot_general | solution.py:62
  2.7 36.5 %all_to_all.24 = bf16[16,32,1152]{2,1,0:T(8,128)(2,1)S(1)} all-to-all(bf16[16,32,1152]{2,1,0:T(8,128)(2,1)S(1)} %bitcast.9), channel_id=1, replica_groups=mesh['groups'=2,'owner'=4,'loop'=4] {'owner','loop'}, dimensions={0} | all-to-all | bytes 2359296 | tf_op jit(solution)/shard_map/all_to_all | solution.py:63
  39.1 0.0 copy-start
  39.2 0.7 %convolution_multiply_fusion = f32[512,512]{0,1:T(8,128)S(1)} fusion(bf16[512,1152]{1,0:T(8,128)(2,1)S(1)} %bitcast.7), kind=kOutput, calls=%fused_computation.2 | convolution fusion | flops 537133056 | bytes 2097152 | tf_op jit(solution)/shard_map/dot_general | solution.py:27
  39.9 0.1 fusion.42
  40.0 0.4 fusion.21
  40.5 0.0 copy-done
  40.5 0.7 select_reduce_fusion
  41.2 0.3 fusion.6
  41.4 0.8 %divide_convert_fusion = bf16[512,1024]{1,0:T(8,128)(2,1)S(1)} fusion(f32[512]{0:T(512)S(1)} %fusion.6, bf16[512,1152]{1,0:T(8,128)(2,1)S(1)} %bitcast.8, pred[512,512]{0,1:T(32,128)(4,1)S(1)} %get-tuple-element.13, f32[512,512]{0,1:T(8,128)S(1)} %convolution_multiply_fusion, f32[512]{0:T(512)S(1)} %get-tuple-element.12), kind=kOutput, calls=%fused_computation.1 | convolution fusion | flops 538705920 | bytes 3411968 | tf_op jit(solution)/shard_map/dot_general | solution.py:37
  42.2 29.7 %all_to_all.25 = bf16[16,32,1024]{2,1,0:T(8,128)(2,1)S(1)} all-to-all(bf16[16,32,1024]{2,1,0:T(8,128)(2,1)S(1)} %bitcast.10), channel_id=1, replica_groups=mesh['groups'=2,'owner'=4,'loop'=4] {'owner','loop'}, dimensions={0} | all-to-all | bytes 2097152 | tf_op jit(solution)/shard_map/all_to_all | solution.py:88
  71.9 1.3 %convolution_convert_fusion.1 = bf16[256,1024]{1,0:T(8,128)(2,1)} fusion(bf16[512,1024]{1,0:T(8,128)(2,1)S(1)} %bitcast.5, s32[256]{0:T(256)S(1)} %convert_add_fusion), kind=kOutput, calls=%fused_computation.3 | convolution fusion | flops 268828672 | bytes 1573888 | tf_op jit(solution)/shard_map/dot_general | solution.py:89
  (6 shorter events, 0.1 us)
Async XLA Ops:
  39.1 1.3 %copy-start = (s32[32,32]{1,0:T(8,128)S(1)}, s32[32,32]{1,0:T(8,128)}, u32[]{:S(2)}) copy-start(s32[32,32]{1,0:T(8,128)} %param.7) | copy-start | bytes 12292

commit v4 on v3

--- a/solution.py
+++ b/solution.py
@@ -49,9 +49,9 @@
     axes = ("owner", "loop")
 
     slot_of_row = route(row_owner, row_sub, loop_count, capacity)
-    placing = (jnp.arange(slots, dtype=jnp.int32)[:, None] == slot_of_row[None, :]).astype(
-        jnp.bfloat16
-    )
+    hit = jnp.arange(slots, dtype=jnp.int32)[:, None] == slot_of_row[None, :]
+    source_row = jnp.sum(jnp.where(hit, jnp.arange(rows, dtype=jnp.int32)[None, :] - rows, 0), axis=1)
+    source_row = source_row + rows
     width = emb.shape[1]
     row_labels = jnp.stack(
         [jnp.arange(rows, dtype=jnp.int32) // BLOCK + 1, row_sub + 1], axis=1
@@ -59,7 +59,7 @@
     labelled = jnp.concatenate(
         [emb, jnp.pad(row_labels, ((0, 0), (0, LABEL_COLUMNS - 2)))], axis=1
     )
-    send = jnp.dot(placing, labelled, preferred_element_type=jnp.float32).astype(jnp.bfloat16)
+    send = jnp.take(labelled, source_row, axis=0, mode="fill", fill_value=0)
     held = lax.all_to_all(send, axes, split_axis=0, concat_axis=0, tiled=True)
     held_emb = held[:, :width]
     held_labels = held[:, width : width + 2].astype(jnp.int32)
@@ -86,10 +86,7 @@
     )
     averaged = attend(held_emb, near, sub)
     returned = lax.all_to_all(averaged, axes, split_axis=0, concat_axis=0, tiled=True)
-    result = lax.dot_general(
-        placing, returned, (((0,), (0,)), ((), ())), preferred_element_type=jnp.float32
-    )
-    return result.astype(jnp.bfloat16)
+    return jnp.take(returned, slot_of_row, axis=0, mode="clip")
 
 
 def solution(mesh):

time: 74.1 us -> 78.1 us (1.054)
  blocking collectives: 66.2 us -> 36.5 us
  waiting for transfers between devices: 0 us -> 26.2 us
  local copies, waits for them, and re-layouts: 0.16 us -> 4.51 us
  starting transfers between devices: 0 us -> 3.86 us
  matrix products: 5.22 us -> 3.37 us
  other arithmetic: 1.57 us -> 2.53 us
    all_to_all x1 -> x0, blocking collectives: 29.7 us -> none  [body(): lax.all_to_all(averaged, axes, split_axis=0, concat_axis=0, tiled=True)]
    all_to_all x0 -> x1, waiting for transfers between devices: none -> 26.2 us  [body(): lax.all_to_all(averaged, axes, split_axis=0, concat_axis=0, tiled=True)]
    gather x0 -> x2, local copies, waits for them, and re-layouts: none -> 4.08 us  [the longest x1 2.12 us: body(): send = jnp.take(labelled, source_row, axis=0, mode='fill', fill_value=0)]
    all_to_all x0 -> x1, starting transfers between devices: none -> 3.86 us  [body(): lax.all_to_all(averaged, axes, split_axis=0, concat_axis=0, tiled=True)]
    dot_general x2 -> x0, matrix products: 2.84 us -> none  [the longest x1 1.55 us: body(): jnp.dot(placing, labelled, preferred_element_type=jnp.float32)]
    concatenate x0 -> x1, other arithmetic: none -> 1.09 us  [body(): jnp.concatenate([emb, jnp.pad(row_labels, ((0, 0), (0, LABEL_COLUMNS - 2)...]
    dot_general x1, matrix products: 0.75 us -> 1.75 us  [attend(): jnp.dot(weights.astype(jnp.bfloat16), keys, preferred_element_type=jnp.fl...]
  transfers between devices with their start and end apart: 0 -> 1, of which waited for: 0 -> 1; matrix products, arithmetic and copies ran while one was open for 0% -> 0% of each run, Pallas kernels for 0% -> 0%
where the time goes in v4:
time: 78.1 us; the launch traced here: 77.1 us
  blocking collectives  36.5 us (47%)
  waiting for transfers between devices  26.2 us (34%)
  local copies, waits for them, and re-layouts  4.51 us (6%)
  starting transfers between devices  3.86 us (5%)
  matrix products  3.37 us (4%)
  other arithmetic  2.53 us (3%)
    all_to_all x1, blocking collectives, body(): held = lax.all_to_all(send, axes, split_axis=0, concat_axis=0, tiled=True)  36.5 us
    all_to_all x1, waiting for transfers between devices, body(): lax.all_to_all(averaged, axes, split_axis=0, concat_axis=0, tiled=True)  26.2 us
    all_to_all x1, starting transfers between devices, body(): lax.all_to_all(averaged, axes, split_axis=0, concat_axis=0, tiled=True)  3.86 us
    gather x1, local copies, waits for them, and re-layouts, body(): send = jnp.take(labelled, source_row, axis=0, mode='fill', fill_value=0)  2.12 us
    gather x1, local copies, waits for them, and re-layouts, body(): return jnp.take(returned, slot_of_row, axis=0, mode='clip')  1.96 us
    dot_general x1, matrix products, attend(): jnp.dot(weights.astype(jnp.bfloat16), keys, preferred_element_type=jnp.fl...  1.75 us
  transfers between devices with their start and end apart: 1, of which 1 were waited for; matrix products, arithmetic and copies ran while one was open for 0% of the time, Pallas kernels for 0%

profile of v4, /device:TPU:1, one launch (start us, length us, event | category | flops | bytes accessed | tf_op | source)
XLA Modules:
  0.0 77.1 jit_solution(1793729652996269033)
XLA Ops:
  0.0 0.7 fusion.22
  0.7 0.2 fusion.3
  0.9 0.1 select_reduce_fusion.1
  1.1 0.1 add.115
  1.2 0.1 add.118
  1.3 0.1 copy.11
  1.4 1.1 %fusion.8 = bf16[256,1152]{1,0:T(8,128)(2,1)S(1)} fusion(bf16[256,2]{1,0:T(8,128)(2,1)S(1)} %copy.11, bf16[256,1024]{1,0:T(8,128)(2,1)} %param.4), kind=kLoop, calls=%fused_computation.20 | loop fusion | flops 1769472 | bytes 1115136 | tf_op jit(solution)/shard_map/concatenate | solution.py:59
  2.5 2.1 %gather_fusion = bf16[512,1152]{1,0:T(8,128)(2,1)S(1)} fusion(bf16[256,1152]{1,0:T(8,128)(2,1)S(1)} %fusion.8, s32[1024]{0:T(1024)S(1)} %pad_clamp_fusion.1), kind=kCustom, calls=%fused_computation | custom fusion | bytes 2361344 | tf_op jit(solution)/shard_map/jit(_take)/gather | solution.py:62
  4.7 0.2 broadcast_select_fusion
  4.9 36.5 %all_to_all.21 = bf16[16,32,1152]{2,1,0:T(8,128)(2,1)S(1)} all-to-all(bf16[16,32,1152]{2,1,0:T(8,128)(2,1)S(1)} %broadcast_select_fusion), channel_id=1, replica_groups=mesh['groups'=2,'owner'=4,'loop'=4] {'owner','loop'}, dimensions={0} | all-to-all | bytes 2359296 | tf_op jit(solution)/shard_map/all_to_all | solution.py:63
  41.4 0.1 copy.13
  41.5 0.0 copy-start
  41.5 0.7 convolution_multiply_fusion
  42.3 0.0 copy-done
  42.3 0.7 select_reduce_fusion
  43.0 0.3 fusion.6
  43.3 1.7 %divide_convert_fusion = bf16[512,1024]{1,0:T(8,128)(2,1)} fusion(f32[512]{0:T(512)S(1)} %fusion.6, bf16[512,1152]{1,0:T(8,128)(2,1)S(1)} %bitcast.14, pred[512,512]{0,1:T(32,128)(4,1)S(1)} %get-tuple-element.13, f32[512,512]{0,1:T(8,128)S(1)} %convolution_multiply_fusion, f32[512]{0:T(512)S(1)} %get-tuple-element.12), kind=kOutput, calls=%fused_computation.2 | convolution fusion | flops 538705920 | bytes 3411968 | tf_op jit(solution)/shard_map/dot_general | solution.py:37
  45.0 3.9 %all-to-all-start.1 = ((bf16[16,32,1024]{2,1,0:T(8,128)(2,1)}), bf16[16,32,1024]{2,1,0:T(8,128)(2,1)S(1)}, u32[]{:S(2)}, u32[]{:S(2)}) async-start(bf16[16,32,1024]{2,1,0:T(8,128)(2,1)} %bitcast.8), calls=%async_computation.1 | async-start | bytes 2097152 | tf_op jit(solution)/shard_map/all_to_all | solution.py:88
  48.9 26.2 %all-to-all-done.1 = bf16[16,32,1024]{2,1,0:T(8,128)(2,1)S(1)} async-done(((bf16[16,32,1024]{2,1,0:T(8,128)(2,1)}), bf16[16,32,1024]{2,1,0:T(8,128)(2,1)S(1)}, u32[]{:S(2)}, u32[]{:S(2)}) %all-to-all-start.1) | async-done | bytes 1048608 | tf_op jit(solution)/shard_map/all_to_all | solution.py:88
  75.1 2.0 %gather_fusion.1 = bf16[256,1024]{1,0:T(8,128)(2,1)} fusion(bf16[512,1024]{1,0:T(8,128)(2,1)S(1)} %bitcast.10, s32[1024]{0:T(1024)S(1)} %pad_clamp_fusion), kind=kCustom, calls=%fused_computation.1 | custom fusion | bytes 1049600 | tf_op jit(solution)/shard_map/jit(_take)/gather | solution.py:89
  (14 shorter events, 0.1 us)
Async XLA Ops:
  41.5 0.8 %copy-start = (s32[32,32]{1,0:T(8,128)S(1)}, s32[32,32]{1,0:T(8,128)}, u32[]{:S(2)}) copy-start(s32[32,32]{1,0:T(8,128)} %param.7) | copy-start | bytes 12292
  45.0 30.1 %all-to-all-start.1 = ((bf16[16,32,1024]{2,1,0:T(8,128)(2,1)}), bf16[16,32,1024]{2,1,0:T(8,128)(2,1)S(1)}, u32[]{:S(2)}, u32[]{:S(2)}) async-start(bf16[16,32,1024]{2,1,0:T(8,128)(2,1)} %bitcast.8), calls=%async_computation.1 | async-start | bytes 2097152 | tf_op jit(solution)/shard_map/all_to_all | solution.py:88

commit v5 on v3

--- a/solution.py
+++ b/solution.py
@@ -8,9 +8,22 @@
 LABEL_COLUMNS = 128
 
 
-def route(row_owner, row_sub, loop_count, capacity):
+PERMUTE_LIMIT = 16
+
+
+def exchange(chunks, axes, devices, sign):
+    if devices > PERMUTE_LIMIT:
+        return lax.all_to_all(chunks, axes, split_axis=0, concat_axis=0, tiled=True)
+    received = [chunks[0]]
+    for k in range(1, devices):
+        pairs = [(d, (d + sign * k) % devices) for d in range(devices)]
+        received.append(lax.ppermute(chunks[k], axes, pairs))
+    return jnp.stack(received)
+
+
+def route(row_owner, row_sub, loop_count, capacity, me):
     devices = lax.axis_size("owner") * loop_count
-    dest = row_owner * loop_count + row_sub % loop_count
+    dest = (row_owner * loop_count + row_sub % loop_count - me) % devices
     onehot = (dest[:, None] == jnp.arange(devices, dtype=jnp.int32)[None, :]).astype(jnp.bfloat16)
     rows = row_owner.shape[0]
     lower = (
@@ -48,7 +61,10 @@
     local_blocks = rows // BLOCK
     axes = ("owner", "loop")
 
-    slot_of_row = route(row_owner, row_sub, loop_count, capacity)
+    me = lax.axis_index("owner") * loop_count + lax.axis_index("loop")
+    if devices > PERMUTE_LIMIT:
+        me = 0
+    slot_of_row = route(row_owner, row_sub, loop_count, capacity, me)
     placing = (jnp.arange(slots, dtype=jnp.int32)[:, None] == slot_of_row[None, :]).astype(
         jnp.bfloat16
     )
@@ -60,13 +76,16 @@
         [emb, jnp.pad(row_labels, ((0, 0), (0, LABEL_COLUMNS - 2)))], axis=1
     )
     send = jnp.dot(placing, labelled, preferred_element_type=jnp.float32).astype(jnp.bfloat16)
-    held = lax.all_to_all(send, axes, split_axis=0, concat_axis=0, tiled=True)
+    held = exchange(send.reshape(devices, capacity, send.shape[1]), axes, devices, 1)
+    held = held.reshape(slots, send.shape[1])
     held_emb = held[:, :width]
     held_labels = held[:, width : width + 2].astype(jnp.int32)
 
     index = jnp.arange(slots, dtype=jnp.int32)
     present = held_labels[:, 0] > 0
     source = index // capacity
+    if devices <= PERMUTE_LIMIT:
+        source = (me - source) % devices
     global_block = source * local_blocks + held_labels[:, 0] - 1
     global_block = jnp.where(present, global_block, 0)
     sub = jnp.where(present, held_labels[:, 1] - 1, -1 - index)
@@ -85,7 +104,8 @@
         > 0.5
     )
     averaged = attend(held_emb, near, sub)
-    returned = lax.all_to_all(averaged, axes, split_axis=0, concat_axis=0, tiled=True)
+    returned = exchange(averaged.reshape(devices, capacity, width), axes, devices, -1)
+    returned = returned.reshape(slots, width)
     result = lax.dot_general(
         placing, returned, (((0,), (0,)), ((), ())), preferred_element_type=jnp.float32
     )

time: 74.1 us -> 138 us (1.86); the launches traced: 73.2 us -> 135 us
  waiting for transfers between devices: 0 us -> 89.4 us
  blocking collectives: 66.2 us -> 0 us
  starting transfers between devices: 0 us -> 38.9 us
    ppermute x0 -> x30, waiting for transfers between devices: none -> 89.4 us  [exchange(): received.append(lax.ppermute(chunks[k], axes, pairs))]
    all_to_all x2 -> x0, blocking collectives: 66.2 us -> none  [the longest x1 36.5 us: body(): held = lax.all_to_all(send, axes, split_axis=0, concat_axis=0, tiled=True)]
    ppermute x0 -> x30, starting transfers between devices: none -> 38.9 us  [exchange(): received.append(lax.ppermute(chunks[k], axes, pairs))]
  transfers between devices with their start and end apart: 0 -> 30, of which waited for: 0 -> 21; matrix products, arithmetic and copies ran while one was open for 0% -> 0% of each run, Pallas kernels for 0% -> 0%
where the time goes in v5:
time: 138 us; the launch traced here: 135 us
  waiting for transfers between devices  89.4 us (65%)
  starting transfers between devices  38.9 us (28%)
  matrix products  5.21 us (4%)
    ppermute x30, waiting for transfers between devices, exchange(): received.append(lax.ppermute(chunks[k], axes, pairs))  89.4 us
    ppermute x30, starting transfers between devices, exchange(): received.append(lax.ppermute(chunks[k], axes, pairs))  38.9 us
  transfers between devices with their start and end apart: 30, of which 21 were waited for; matrix products, arithmetic and copies ran while one was open for 0% of the time, Pallas kernels for 0%

profile of v5, /device:TPU:1, one launch (start us, length us, event | category | flops | bytes accessed | tf_op | source)
XLA Modules:
  0.0 135.5 jit_solution(11966401418521216073)
XLA Ops:
  1.1 1.6 %convolution_convert_fusion = bf16[512,1152]{1,0:T(8,128)(2,1)S(1)} fusion(bf16[256,2]{1,0:T(8,128)(2,1)S(1)} %copy.8, bf16[256,1024]{1,0:T(8,128)(2,1)} %param.4, s32[256]{0:T(256)S(1)} %convert_add_fusion), kind=kOutput, calls=%fused_computation | convolution fusion | flops 304480256 | bytes 1705984 | tf_op jit(solution)/shard_map/dot_general | solution.py:78
  2.8 4.8 %collective-permute-start.14 = (bf16[32,1152]{1,0:T(8,128)(2,1)S(1)}, bf16[32,1152]{1,0:T(8,128)(2,1)S(1)}, u32[]{:S(2)}, u32[]{:S(2)}) collective-permute-start(bf16[32,1152]{1,0:T(8,128)(2,1)S(1)} %get-tuple-element.5), channel_id=1, source_target_pairs={{0,15},{1,0},{2,1},{3,2},{4,3},{5,4},{6,5},{7,6},{8,7},{9,8},{10,9... | collective-permute-start | bytes 221192 | tf_op jit(solution)/shard_map/ppermute | solution.py:20
  9.6 1.9 %collective-permute-start = (bf16[32,1152]{1,0:T(8,128)(2,1)S(1)}, bf16[32,1152]{1,0:T(8,128)(2,1)S(1)}, u32[]{:S(2)}, u32[]{:S(2)}) collective-permute-start(bf16[32,1152]{1,0:T(8,128)(2,1)S(1)} %get-tuple-element.19), channel_id=1, source_target_pairs={{0,1},{1,2},{2,3},{3,4},{4,5},{5,6},{6,7},{7,8},{8,9},{9,10},{10,1... | collective-permute-start | bytes 221192 | tf_op jit(solution)/shard_map/ppermute | solution.py:20
  11.5 4.7 %collective-permute-done = bf16[32,1152]{1,0:T(8,128)(2,1)S(1)} collective-permute-done((bf16[32,1152]{1,0:T(8,128)(2,1)S(1)}, bf16[32,1152]{1,0:T(8,128)(2,1)S(1)}, u32[]{:S(2)}, u32[]{:S(2)}) %collective-permute-start) | collective-permute-done | bytes 73760 | tf_op jit(solution)/shard_map/ppermute | solution.py:20
  16.2 1.8 %collective-permute-start.1 = (bf16[32,1152]{1,0:T(8,128)(2,1)S(1)}, bf16[32,1152]{1,0:T(8,128)(2,1)S(1)}, u32[]{:S(2)}, u32[]{:S(2)}) collective-permute-start(bf16[32,1152]{1,0:T(8,128)(2,1)S(1)} %get-tuple-element.18), channel_id=1, source_target_pairs={{0,2},{1,3},{2,4},{3,5},{4,6},{5,7},{6,8},{7,9},{8,10},{9,11},{10,... | collective-permute-start | bytes 221192 | tf_op jit(solution)/shard_map/ppermute | solution.py:20
  18.1 4.9 %collective-permute-done.1 = bf16[32,1152]{1,0:T(8,128)(2,1)S(1)} collective-permute-done((bf16[32,1152]{1,0:T(8,128)(2,1)S(1)}, bf16[32,1152]{1,0:T(8,128)(2,1)S(1)}, u32[]{:S(2)}, u32[]{:S(2)}) %collective-permute-start.1) | collective-permute-done | bytes 73760 | tf_op jit(solution)/shard_map/ppermute | solution.py:20
  23.0 3.8 %collective-permute-done.2 = bf16[32,1152]{1,0:T(8,128)(2,1)S(1)} collective-permute-done((bf16[32,1152]{1,0:T(8,128)(2,1)S(1)}, bf16[32,1152]{1,0:T(8,128)(2,1)S(1)}, u32[]{:S(2)}, u32[]{:S(2)}) %collective-permute-start.2) | collective-permute-done | bytes 73760 | tf_op jit(solution)/shard_map/ppermute | solution.py:20
  26.8 2.6 %collective-permute-start.3 = (bf16[32,1152]{1,0:T(8,128)(2,1)S(1)}, bf16[32,1152]{1,0:T(8,128)(2,1)S(1)}, u32[]{:S(2)}, u32[]{:S(2)}) collective-permute-start(bf16[32,1152]{1,0:T(8,128)(2,1)S(1)} %get-tuple-element.16), channel_id=1, source_target_pairs={{0,4},{1,5},{2,6},{3,7},{4,8},{5,9},{6,10},{7,11},{8,12},{9,13},{1... | collective-permute-start | bytes 221192 | tf_op jit(solution)/shard_map/ppermute | solution.py:20
  30.7 1.8 %collective-permute-start.4 = (bf16[32,1152]{1,0:T(8,128)(2,1)S(1)}, bf16[32,1152]{1,0:T(8,128)(2,1)S(1)}, u32[]{:S(2)}, u32[]{:S(2)}) collective-permute-start(bf16[32,1152]{1,0:T(8,128)(2,1)S(1)} %get-tuple-element.15), channel_id=1, source_target_pairs={{0,5},{1,6},{2,7},{3,8},{4,9},{5,10},{6,11},{7,12},{8,13},{9,14},{... | collective-permute-start | bytes 221192 | tf_op jit(solution)/shard_map/ppermute | solution.py:20
  32.5 4.1 %collective-permute-done.4 = bf16[32,1152]{1,0:T(8,128)(2,1)S(1)} collective-permute-done((bf16[32,1152]{1,0:T(8,128)(2,1)S(1)}, bf16[32,1152]{1,0:T(8,128)(2,1)S(1)}, u32[]{:S(2)}, u32[]{:S(2)}) %collective-permute-start.4) | collective-permute-done | bytes 73760 | tf_op jit(solution)/shard_map/ppermute | solution.py:20
  37.6 5.4 %collective-permute-done.5 = bf16[32,1152]{1,0:T(8,128)(2,1)S(1)} collective-permute-done((bf16[32,1152]{1,0:T(8,128)(2,1)S(1)}, bf16[32,1152]{1,0:T(8,128)(2,1)S(1)}, u32[]{:S(2)}, u32[]{:S(2)}) %collective-permute-start.5) | collective-permute-done | bytes 73760 | tf_op jit(solution)/shard_map/ppermute | solution.py:20
  43.1 3.6 %collective-permute-start.6 = (bf16[32,1152]{1,0:T(8,128)(2,1)S(1)}, bf16[32,1152]{1,0:T(8,128)(2,1)S(1)}, u32[]{:S(2)}, u32[]{:S(2)}) collective-permute-start(bf16[32,1152]{1,0:T(8,128)(2,1)S(1)} %get-tuple-element.13), channel_id=1, source_target_pairs={{0,7},{1,8},{2,9},{3,10},{4,11},{5,12},{6,13},{7,14},{8,15},{9,0},... | collective-permute-start | bytes 221192 | tf_op jit(solution)/shard_map/ppermute | solution.py:20
  46.6 1.6 %collective-permute-done.6 = bf16[32,1152]{1,0:T(8,128)(2,1)S(1)} collective-permute-done((bf16[32,1152]{1,0:T(8,128)(2,1)S(1)}, bf16[32,1152]{1,0:T(8,128)(2,1)S(1)}, u32[]{:S(2)}, u32[]{:S(2)}) %collective-permute-start.6) | collective-permute-done | bytes 73760 | tf_op jit(solution)/shard_map/ppermute | solution.py:20
  48.7 2.7 %collective-permute-done.7 = bf16[32,1152]{1,0:T(8,128)(2,1)S(1)} collective-permute-done((bf16[32,1152]{1,0:T(8,128)(2,1)S(1)}, bf16[32,1152]{1,0:T(8,128)(2,1)S(1)}, u32[]{:S(2)}, u32[]{:S(2)}) %collective-permute-start.7) | collective-permute-done | bytes 73760 | tf_op jit(solution)/shard_map/ppermute | solution.py:20
  51.5 8.3 %collective-permute-done.8 = bf16[32,1152]{1,0:T(8,128)(2,1)S(1)} collective-permute-done((bf16[32,1152]{1,0:T(8,128)(2,1)S(1)}, bf16[32,1152]{1,0:T(8,128)(2,1)S(1)}, u32[]{:S(2)}, u32[]{:S(2)}) %collective-permute-start.8) | collective-permute-done | bytes 73760 | tf_op jit(solution)/shard_map/ppermute | solution.py:20
  59.8 6.8 %collective-permute-done.9 = bf16[32,1152]{1,0:T(8,128)(2,1)S(1)} collective-permute-done((bf16[32,1152]{1,0:T(8,128)(2,1)S(1)}, bf16[32,1152]{1,0:T(8,128)(2,1)S(1)}, u32[]{:S(2)}, u32[]{:S(2)}) %collective-permute-start.9) | collective-permute-done | bytes 73760 | tf_op jit(solution)/shard_map/ppermute | solution.py:20
  66.7 4.7 %collective-permute-done.10 = bf16[32,1152]{1,0:T(8,128)(2,1)S(1)} collective-permute-done((bf16[32,1152]{1,0:T(8,128)(2,1)S(1)}, bf16[32,1152]{1,0:T(8,128)(2,1)S(1)}, u32[]{:S(2)}, u32[]{:S(2)}) %collective-permute-start.10) | collective-permute-done | bytes 73760 | tf_op jit(solution)/shard_map/ppermute | solution.py:20
  74.2 4.2 %collective-permute-start.15 = (bf16[32,1024]{1,0:T(8,128)(2,1)S(1)}, bf16[32,1024]{1,0:T(8,128)(2,1)S(1)}, u32[]{:S(2)}, u32[]{:S(2)}) collective-permute-start(bf16[32,1024]{1,0:T(8,128)(2,1)S(1)} %get-tuple-element.34), channel_id=1, source_target_pairs={{0,15},{1,0},{2,1},{3,2},{4,3},{5,4},{6,5},{7,6},{8,7},{9,8},{10,9... | collective-permute-start | bytes 196616 | tf_op jit(solution)/shard_map/ppermute | solution.py:20
  79.2 4.1 %collective-permute-start.26 = (bf16[32,1024]{1,0:T(8,128)(2,1)S(1)}, bf16[32,1024]{1,0:T(8,128)(2,1)S(1)}, u32[]{:S(2)}, u32[]{:S(2)}) collective-permute-start(bf16[32,1024]{1,0:T(8,128)(2,1)S(1)} %get-tuple-element.23), channel_id=1, source_target_pairs={{0,4},{1,5},{2,6},{3,7},{4,8},{5,9},{6,10},{7,11},{8,12},{9,13},{1... | collective-permute-start | bytes 196616 | tf_op jit(solution)/shard_map/ppermute | solution.py:20
  83.3 1.6 %collective-permute-start.16 = (bf16[32,1024]{1,0:T(8,128)(2,1)S(1)}, bf16[32,1024]{1,0:T(8,128)(2,1)S(1)}, u32[]{:S(2)}, u32[]{:S(2)}) collective-permute-start(bf16[32,1024]{1,0:T(8,128)(2,1)S(1)} %get-tuple-element.33), channel_id=1, source_target_pairs={{0,14},{1,15},{2,0},{3,1},{4,2},{5,3},{6,4},{7,5},{8,6},{9,7},{10,... | collective-permute-start | bytes 196616 | tf_op jit(solution)/shard_map/ppermute | solution.py:20
  84.9 4.2 %collective-permute-done.16 = bf16[32,1024]{1,0:T(8,128)(2,1)S(1)} collective-permute-done((bf16[32,1024]{1,0:T(8,128)(2,1)S(1)}, bf16[32,1024]{1,0:T(8,128)(2,1)S(1)}, u32[]{:S(2)}, u32[]{:S(2)}) %collective-permute-start.16) | collective-permute-done | bytes 65568 | tf_op jit(solution)/shard_map/ppermute | solution.py:20
  89.1 4.9 %collective-permute-done.17 = bf16[32,1024]{1,0:T(8,128)(2,1)S(1)} collective-permute-done((bf16[32,1024]{1,0:T(8,128)(2,1)S(1)}, bf16[32,1024]{1,0:T(8,128)(2,1)S(1)}, u32[]{:S(2)}, u32[]{:S(2)}) %collective-permute-start.17) | collective-permute-done | bytes 65568 | tf_op jit(solution)/shard_map/ppermute | solution.py:20
  94.0 1.5 %collective-permute-start.18 = (bf16[32,1024]{1,0:T(8,128)(2,1)S(1)}, bf16[32,1024]{1,0:T(8,128)(2,1)S(1)}, u32[]{:S(2)}, u32[]{:S(2)}) collective-permute-start(bf16[32,1024]{1,0:T(8,128)(2,1)S(1)} %get-tuple-element.31), channel_id=1, source_target_pairs={{0,12},{1,13},{2,14},{3,15},{4,0},{5,1},{6,2},{7,3},{8,4},{9,5},{1... | collective-permute-start | bytes 196616 | tf_op jit(solution)/shard_map/ppermute | solution.py:20
  95.6 2.9 %collective-permute-done.18 = bf16[32,1024]{1,0:T(8,128)(2,1)S(1)} collective-permute-done((bf16[32,1024]{1,0:T(8,128)(2,1)S(1)}, bf16[32,1024]{1,0:T(8,128)(2,1)S(1)}, u32[]{:S(2)}, u32[]{:S(2)}) %collective-permute-start.18) | collective-permute-done | bytes 65568 | tf_op jit(solution)/shard_map/ppermute | solution.py:20
  98.5 4.6 %collective-permute-done.19 = bf16[32,1024]{1,0:T(8,128)(2,1)S(1)} collective-permute-done((bf16[32,1024]{1,0:T(8,128)(2,1)S(1)}, bf16[32,1024]{1,0:T(8,128)(2,1)S(1)}, u32[]{:S(2)}, u32[]{:S(2)}) %collective-permute-start.19) | collective-permute-done | bytes 65568 | tf_op jit(solution)/shard_map/ppermute | solution.py:20
  103.4 5.3 %collective-permute-done.20 = bf16[32,1024]{1,0:T(8,128)(2,1)S(1)} collective-permute-done((bf16[32,1024]{1,0:T(8,128)(2,1)S(1)}, bf16[32,1024]{1,0:T(8,128)(2,1)S(1)}, u32[]{:S(2)}, u32[]{:S(2)}) %collective-permute-start.20) | collective-permute-done | bytes 65568 | tf_op jit(solution)/shard_map/ppermute | solution.py:20
  108.7 6.4 %collective-permute-done.21 = bf16[32,1024]{1,0:T(8,128)(2,1)S(1)} collective-permute-done((bf16[32,1024]{1,0:T(8,128)(2,1)S(1)}, bf16[32,1024]{1,0:T(8,128)(2,1)S(1)}, u32[]{:S(2)}, u32[]{:S(2)}) %collective-permute-start.21) | collective-permute-done | bytes 65568 | tf_op jit(solution)/shard_map/ppermute | solution.py:20
  115.4 2.8 %collective-permute-done.22 = bf16[32,1024]{1,0:T(8,128)(2,1)S(1)} collective-permute-done((bf16[32,1024]{1,0:T(8,128)(2,1)S(1)}, bf16[32,1024]{1,0:T(8,128)(2,1)S(1)}, u32[]{:S(2)}, u32[]{:S(2)}) %collective-permute-start.22) | collective-permute-done | bytes 65568 | tf_op jit(solution)/shard_map/ppermute | solution.py:20
  118.2 3.4 %collective-permute-start.23 = (bf16[32,1024]{1,0:T(8,128)(2,1)S(1)}, bf16[32,1024]{1,0:T(8,128)(2,1)S(1)}, u32[]{:S(2)}, u32[]{:S(2)}) collective-permute-start(bf16[32,1024]{1,0:T(8,128)(2,1)S(1)} %get-tuple-element.26), channel_id=1, source_target_pairs={{0,7},{1,8},{2,9},{3,10},{4,11},{5,12},{6,13},{7,14},{8,15},{9,0},... | collective-permute-start | bytes 196616 | tf_op jit(solution)/shard_map/ppermute | solution.py:20
  123.8 4.5 %collective-permute-done.24 = bf16[32,1024]{1,0:T(8,128)(2,1)S(1)} collective-permute-done((bf16[32,1024]{1,0:T(8,128)(2,1)S(1)}, bf16[32,1024]{1,0:T(8,128)(2,1)S(1)}, u32[]{:S(2)}, u32[]{:S(2)}) %collective-permute-start.24) | collective-permute-done | bytes 65568 | tf_op jit(solution)/shard_map/ppermute | solution.py:20
  128.3 1.9 %collective-permute-start.25 = (bf16[32,1024]{1,0:T(8,128)(2,1)S(1)}, bf16[32,1024]{1,0:T(8,128)(2,1)S(1)}, u32[]{:S(2)}, u32[]{:S(2)}) collective-permute-start(bf16[32,1024]{1,0:T(8,128)(2,1)S(1)} %get-tuple-element.24), channel_id=1, source_target_pairs={{0,5},{1,6},{2,7},{3,8},{4,9},{5,10},{6,11},{7,12},{8,13},{9,14},{... | collective-permute-start | bytes 196616 | tf_op jit(solution)/shard_map/ppermute | solution.py:20
  130.2 3.9 %collective-permute-done.25 = bf16[32,1024]{1,0:T(8,128)(2,1)S(1)} collective-permute-done((bf16[32,1024]{1,0:T(8,128)(2,1)S(1)}, bf16[32,1024]{1,0:T(8,128)(2,1)S(1)}, u32[]{:S(2)}, u32[]{:S(2)}) %collective-permute-start.25) | collective-permute-done | bytes 65568 | tf_op jit(solution)/shard_map/ppermute | solution.py:20
  (83 shorter events, 14.0 us)
Async XLA Ops:
  2.8 68.6 %collective-permute-start.14 = (bf16[32,1152]{1,0:T(8,128)(2,1)S(1)}, bf16[32,1152]{1,0:T(8,128)(2,1)S(1)}, u32[]{:S(2)}, u32[]{:S(2)}) collective-permute-start(bf16[32,1152]{1,0:T(8,128)(2,1)S(1)} %get-tuple-element.5), channel_id=1, source_target_pairs={{0,15},{1,0},{2,1},{3,2},{4,3},{5,4},{6,5},{7,6},{8,7},{9,8},{10,9... | collective-permute-start | bytes 221192 | tf_op jit(solution)/shard_map/ppermute | solution.py:20
  7.5 63.9 %collective-permute-start.13 = (bf16[32,1152]{1,0:T(8,128)(2,1)S(1)}, bf16[32,1152]{1,0:T(8,128)(2,1)S(1)}, u32[]{:S(2)}, u32[]{:S(2)}) collective-permute-start(bf16[32,1152]{1,0:T(8,128)(2,1)S(1)} %get-tuple-element.6), channel_id=1, source_target_pairs={{0,14},{1,15},{2,0},{3,1},{4,2},{5,3},{6,4},{7,5},{8,6},{9,7},{10,... | collective-permute-start | bytes 221192 | tf_op jit(solution)/shard_map/ppermute | solution.py:20
  7.5 63.8 %collective-permute-start.12 = (bf16[32,1152]{1,0:T(8,128)(2,1)S(1)}, bf16[32,1152]{1,0:T(8,128)(2,1)S(1)}, u32[]{:S(2)}, u32[]{:S(2)}) collective-permute-start(bf16[32,1152]{1,0:T(8,128)(2,1)S(1)} %get-tuple-element.7), channel_id=1, source_target_pairs={{0,13},{1,14},{2,15},{3,0},{4,1},{5,2},{6,3},{7,4},{8,5},{9,6},{10... | collective-permute-start | bytes 221192 | tf_op jit(solution)/shard_map/ppermute | solution.py:20
  8.6 62.7 %collective-permute-start.11 = (bf16[32,1152]{1,0:T(8,128)(2,1)S(1)}, bf16[32,1152]{1,0:T(8,128)(2,1)S(1)}, u32[]{:S(2)}, u32[]{:S(2)}) collective-permute-start(bf16[32,1152]{1,0:T(8,128)(2,1)S(1)} %get-tuple-element.8), channel_id=1, source_target_pairs={{0,12},{1,13},{2,14},{3,15},{4,0},{5,1},{6,2},{7,3},{8,4},{9,5},{1... | collective-permute-start | bytes 221192 | tf_op jit(solution)/shard_map/ppermute | solution.py:20
  9.6 6.6 %collective-permute-start = (bf16[32,1152]{1,0:T(8,128)(2,1)S(1)}, bf16[32,1152]{1,0:T(8,128)(2,1)S(1)}, u32[]{:S(2)}, u32[]{:S(2)}) collective-permute-start(bf16[32,1152]{1,0:T(8,128)(2,1)S(1)} %get-tuple-element.19), channel_id=1, source_target_pairs={{0,1},{1,2},{2,3},{3,4},{4,5},{5,6},{6,7},{7,8},{8,9},{9,10},{10,1... | collective-permute-start | bytes 221192 | tf_op jit(solution)/shard_map/ppermute | solution.py:20
  16.2 6.8 %collective-permute-start.1 = (bf16[32,1152]{1,0:T(8,128)(2,1)S(1)}, bf16[32,1152]{1,0:T(8,128)(2,1)S(1)}, u32[]{:S(2)}, u32[]{:S(2)}) collective-permute-start(bf16[32,1152]{1,0:T(8,128)(2,1)S(1)} %get-tuple-element.18), channel_id=1, source_target_pairs={{0,2},{1,3},{2,4},{3,5},{4,6},{5,7},{6,8},{7,9},{8,10},{9,11},{10,... | collective-permute-start | bytes 221192 | tf_op jit(solution)/shard_map/ppermute | solution.py:20
  23.0 3.8 %collective-permute-start.2 = (bf16[32,1152]{1,0:T(8,128)(2,1)S(1)}, bf16[32,1152]{1,0:T(8,128)(2,1)S(1)}, u32[]{:S(2)}, u32[]{:S(2)}) collective-permute-start(bf16[32,1152]{1,0:T(8,128)(2,1)S(1)} %get-tuple-element.17), channel_id=1, source_target_pairs={{0,3},{1,4},{2,5},{3,6},{4,7},{5,8},{6,9},{7,10},{8,11},{9,12},{10... | collective-permute-start | bytes 221192 | tf_op jit(solution)/shard_map/ppermute | solution.py:20
  26.8 4.0 %collective-permute-start.3 = (bf16[32,1152]{1,0:T(8,128)(2,1)S(1)}, bf16[32,1152]{1,0:T(8,128)(2,1)S(1)}, u32[]{:S(2)}, u32[]{:S(2)}) collective-permute-start(bf16[32,1152]{1,0:T(8,128)(2,1)S(1)} %get-tuple-element.16), channel_id=1, source_target_pairs={{0,4},{1,5},{2,6},{3,7},{4,8},{5,9},{6,10},{7,11},{8,12},{9,13},{1... | collective-permute-start | bytes 221192 | tf_op jit(solution)/shard_map/ppermute | solution.py:20
  30.7 5.9 %collective-permute-start.4 = (bf16[32,1152]{1,0:T(8,128)(2,1)S(1)}, bf16[32,1152]{1,0:T(8,128)(2,1)S(1)}, u32[]{:S(2)}, u32[]{:S(2)}) collective-permute-start(bf16[32,1152]{1,0:T(8,128)(2,1)S(1)} %get-tuple-element.15), channel_id=1, source_target_pairs={{0,5},{1,6},{2,7},{3,8},{4,9},{5,10},{6,11},{7,12},{8,13},{9,14},{... | collective-permute-start | bytes 221192 | tf_op jit(solution)/shard_map/ppermute | solution.py:20
  36.6 6.4 %collective-permute-start.5 = (bf16[32,1152]{1,0:T(8,128)(2,1)S(1)}, bf16[32,1152]{1,0:T(8,128)(2,1)S(1)}, u32[]{:S(2)}, u32[]{:S(2)}) collective-permute-start(bf16[32,1152]{1,0:T(8,128)(2,1)S(1)} %get-tuple-element.14), channel_id=1, source_target_pairs={{0,6},{1,7},{2,8},{3,9},{4,10},{5,11},{6,12},{7,13},{8,14},{9,15},... | collective-permute-start | bytes 221192 | tf_op jit(solution)/shard_map/ppermute | solution.py:20
  43.1 5.2 %collective-permute-start.6 = (bf16[32,1152]{1,0:T(8,128)(2,1)S(1)}, bf16[32,1152]{1,0:T(8,128)(2,1)S(1)}, u32[]{:S(2)}, u32[]{:S(2)}) collective-permute-start(bf16[32,1152]{1,0:T(8,128)(2,1)S(1)} %get-tuple-element.13), channel_id=1, source_target_pairs={{0,7},{1,8},{2,9},{3,10},{4,11},{5,12},{6,13},{7,14},{8,15},{9,0},... | collective-permute-start | bytes 221192 | tf_op jit(solution)/shard_map/ppermute | solution.py:20
  48.2 3.2 %collective-permute-start.7 = (bf16[32,1152]{1,0:T(8,128)(2,1)S(1)}, bf16[32,1152]{1,0:T(8,128)(2,1)S(1)}, u32[]{:S(2)}, u32[]{:S(2)}) collective-permute-start(bf16[32,1152]{1,0:T(8,128)(2,1)S(1)} %get-tuple-element.12), channel_id=1, source_target_pairs={{0,8},{1,9},{2,10},{3,11},{4,12},{5,13},{6,14},{7,15},{8,0},{9,1},... | collective-permute-start | bytes 221192 | tf_op jit(solution)/shard_map/ppermute | solution.py:20
  51.4 8.4 %collective-permute-start.8 = (bf16[32,1152]{1,0:T(8,128)(2,1)S(1)}, bf16[32,1152]{1,0:T(8,128)(2,1)S(1)}, u32[]{:S(2)}, u32[]{:S(2)}) collective-permute-start(bf16[32,1152]{1,0:T(8,128)(2,1)S(1)} %get-tuple-element.11), channel_id=1, source_target_pairs={{0,9},{1,10},{2,11},{3,12},{4,13},{5,14},{6,15},{7,0},{8,1},{9,2},... | collective-permute-start | bytes 221192 | tf_op jit(solution)/shard_map/ppermute | solution.py:20
  59.8 6.8 %collective-permute-start.9 = (bf16[32,1152]{1,0:T(8,128)(2,1)S(1)}, bf16[32,1152]{1,0:T(8,128)(2,1)S(1)}, u32[]{:S(2)}, u32[]{:S(2)}) collective-permute-start(bf16[32,1152]{1,0:T(8,128)(2,1)S(1)} %get-tuple-element.10), channel_id=1, source_target_pairs={{0,10},{1,11},{2,12},{3,13},{4,14},{5,15},{6,0},{7,1},{8,2},{9,3},... | collective-permute-start | bytes 221192 | tf_op jit(solution)/shard_map/ppermute | solution.py:20
  66.6 4.7 %collective-permute-start.10 = (bf16[32,1152]{1,0:T(8,128)(2,1)S(1)}, bf16[32,1152]{1,0:T(8,128)(2,1)S(1)}, u32[]{:S(2)}, u32[]{:S(2)}) collective-permute-start(bf16[32,1152]{1,0:T(8,128)(2,1)S(1)} %get-tuple-element.9), channel_id=1, source_target_pairs={{0,11},{1,12},{2,13},{3,14},{4,15},{5,0},{6,1},{7,2},{8,3},{9,4},{... | collective-permute-start | bytes 221192 | tf_op jit(solution)/shard_map/ppermute | solution.py:20
  71.6 0.8 copy-start
  74.2 9.1 %collective-permute-start.15 = (bf16[32,1024]{1,0:T(8,128)(2,1)S(1)}, bf16[32,1024]{1,0:T(8,128)(2,1)S(1)}, u32[]{:S(2)}, u32[]{:S(2)}) collective-permute-start(bf16[32,1024]{1,0:T(8,128)(2,1)S(1)} %get-tuple-element.34), channel_id=1, source_target_pairs={{0,15},{1,0},{2,1},{3,2},{4,3},{5,4},{6,5},{7,6},{8,7},{9,8},{10,9... | collective-permute-start | bytes 196616 | tf_op jit(solution)/shard_map/ppermute | solution.py:20
  78.5 55.7 %collective-permute-start.29 = (bf16[32,1024]{1,0:T(8,128)(2,1)S(1)}, bf16[32,1024]{1,0:T(8,128)(2,1)S(1)}, u32[]{:S(2)}, u32[]{:S(2)}) collective-permute-start(bf16[32,1024]{1,0:T(8,128)(2,1)S(1)} %get-tuple-element.20), channel_id=1, source_target_pairs={{0,1},{1,2},{2,3},{3,4},{4,5},{5,6},{6,7},{7,8},{8,9},{9,10},{10,1... | collective-permute-start | bytes 196616 | tf_op jit(solution)/shard_map/ppermute | solution.py:20
  78.5 55.7 %collective-permute-start.28 = (bf16[32,1024]{1,0:T(8,128)(2,1)S(1)}, bf16[32,1024]{1,0:T(8,128)(2,1)S(1)}, u32[]{:S(2)}, u32[]{:S(2)}) collective-permute-start(bf16[32,1024]{1,0:T(8,128)(2,1)S(1)} %get-tuple-element.21), channel_id=1, source_target_pairs={{0,2},{1,3},{2,4},{3,5},{4,6},{5,7},{6,8},{7,9},{8,10},{9,11},{10,... | collective-permute-start | bytes 196616 | tf_op jit(solution)/shard_map/ppermute | solution.py:20
  78.5 55.6 %collective-permute-start.27 = (bf16[32,1024]{1,0:T(8,128)(2,1)S(1)}, bf16[32,1024]{1,0:T(8,128)(2,1)S(1)}, u32[]{:S(2)}, u32[]{:S(2)}) collective-permute-start(bf16[32,1024]{1,0:T(8,128)(2,1)S(1)} %get-tuple-element.22), channel_id=1, source_target_pairs={{0,3},{1,4},{2,5},{3,6},{4,7},{5,8},{6,9},{7,10},{8,11},{9,12},{10... | collective-permute-start | bytes 196616 | tf_op jit(solution)/shard_map/ppermute | solution.py:20
  79.2 54.9 %collective-permute-start.26 = (bf16[32,1024]{1,0:T(8,128)(2,1)S(1)}, bf16[32,1024]{1,0:T(8,128)(2,1)S(1)}, u32[]{:S(2)}, u32[]{:S(2)}) collective-permute-start(bf16[32,1024]{1,0:T(8,128)(2,1)S(1)} %get-tuple-element.23), channel_id=1, source_target_pairs={{0,4},{1,5},{2,6},{3,7},{4,8},{5,9},{6,10},{7,11},{8,12},{9,13},{1... | collective-permute-start | bytes 196616 | tf_op jit(solution)/shard_map/ppermute | solution.py:20
  83.3 5.8 %collective-permute-start.16 = (bf16[32,1024]{1,0:T(8,128)(2,1)S(1)}, bf16[32,1024]{1,0:T(8,128)(2,1)S(1)}, u32[]{:S(2)}, u32[]{:S(2)}) collective-permute-start(bf16[32,1024]{1,0:T(8,128)(2,1)S(1)} %get-tuple-element.33), channel_id=1, source_target_pairs={{0,14},{1,15},{2,0},{3,1},{4,2},{5,3},{6,4},{7,5},{8,6},{9,7},{10,... | collective-permute-start | bytes 196616 | tf_op jit(solution)/shard_map/ppermute | solution.py:20
  89.1 4.9 %collective-permute-start.17 = (bf16[32,1024]{1,0:T(8,128)(2,1)S(1)}, bf16[32,1024]{1,0:T(8,128)(2,1)S(1)}, u32[]{:S(2)}, u32[]{:S(2)}) collective-permute-start(bf16[32,1024]{1,0:T(8,128)(2,1)S(1)} %get-tuple-element.32), channel_id=1, source_target_pairs={{0,13},{1,14},{2,15},{3,0},{4,1},{5,2},{6,3},{7,4},{8,5},{9,6},{10... | collective-permute-start | bytes 196616 | tf_op jit(solution)/shard_map/ppermute | solution.py:20
  94.0 4.4 %collective-permute-start.18 = (bf16[32,1024]{1,0:T(8,128)(2,1)S(1)}, bf16[32,1024]{1,0:T(8,128)(2,1)S(1)}, u32[]{:S(2)}, u32[]{:S(2)}) collective-permute-start(bf16[32,1024]{1,0:T(8,128)(2,1)S(1)} %get-tuple-element.31), channel_id=1, source_target_pairs={{0,12},{1,13},{2,14},{3,15},{4,0},{5,1},{6,2},{7,3},{8,4},{9,5},{1... | collective-permute-start | bytes 196616 | tf_op jit(solution)/shard_map/ppermute | solution.py:20
  98.5 4.6 %collective-permute-start.19 = (bf16[32,1024]{1,0:T(8,128)(2,1)S(1)}, bf16[32,1024]{1,0:T(8,128)(2,1)S(1)}, u32[]{:S(2)}, u32[]{:S(2)}) collective-permute-start(bf16[32,1024]{1,0:T(8,128)(2,1)S(1)} %get-tuple-element.30), channel_id=1, source_target_pairs={{0,11},{1,12},{2,13},{3,14},{4,15},{5,0},{6,1},{7,2},{8,3},{9,4},{... | collective-permute-start | bytes 196616 | tf_op jit(solution)/shard_map/ppermute | solution.py:20
  103.1 5.6 %collective-permute-start.20 = (bf16[32,1024]{1,0:T(8,128)(2,1)S(1)}, bf16[32,1024]{1,0:T(8,128)(2,1)S(1)}, u32[]{:S(2)}, u32[]{:S(2)}) collective-permute-start(bf16[32,1024]{1,0:T(8,128)(2,1)S(1)} %get-tuple-element.29), channel_id=1, source_target_pairs={{0,10},{1,11},{2,12},{3,13},{4,14},{5,15},{6,0},{7,1},{8,2},{9,3},... | collective-permute-start | bytes 196616 | tf_op jit(solution)/shard_map/ppermute | solution.py:20
  108.7 6.4 %collective-permute-start.21 = (bf16[32,1024]{1,0:T(8,128)(2,1)S(1)}, bf16[32,1024]{1,0:T(8,128)(2,1)S(1)}, u32[]{:S(2)}, u32[]{:S(2)}) collective-permute-start(bf16[32,1024]{1,0:T(8,128)(2,1)S(1)} %get-tuple-element.28), channel_id=1, source_target_pairs={{0,9},{1,10},{2,11},{3,12},{4,13},{5,14},{6,15},{7,0},{8,1},{9,2},... | collective-permute-start | bytes 196616 | tf_op jit(solution)/shard_map/ppermute | solution.py:20
  115.1 3.1 %collective-permute-start.22 = (bf16[32,1024]{1,0:T(8,128)(2,1)S(1)}, bf16[32,1024]{1,0:T(8,128)(2,1)S(1)}, u32[]{:S(2)}, u32[]{:S(2)}) collective-permute-start(bf16[32,1024]{1,0:T(8,128)(2,1)S(1)} %get-tuple-element.27), channel_id=1, source_target_pairs={{0,8},{1,9},{2,10},{3,11},{4,12},{5,13},{6,14},{7,15},{8,0},{9,1},... | collective-permute-start | bytes 196616 | tf_op jit(solution)/shard_map/ppermute | solution.py:20
  118.2 4.7 %collective-permute-start.23 = (bf16[32,1024]{1,0:T(8,128)(2,1)S(1)}, bf16[32,1024]{1,0:T(8,128)(2,1)S(1)}, u32[]{:S(2)}, u32[]{:S(2)}) collective-permute-start(bf16[32,1024]{1,0:T(8,128)(2,1)S(1)} %get-tuple-element.26), channel_id=1, source_target_pairs={{0,7},{1,8},{2,9},{3,10},{4,11},{5,12},{6,13},{7,14},{8,15},{9,0},... | collective-permute-start | bytes 196616 | tf_op jit(solution)/shard_map/ppermute | solution.py:20
  122.9 5.4 %collective-permute-start.24 = (bf16[32,1024]{1,0:T(8,128)(2,1)S(1)}, bf16[32,1024]{1,0:T(8,128)(2,1)S(1)}, u32[]{:S(2)}, u32[]{:S(2)}) collective-permute-start(bf16[32,1024]{1,0:T(8,128)(2,1)S(1)} %get-tuple-element.25), channel_id=1, source_target_pairs={{0,6},{1,7},{2,8},{3,9},{4,10},{5,11},{6,12},{7,13},{8,14},{9,15},... | collective-permute-start | bytes 196616 | tf_op jit(solution)/shard_map/ppermute | solution.py:20
  128.3 5.8 %collective-permute-start.25 = (bf16[32,1024]{1,0:T(8,128)(2,1)S(1)}, bf16[32,1024]{1,0:T(8,128)(2,1)S(1)}, u32[]{:S(2)}, u32[]{:S(2)}) collective-permute-start(bf16[32,1024]{1,0:T(8,128)(2,1)S(1)} %get-tuple-element.24), channel_id=1, source_target_pairs={{0,5},{1,6},{2,7},{3,8},{4,9},{5,10},{6,11},{7,12},{8,13},{9,14},{... | collective-permute-start | bytes 196616 | tf_op jit(solution)/shard_map/ppermute | solution.py:20

commit v6 on v3

--- a/solution.py
+++ b/solution.py
@@ -1,6 +1,10 @@
+import functools
+
 import jax
 import jax.numpy as jnp
 from jax import lax
+from jax.experimental import pallas as pl
+from jax.experimental.pallas import tpu as pltpu
 from jax.sharding import PartitionSpec as P
 
 BLOCK = 128
@@ -21,21 +25,54 @@
     return dest * capacity + within
 
 
-def attend(keys, near, sub):
-    slots = keys.shape[0]
-    scale = 4.0 / keys.shape[1]
+def attend_kernel(held_ref, cand_ref, base_col_ref, base_row_ref, out_ref, *, width):
+    slots = held_ref.shape[0]
+    block_count = cand_ref.shape[0]
+    keys = held_ref[:, :width]
+    labels = held_ref[:, width:].astype(jnp.float32)
+    labels_t = labels.T
+    index_col = lax.broadcasted_iota(jnp.int32, (slots, 1), 0)
+    index_row = lax.broadcasted_iota(jnp.int32, (1, slots), 1)
+    block_col = labels[:, 0:1].astype(jnp.int32)
+    block_row = labels_t[0:1, :].astype(jnp.int32)
+    sub_col = jnp.where(block_col > 0, labels[:, 1:2].astype(jnp.int32) - 1, -1 - index_col)
+    sub_row = jnp.where(block_row > 0, labels_t[1:2, :].astype(jnp.int32) - 1, -1 - index_row)
+    global_col = jnp.where(block_col > 0, base_col_ref[...] + block_col - 1, 0)
+    global_row = jnp.where(block_row > 0, base_row_ref[...] + block_row - 1, 0)
+    onehot = (global_col == lax.broadcasted_iota(jnp.int32, (1, block_count), 1)).astype(jnp.bfloat16)
+    onehot_t = (lax.broadcasted_iota(jnp.int32, (block_count, 1), 0) == global_row).astype(
+        jnp.bfloat16
+    )
+    cand_rows = jnp.dot(onehot, cand_ref[...], preferred_element_type=jnp.float32)
+    near = jnp.dot(cand_rows.astype(jnp.bfloat16), onehot_t, preferred_element_type=jnp.float32) > 0.5
+    scale = 4.0 / width
     scores = scale * lax.dot_general(
         keys, keys, (((1,), (1,)), ((), ())), preferred_element_type=jnp.float32
     )
-    index = jnp.arange(slots, dtype=jnp.int32)
-    same = (index[:, None] == index[None, :]) | (
-        (sub[:, None] == sub[None, :]) & near
+    same = (index_col == index_row) | ((sub_col == sub_row) & near)
+    top = jnp.max(jnp.where(same, scores, jnp.float32(-1e30)), axis=1, keepdims=True)
+    weights = jnp.where(same, jnp.exp(scores - top), jnp.float32(0.0))
+    total = jnp.sum(weights, axis=1, keepdims=True)
+    summed = jnp.dot(weights.astype(jnp.bfloat16), keys, preferred_element_type=jnp.float32)
+    out_ref[...] = (summed / total).astype(out_ref.dtype)
+
+
+def attend(held, cand, capacity, local_blocks, width):
+    slots = held.shape[0]
+    base = jnp.arange(slots, dtype=jnp.int32) // capacity * local_blocks
+    vmem = pl.BlockSpec(memory_space=pltpu.VMEM)
+    cost = pl.CostEstimate(
+        flops=4 * slots * slots * width,
+        transcendentals=slots * slots,
+        bytes_accessed=held.size * 2 + slots * width * 2,
     )
-    top = jnp.max(jnp.where(same, scores, jnp.float32(-1e30)), axis=1)
-    weights = jnp.where(same, jnp.exp(scores - top[:, None]), jnp.float32(0.0))
-    total = jnp.sum(weights, axis=1)
-    summed = jnp.dot(weights.astype(jnp.bfloat16), keys, preferred_element_type=jnp.float32)
-    return (summed / total[:, None]).astype(jnp.bfloat16)
+    return pl.pallas_call(
+        functools.partial(attend_kernel, width=width),
+        out_shape=jax.ShapeDtypeStruct((slots, width), jnp.bfloat16),
+        in_specs=[vmem] * 4,
+        out_specs=vmem,
+        cost_estimate=cost,
+    )(held, cand.astype(jnp.bfloat16), base[:, None], base[None, :])
 
 
 def body(emb, row_owner, row_sub, cand):
@@ -61,30 +98,7 @@
     )
     send = jnp.dot(placing, labelled, preferred_element_type=jnp.float32).astype(jnp.bfloat16)
     held = lax.all_to_all(send, axes, split_axis=0, concat_axis=0, tiled=True)
-    held_emb = held[:, :width]
-    held_labels = held[:, width : width + 2].astype(jnp.int32)
-
-    index = jnp.arange(slots, dtype=jnp.int32)
-    present = held_labels[:, 0] > 0
-    source = index // capacity
-    global_block = source * local_blocks + held_labels[:, 0] - 1
-    global_block = jnp.where(present, global_block, 0)
-    sub = jnp.where(present, held_labels[:, 1] - 1, -1 - index)
-    block_count = cand.shape[1]
-    block_onehot = (
-        global_block[:, None] == jnp.arange(block_count, dtype=jnp.int32)[None, :]
-    ).astype(jnp.bfloat16)
-    cand_rows = jnp.dot(block_onehot, cand.astype(jnp.bfloat16), preferred_element_type=jnp.float32)
-    near = (
-        lax.dot_general(
-            cand_rows.astype(jnp.bfloat16),
-            block_onehot,
-            (((1,), (1,)), ((), ())),
-            preferred_element_type=jnp.float32,
-        )
-        > 0.5
-    )
-    averaged = attend(held_emb, near, sub)
+    averaged = attend(held, cand, capacity, local_blocks, width)
     returned = lax.all_to_all(averaged, axes, split_axis=0, concat_axis=0, tiled=True)
     result = lax.dot_general(
         placing, returned, (((0,), (0,)), ((), ())), preferred_element_type=jnp.float32

time: 74.1 us -> 78.4 us (1.058)
  blocking collectives: 66.2 us -> 30.4 us
  waiting for transfers between devices: 0 us -> 27.1 us
  starting transfers between devices: 0 us -> 7.44 us
  Pallas kernels: 0 us -> 4.34 us
  matrix products: 5.22 us -> 4.06 us
  other arithmetic: 1.57 us -> 2.65 us
  local copies, waits for them, and re-layouts: 0.16 us -> 1.17 us
    all_to_all x1 -> x0, blocking collectives: 36.5 us -> none  [body(): held = lax.all_to_all(send, axes, split_axis=0, concat_axis=0, tiled=True)]
    all_to_all x0 -> x1, waiting for transfers between devices: none -> 27.1 us  [body(): held = lax.all_to_all(send, axes, split_axis=0, concat_axis=0, tiled=True)]
    all_to_all x0 -> x1, starting transfers between devices: none -> 7.44 us  [body(): held = lax.all_to_all(send, axes, split_axis=0, concat_axis=0, tiled=True)]
    pallas_call x0 -> x1, Pallas kernels: none -> 4.34 us  [attend(): pl.pallas_call(functools.partial(attend_kernel, width=width), out_shape=j...]
    dot_general x3 -> x0, matrix products: 2.18 us -> none  [the longest x1 0.75 us: attend(): jnp.dot(weights.astype(jnp.bfloat16), keys, preferred_element_type=jnp.fl...]
    mul x0 -> x2, other arithmetic: none -> 1.32 us  [attend(): base = jnp.arange(slots, dtype=jnp.int32) // capacity * local_blocks]
    dot_general x1, matrix products: 1.55 us -> 2.58 us  [body(): jnp.dot(placing, labelled, preferred_element_type=jnp.float32)]
    unnamed x3 -> x5, local copies, waits for them, and re-layouts: 0.15 us -> 1.17 us
  transfers between devices with their start and end apart: 0 -> 1, of which waited for: 0 -> 1; matrix products, arithmetic and copies ran while one was open for 0% -> 2% of each run, Pallas kernels for 0% -> 0%
where the time goes in v6:
time: 78.4 us; the launch traced here: 77.2 us
  blocking collectives  30.4 us (39%)
  waiting for transfers between devices  27.1 us (35%)
  starting transfers between devices  7.44 us (9%)
  Pallas kernels  4.34 us (6%)
  matrix products  4.06 us (5%)
  other arithmetic  2.65 us (3%)
  local copies, waits for them, and re-layouts  1.17 us (1%)
    all_to_all x1, blocking collectives, body(): lax.all_to_all(averaged, axes, split_axis=0, concat_axis=0, tiled=True)  30.4 us
    all_to_all x1, waiting for transfers between devices, body(): held = lax.all_to_all(send, axes, split_axis=0, concat_axis=0, tiled=True)  27.1 us
    all_to_all x1, starting transfers between devices, body(): held = lax.all_to_all(send, axes, split_axis=0, concat_axis=0, tiled=True)  7.44 us
    pallas_call x1, Pallas kernels, attend(): pl.pallas_call(functools.partial(attend_kernel, width=width), out_shape=j...  4.34 us
    dot_general x1, matrix products, body(): jnp.dot(placing, labelled, preferred_element_type=jnp.float32)  2.58 us
  transfers between devices with their start and end apart: 1, of which 1 were waited for; matrix products, arithmetic and copies ran while one was open for 2% of the time, Pallas kernels for 0%

profile of v6, /device:TPU:1, one launch (start us, length us, event | category | flops | bytes accessed | tf_op | source)
XLA Modules:
  0.0 77.2 jit_solution(3912809601024265428)
XLA Ops:
  0.0 0.7 fusion.17
  0.7 0.2 fusion.1
  1.0 0.1 copy.6
  1.1 2.6 %convolution_convert_fusion = bf16[512,1152]{1,0:T(8,128)(2,1)} fusion(bf16[256,2]{1,0:T(8,128)(2,1)S(1)} %copy.6, bf16[256,1024]{1,0:T(8,128)(2,1)} %param.4, s32[256]{0:T(256)S(1)} %convert_add_fusion), kind=kOutput, calls=%fused_computation | convolution fusion | flops 304480256 | bytes 1705984 | tf_op jit(solution)/shard_map/dot_general | solution.py:99
  3.7 0.0 copy-start.1
  3.7 7.4 %all-to-all-start = ((bf16[16,32,1152]{2,1,0:T(8,128)(2,1)}), bf16[16,32,1152]{2,1,0:T(8,128)(2,1)S(1)}, u32[]{:S(2)}, u32[]{:S(2)}) async-start(bf16[16,32,1152]{2,1,0:T(8,128)(2,1)} %bitcast), calls=%async_computation | async-start | bytes 2359296 | tf_op jit(solution)/shard_map/all_to_all | solution.py:100
  11.1 0.0 copy-done.1
  11.1 0.6 convert_element_type.27.cand_ref
  11.7 0.6 fusion.16.base_row_ref
  12.3 0.7 fusion.8.base_col_ref
  13.1 27.1 %all-to-all-done = bf16[16,32,1152]{2,1,0:T(8,128)(2,1)S(1)} async-done(((bf16[16,32,1152]{2,1,0:T(8,128)(2,1)}), bf16[16,32,1152]{2,1,0:T(8,128)(2,1)S(1)}, u32[]{:S(2)}, u32[]{:S(2)}) %all-to-all-start) | async-done | bytes 1179680 | tf_op jit(solution)/shard_map/all_to_all | solution.py:100
  40.2 0.0 copy-start
  40.2 1.0 %copy-done = bf16[16,32,1152]{2,1,0:T(8,128)(2,1)} copy-done((bf16[16,32,1152]{2,1,0:T(8,128)(2,1)}, bf16[16,32,1152]{2,1,0:T(8,128)(2,1)S(1)}, u32[]{:S(2)}) %copy-start) | copy-done | bytes 1179672
  41.2 4.3 %shard_map.46 = bf16[512,1024]{1,0:T(8,128)(2,1)} custom-call(bf16[512,1152]{1,0:T(8,128)(2,1)} %bitcast.6, bf16[32,32]{1,0:T(8,128)(2,1)} %convert_element_type.27.cand_ref, s32[512,1]{1,0:T(8,128)} %fusion.8.base_col_ref, s32[1,512]{1,0:T(1,128)} %fusion.16.base_row_ref), custom_call_target="tpu_custom_call" | custom-call | flops 1073741824 | bytes 2228224 | tf_op jit(solution)/shard_map/pallas_call | solution.py:69
  45.5 30.4 %all_to_all.23 = bf16[16,32,1024]{2,1,0:T(8,128)(2,1)S(1)} all-to-all(bf16[16,32,1024]{2,1,0:T(8,128)(2,1)} %bitcast.7), channel_id=1, replica_groups=mesh['groups'=2,'owner'=4,'loop'=4] {'owner','loop'}, dimensions={0} | all-to-all | bytes 2097152 | tf_op jit(solution)/shard_map/all_to_all | solution.py:102
  75.9 1.3 %convolution_convert_fusion.1 = bf16[256,1024]{1,0:T(8,128)(2,1)} fusion(bf16[512,1024]{1,0:T(8,128)(2,1)S(1)} %bitcast.5, s32[256]{0:T(256)S(1)} %convert_add_fusion), kind=kOutput, calls=%fused_computation.1 | convolution fusion | flops 268828672 | bytes 1573888 | tf_op jit(solution)/shard_map/dot_general | solution.py:103
  (4 shorter events, 0.0 us)
Async XLA Ops:
  3.7 7.4 %copy-start.1 = (s32[32,32]{1,0:T(8,128)S(1)}, s32[32,32]{1,0:T(8,128)}, u32[]{:S(2)}) copy-start(s32[32,32]{1,0:T(8,128)} %param.7) | copy-start | bytes 12292
  3.7 36.5 %all-to-all-start = ((bf16[16,32,1152]{2,1,0:T(8,128)(2,1)}), bf16[16,32,1152]{2,1,0:T(8,128)(2,1)S(1)}, u32[]{:S(2)}, u32[]{:S(2)}) async-start(bf16[16,32,1152]{2,1,0:T(8,128)(2,1)} %bitcast), calls=%async_computation | async-start | bytes 2359296 | tf_op jit(solution)/shard_map/all_to_all | solution.py:100
  40.2 1.0 %copy-start = (bf16[16,32,1152]{2,1,0:T(8,128)(2,1)}, bf16[16,32,1152]{2,1,0:T(8,128)(2,1)S(1)}, u32[]{:S(2)}) copy-start(bf16[16,32,1152]{2,1,0:T(8,128)(2,1)S(1)} %all-to-all-done) | copy-start | bytes 3538948

commit v7 on v3

--- a/solution.py
+++ b/solution.py
@@ -1,6 +1,10 @@
+import functools
+
 import jax
 import jax.numpy as jnp
 from jax import lax
+from jax.experimental import pallas as pl
+from jax.experimental.pallas import tpu as pltpu
 from jax.sharding import PartitionSpec as P
 
 BLOCK = 128
@@ -8,17 +12,55 @@
 LABEL_COLUMNS = 128
 
 
-def route(row_owner, row_sub, loop_count, capacity):
-    devices = lax.axis_size("owner") * loop_count
-    dest = row_owner * loop_count + row_sub % loop_count
-    onehot = (dest[:, None] == jnp.arange(devices, dtype=jnp.int32)[None, :]).astype(jnp.bfloat16)
-    rows = row_owner.shape[0]
-    lower = (
-        jnp.arange(rows, dtype=jnp.int32)[:, None] > jnp.arange(rows, dtype=jnp.int32)[None, :]
+def place_kernel(emb_ref, owner_ref, sub_ref, send_ref, slot_ref, *, loop_count, capacity, devices):
+    rows, width = emb_ref.shape
+    slots = send_ref.shape[0]
+    owner = owner_ref[...]
+    sub = sub_ref[...]
+    dest = owner * loop_count + sub % loop_count
+    onehot_t = (lax.broadcasted_iota(jnp.int32, (devices, rows), 0) == dest).astype(jnp.bfloat16)
+    upper = (
+        lax.broadcasted_iota(jnp.int32, (rows, rows), 0)
+        < lax.broadcasted_iota(jnp.int32, (rows, rows), 1)
     ).astype(jnp.bfloat16)
-    earlier = jnp.dot(lower, onehot, preferred_element_type=jnp.float32)
-    within = jnp.sum(earlier * onehot.astype(jnp.float32), axis=1).astype(jnp.int32)
-    return dest * capacity + within
+    earlier_t = jnp.dot(onehot_t, upper, preferred_element_type=jnp.float32)
+    within = jnp.sum(earlier_t * onehot_t.astype(jnp.float32), axis=0, keepdims=True)
+    slot = dest * capacity + within.astype(jnp.int32)
+    slot_ref[...] = slot
+    placing = (lax.broadcasted_iota(jnp.int32, (slots, rows), 0) == slot).astype(jnp.bfloat16)
+    send_ref[:, :width] = jnp.dot(
+        placing, emb_ref[...], preferred_element_type=jnp.float32
+    ).astype(send_ref.dtype)
+    which = lax.broadcasted_iota(jnp.int32, (LABEL_COLUMNS, rows), 0)
+    block = lax.broadcasted_iota(jnp.int32, (LABEL_COLUMNS, rows), 1) // BLOCK
+    labels_t = jnp.where(which == 0, block + 1, jnp.where(which == 1, sub + 1, 0))
+    labels = labels_t.astype(jnp.float32).T.astype(jnp.bfloat16)
+    send_ref[:, width:] = jnp.dot(
+        placing, labels, preferred_element_type=jnp.float32
+    ).astype(send_ref.dtype)
+
+
+def place(emb, row_owner, row_sub, loop_count, capacity, devices):
+    rows, width = emb.shape
+    slots = devices * capacity
+    vmem = pl.BlockSpec(memory_space=pltpu.VMEM)
+    cost = pl.CostEstimate(
+        flops=2 * slots * rows * (width + LABEL_COLUMNS) + 2 * devices * rows * rows,
+        transcendentals=0,
+        bytes_accessed=rows * width * 2 + slots * (width + LABEL_COLUMNS) * 2,
+    )
+    return pl.pallas_call(
+        functools.partial(
+            place_kernel, loop_count=loop_count, capacity=capacity, devices=devices
+        ),
+        out_shape=(
+            jax.ShapeDtypeStruct((slots, width + LABEL_COLUMNS), jnp.bfloat16),
+            jax.ShapeDtypeStruct((1, rows), jnp.int32),
+        ),
+        in_specs=[vmem] * 3,
+        out_specs=(vmem, vmem),
+        cost_estimate=cost,
+    )(emb, row_owner[None, :], row_sub[None, :])
 
 
 def attend(keys, near, sub):
@@ -48,18 +90,12 @@
     local_blocks = rows // BLOCK
     axes = ("owner", "loop")
 
-    slot_of_row = route(row_owner, row_sub, loop_count, capacity)
+    send, slot_of_row = place(emb, row_owner, row_sub, loop_count, capacity, devices)
+    slot_of_row = slot_of_row[0]
     placing = (jnp.arange(slots, dtype=jnp.int32)[:, None] == slot_of_row[None, :]).astype(
         jnp.bfloat16
     )
     width = emb.shape[1]
-    row_labels = jnp.stack(
-        [jnp.arange(rows, dtype=jnp.int32) // BLOCK + 1, row_sub + 1], axis=1
-    ).astype(jnp.bfloat16)
-    labelled = jnp.concatenate(
-        [emb, jnp.pad(row_labels, ((0, 0), (0, LABEL_COLUMNS - 2)))], axis=1
-    )
-    send = jnp.dot(placing, labelled, preferred_element_type=jnp.float32).astype(jnp.bfloat16)
     held = lax.all_to_all(send, axes, split_axis=0, concat_axis=0, tiled=True)
     held_emb = held[:, :width]
     held_labels = held[:, width : width + 2].astype(jnp.int32)

time: 74.1 us -> 74.4 us (level)
  Pallas kernels: 0 us -> 2.73 us
  matrix products: 5.22 us -> 3.47 us
    pallas_call x0 -> x1, Pallas kernels: none -> 2.73 us  [place(): pl.pallas_call(functools.partial(place_kernel, loop_count=loop_count, cap...]
    dot_general x2 -> x0, matrix products: 1.75 us -> none  [the longest x1 1.55 us: body(): jnp.dot(placing, labelled, preferred_element_type=jnp.float32)]
where the time goes in v7:
time: 74.4 us; the launch traced here: 73.5 us
  blocking collectives  66.4 us (89%)
  matrix products  3.47 us (5%)
  Pallas kernels  2.73 us (4%)
  other arithmetic  0.84 us (1%)
    all_to_all x1, blocking collectives, body(): held = lax.all_to_all(send, axes, split_axis=0, concat_axis=0, tiled=True)  36.7 us
    all_to_all x1, blocking collectives, body(): lax.all_to_all(averaged, axes, split_axis=0, concat_axis=0, tiled=True)  29.7 us
    pallas_call x1, Pallas kernels, place(): pl.pallas_call(functools.partial(place_kernel, loop_count=loop_count, cap...  2.73 us

profile of v7, /device:TPU:1, one launch (start us, length us, event | category | flops | bytes accessed | tf_op | source)
XLA Modules:
  0.0 73.5 jit_solution(17857172629379542935)
XLA Ops:
  0.0 2.7 %shard_map.46 = (bf16[512,1152]{1,0:T(8,128)(2,1)}, s32[1,256]{1,0:T(1,128)}) custom-call(bf16[256,1024]{1,0:T(8,128)(2,1)} %emb_ref.1, s32[1,256]{1,0:T(1,128)} %bitcast.15, s32[1,256]{1,0:T(1,128)} %bitcast.16), custom_call_target="tpu_custom_call" | custom-call | flops 304087040 | bytes 1703936 | tf_op jit(solution)/shard_map/pallas_call | solution.py:52
  2.7 36.7 %all_to_all.24 = bf16[16,32,1152]{2,1,0:T(8,128)(2,1)S(1)} all-to-all(bf16[16,32,1152]{2,1,0:T(8,128)(2,1)} %bitcast.12), channel_id=1, replica_groups=mesh['groups'=2,'owner'=4,'loop'=4] {'owner','loop'}, dimensions={0} | all-to-all | bytes 2359296 | tf_op jit(solution)/shard_map/all_to_all | solution.py:99
  39.4 0.0 copy-start.1
  39.4 0.7 %convolution_multiply_fusion = f32[512,512]{0,1:T(8,128)S(1)} fusion(bf16[512,1152]{1,0:T(8,128)(2,1)S(1)} %bitcast.10), kind=kOutput, calls=%fused_computation.1 | convolution fusion | flops 537133056 | bytes 2097152 | tf_op jit(solution)/shard_map/dot_general | solution.py:69
  40.2 0.1 fusion.24
  40.3 0.4 fusion.13
  40.7 0.0 copy-done.1
  40.7 0.7 select_reduce_fusion
  41.4 0.3 fusion.4
  41.7 0.8 %divide_convert_fusion = bf16[512,1024]{1,0:T(8,128)(2,1)S(1)} fusion(f32[512]{0:T(512)S(1)} %fusion.4, bf16[512,1152]{1,0:T(8,128)(2,1)S(1)} %bitcast.11, pred[512,512]{0,1:T(32,128)(4,1)S(1)} %get-tuple-element.15, f32[512,512]{0,1:T(8,128)S(1)} %convolution_multiply_fusion, f32[512]{0:T(512)S(1)} %get-tuple-element.14), kind=kOutput, calls=%fused_computation | convolution fusion | flops 538705920 | bytes 3411968 | tf_op jit(solution)/shard_map/dot_general | solution.py:79
  42.5 0.0 copy-start
  42.5 29.7 %all_to_all.25 = bf16[16,32,1024]{2,1,0:T(8,128)(2,1)S(1)} all-to-all(bf16[16,32,1024]{2,1,0:T(8,128)(2,1)S(1)} %bitcast.13), channel_id=1, replica_groups=mesh['groups'=2,'owner'=4,'loop'=4] {'owner','loop'}, dimensions={0} | all-to-all | bytes 2097152 | tf_op jit(solution)/shard_map/all_to_all | solution.py:124
  72.2 0.0 copy-done
  72.2 1.3 %convolution_convert_fusion = bf16[256,1024]{1,0:T(8,128)(2,1)} fusion(bf16[512,1024]{1,0:T(8,128)(2,1)S(1)} %bitcast.8, s32[256]{0:T(256)S(1)} %bitcast.14), kind=kOutput, calls=%fused_computation.2 | convolution fusion | flops 268828672 | bytes 1573888 | tf_op jit(solution)/shard_map/dot_general | solution.py:125
  (2 shorter events, 0.0 us)
Async XLA Ops:
  39.4 1.3 %copy-start.1 = (s32[32,32]{1,0:T(8,128)S(1)}, s32[32,32]{1,0:T(8,128)}, u32[]{:S(2)}) copy-start(s32[32,32]{1,0:T(8,128)} %param.7) | copy-start | bytes 12292
  42.5 29.7 %copy-start = (s32[1,256]{1,0:T(1,128)S(1)}, s32[1,256]{1,0:T(1,128)}, u32[]{:S(2)}) copy-start(s32[1,256]{1,0:T(1,128)} %get-tuple-element.7) | copy-start | bytes 3076

commit v8 on v7

--- a/solution.py
+++ b/solution.py
@@ -10,55 +10,78 @@
 BLOCK = 128
 SUB = 16
 LABEL_COLUMNS = 128
+PLACE_STEP = 128
 
 
-def place_kernel(emb_ref, owner_ref, sub_ref, send_ref, slot_ref, *, loop_count, capacity, devices):
+def place_kernel(
+    emb_ref, owner_ref, sub_ref, send_ref, slot_ref, labels_ref, *, loop_count, capacity, devices
+):
     rows, width = emb_ref.shape
-    slots = send_ref.shape[0]
-    owner = owner_ref[...]
-    sub = sub_ref[...]
-    dest = owner * loop_count + sub % loop_count
-    onehot_t = (lax.broadcasted_iota(jnp.int32, (devices, rows), 0) == dest).astype(jnp.bfloat16)
-    upper = (
-        lax.broadcasted_iota(jnp.int32, (rows, rows), 0)
-        < lax.broadcasted_iota(jnp.int32, (rows, rows), 1)
+    step_slots = send_ref.shape[0]
+    step = pl.program_id(0)
+
+    @pl.when(step == 0)
+    def _():
+        owner = owner_ref[...]
+        sub = sub_ref[...]
+        dest = owner * loop_count + sub % loop_count
+        onehot_t = (lax.broadcasted_iota(jnp.int32, (devices, rows), 0) == dest).astype(
+            jnp.bfloat16
+        )
+        upper = (
+            lax.broadcasted_iota(jnp.int32, (rows, rows), 0)
+            < lax.broadcasted_iota(jnp.int32, (rows, rows), 1)
+        ).astype(jnp.bfloat16)
+        earlier_t = jnp.dot(onehot_t, upper, preferred_element_type=jnp.float32)
+        within = jnp.sum(earlier_t * onehot_t.astype(jnp.float32), axis=0, keepdims=True)
+        slot_ref[...] = dest * capacity + within.astype(jnp.int32)
+        which = lax.broadcasted_iota(jnp.int32, (LABEL_COLUMNS, rows), 0)
+        block = lax.broadcasted_iota(jnp.int32, (LABEL_COLUMNS, rows), 1) // BLOCK
+        labels_t = jnp.where(which == 0, block + 1, jnp.where(which == 1, sub + 1, 0))
+        labels_ref[...] = labels_t.astype(jnp.float32).T.astype(jnp.bfloat16)
+
+    first = step * step_slots
+    placing = (
+        lax.broadcasted_iota(jnp.int32, (step_slots, rows), 0) + first == slot_ref[...]
     ).astype(jnp.bfloat16)
-    earlier_t = jnp.dot(onehot_t, upper, preferred_element_type=jnp.float32)
-    within = jnp.sum(earlier_t * onehot_t.astype(jnp.float32), axis=0, keepdims=True)
-    slot = dest * capacity + within.astype(jnp.int32)
-    slot_ref[...] = slot
-    placing = (lax.broadcasted_iota(jnp.int32, (slots, rows), 0) == slot).astype(jnp.bfloat16)
     send_ref[:, :width] = jnp.dot(
         placing, emb_ref[...], preferred_element_type=jnp.float32
     ).astype(send_ref.dtype)
-    which = lax.broadcasted_iota(jnp.int32, (LABEL_COLUMNS, rows), 0)
-    block = lax.broadcasted_iota(jnp.int32, (LABEL_COLUMNS, rows), 1) // BLOCK
-    labels_t = jnp.where(which == 0, block + 1, jnp.where(which == 1, sub + 1, 0))
-    labels = labels_t.astype(jnp.float32).T.astype(jnp.bfloat16)
     send_ref[:, width:] = jnp.dot(
-        placing, labels, preferred_element_type=jnp.float32
+        placing, labels_ref[...], preferred_element_type=jnp.float32
     ).astype(send_ref.dtype)
 
 
 def place(emb, row_owner, row_sub, loop_count, capacity, devices):
     rows, width = emb.shape
     slots = devices * capacity
-    vmem = pl.BlockSpec(memory_space=pltpu.VMEM)
+    step_slots = min(slots, PLACE_STEP)
     cost = pl.CostEstimate(
         flops=2 * slots * rows * (width + LABEL_COLUMNS) + 2 * devices * rows * rows,
         transcendentals=0,
         bytes_accessed=rows * width * 2 + slots * (width + LABEL_COLUMNS) * 2,
     )
+    whole = lambda step: (0, 0)
     return pl.pallas_call(
         functools.partial(
             place_kernel, loop_count=loop_count, capacity=capacity, devices=devices
         ),
+        grid=(slots // step_slots,),
         out_shape=(
             jax.ShapeDtypeStruct((slots, width + LABEL_COLUMNS), jnp.bfloat16),
             jax.ShapeDtypeStruct((1, rows), jnp.int32),
         ),
-        in_specs=[vmem] * 3,
-        out_specs=(vmem, vmem),
+        in_specs=[
+            pl.BlockSpec((rows, width), whole),
+            pl.BlockSpec((1, rows), whole),
+            pl.BlockSpec((1, rows), whole),
+        ],
+        out_specs=(
+            pl.BlockSpec((step_slots, width + LABEL_COLUMNS), lambda step: (step, 0)),
+            pl.BlockSpec((1, rows), whole),
+        ),
+        scratch_shapes=[pltpu.VMEM((rows, LABEL_COLUMNS), jnp.bfloat16)],
+        compiler_params=pltpu.CompilerParams(dimension_semantics=("arbitrary",)),
         cost_estimate=cost,
     )(emb, row_owner[None, :], row_sub[None, :])
 

time: 74.4 us -> 75.1 us (level)
  no operation moved by 1% of the time
where the time goes in v8:
time: 75.1 us; the launch traced here: 74.2 us
  blocking collectives  66.4 us (88%)
  matrix products  3.47 us (5%)
  Pallas kernels  3.42 us (5%)
  other arithmetic  0.84 us (1%)
    all_to_all x1, blocking collectives, body(): held = lax.all_to_all(send, axes, split_axis=0, concat_axis=0, tiled=True)  36.7 us
    all_to_all x1, blocking collectives, body(): lax.all_to_all(averaged, axes, split_axis=0, concat_axis=0, tiled=True)  29.7 us
    pallas_call x1, Pallas kernels, place(): pl.pallas_call(functools.partial(place_kernel, loop_count=loop_count, cap...  3.42 us

profile of v8, /device:TPU:1, one launch (start us, length us, event | category | flops | bytes accessed | tf_op | source)
XLA Modules:
  0.0 74.2 jit_solution(13563999503752272453)
XLA Ops:
  0.0 3.4 %shard_map.46 = (bf16[512,1152]{1,0:T(8,128)(2,1)}, s32[1,256]{1,0:T(1,128)}) custom-call(bf16[256,1024]{1,0:T(8,128)(2,1)} %emb_ref.1, s32[1,256]{1,0:T(1,128)} %bitcast.15, s32[1,256]{1,0:T(1,128)} %bitcast.16), custom_call_target="tpu_custom_call" | custom-call | flops 304087040 | bytes 1703936 | tf_op jit(solution)/shard_map/pallas_call | solution.py:65
  3.4 36.7 %all_to_all.24 = bf16[16,32,1152]{2,1,0:T(8,128)(2,1)S(1)} all-to-all(bf16[16,32,1152]{2,1,0:T(8,128)(2,1)} %bitcast.12), channel_id=1, replica_groups=mesh['groups'=2,'owner'=4,'loop'=4] {'owner','loop'}, dimensions={0} | all-to-all | bytes 2359296 | tf_op jit(solution)/shard_map/all_to_all | solution.py:122
  40.1 0.0 copy-start.1
  40.1 0.7 convolution_multiply_fusion
  40.9 0.1 fusion.24
  41.0 0.4 fusion.13
  41.4 0.0 copy-done.1
  41.4 0.7 select_reduce_fusion
  42.1 0.3 fusion.4
  42.4 0.8 %divide_convert_fusion = bf16[512,1024]{1,0:T(8,128)(2,1)S(1)} fusion(f32[512]{0:T(512)S(1)} %fusion.4, bf16[512,1152]{1,0:T(8,128)(2,1)S(1)} %bitcast.11, pred[512,512]{0,1:T(32,128)(4,1)S(1)} %get-tuple-element.15, f32[512,512]{0,1:T(8,128)S(1)} %convolution_multiply_fusion, f32[512]{0:T(512)S(1)} %get-tuple-element.14), kind=kOutput, calls=%fused_computation | convolution fusion | flops 538705920 | bytes 3411968 | tf_op jit(solution)/shard_map/dot_general | solution.py:102
  43.1 0.0 copy-start
  43.2 29.7 %all_to_all.25 = bf16[16,32,1024]{2,1,0:T(8,128)(2,1)S(1)} all-to-all(bf16[16,32,1024]{2,1,0:T(8,128)(2,1)S(1)} %bitcast.13), channel_id=1, replica_groups=mesh['groups'=2,'owner'=4,'loop'=4] {'owner','loop'}, dimensions={0} | all-to-all | bytes 2097152 | tf_op jit(solution)/shard_map/all_to_all | solution.py:147
  72.9 0.0 copy-done
  72.9 1.3 %convolution_convert_fusion = bf16[256,1024]{1,0:T(8,128)(2,1)} fusion(bf16[512,1024]{1,0:T(8,128)(2,1)S(1)} %bitcast.8, s32[256]{0:T(256)S(1)} %bitcast.14), kind=kOutput, calls=%fused_computation.2 | convolution fusion | flops 268828672 | bytes 1573888 | tf_op jit(solution)/shard_map/dot_general | solution.py:148
  (2 shorter events, 0.0 us)
Async XLA Ops:
  40.1 1.3 %copy-start.1 = (s32[32,32]{1,0:T(8,128)S(1)}, s32[32,32]{1,0:T(8,128)}, u32[]{:S(2)}) copy-start(s32[32,32]{1,0:T(8,128)} %param.7) | copy-start | bytes 12292
  43.1 29.7 %copy-start = (s32[1,256]{1,0:T(1,128)S(1)}, s32[1,256]{1,0:T(1,128)}, u32[]{:S(2)}) copy-start(s32[1,256]{1,0:T(1,128)} %get-tuple-element.7) | copy-start | bytes 3076

commit v9 on v7

--- a/solution.py
+++ b/solution.py
@@ -10,11 +10,14 @@
 BLOCK = 128
 SUB = 16
 LABEL_COLUMNS = 128
+TILE = 16
 
 
-def place_kernel(emb_ref, owner_ref, sub_ref, send_ref, slot_ref, *, loop_count, capacity, devices):
+def place_kernel(
+    emb_ref, owner_ref, sub_ref, send_ref, slot_ref, *, loop_count, capacity, devices, tiled
+):
     rows, width = emb_ref.shape
-    slots = send_ref.shape[0]
+    slots = devices * capacity
     owner = owner_ref[...]
     sub = sub_ref[...]
     dest = owner * loop_count + sub % loop_count
@@ -28,19 +31,39 @@
     slot = dest * capacity + within.astype(jnp.int32)
     slot_ref[...] = slot
     placing = (lax.broadcasted_iota(jnp.int32, (slots, rows), 0) == slot).astype(jnp.bfloat16)
-    send_ref[:, :width] = jnp.dot(
-        placing, emb_ref[...], preferred_element_type=jnp.float32
-    ).astype(send_ref.dtype)
+    placed = jnp.dot(placing, emb_ref[...], preferred_element_type=jnp.float32).astype(
+        send_ref.dtype
+    )
     which = lax.broadcasted_iota(jnp.int32, (LABEL_COLUMNS, rows), 0)
     block = lax.broadcasted_iota(jnp.int32, (LABEL_COLUMNS, rows), 1) // BLOCK
-    labels_t = jnp.where(which == 0, block + 1, jnp.where(which == 1, sub + 1, 0))
+    column = 0
+    if tiled:
+        column = slot % capacity // TILE * 2
+    labels_t = jnp.where(which == column, block + 1, jnp.where(which == column + 1, sub + 1, 0))
     labels = labels_t.astype(jnp.float32).T.astype(jnp.bfloat16)
-    send_ref[:, width:] = jnp.dot(
-        placing, labels, preferred_element_type=jnp.float32
-    ).astype(send_ref.dtype)
+    placed_labels = jnp.dot(placing, labels, preferred_element_type=jnp.float32).astype(
+        send_ref.dtype
+    )
+    if not tiled:
+        send_ref[:, :width] = placed
+        send_ref[:, width:] = placed_labels
+        return
+    row_tiles = capacity // TILE
+    col_tiles = width // LABEL_COLUMNS
+    for chunk in range(devices):
+        base = chunk * capacity
+        for a in range(row_tiles):
+            for e in range(col_tiles):
+                send_ref[chunk, (a * col_tiles + e) * TILE : (a * col_tiles + e + 1) * TILE, :] = placed[
+                    base + a * TILE : base + (a + 1) * TILE, e * LABEL_COLUMNS : (e + 1) * LABEL_COLUMNS
+                ]
+        tile = placed_labels[base : base + TILE]
+        for a in range(1, row_tiles):
+            tile = tile + placed_labels[base + a * TILE : base + (a + 1) * TILE]
+        send_ref[chunk, row_tiles * col_tiles * TILE :, :] = tile
 
 
-def place(emb, row_owner, row_sub, loop_count, capacity, devices):
+def place(emb, row_owner, row_sub, loop_count, capacity, devices, tiled):
     rows, width = emb.shape
     slots = devices * capacity
     vmem = pl.BlockSpec(memory_space=pltpu.VMEM)
@@ -49,12 +72,16 @@
         transcendentals=0,
         bytes_accessed=rows * width * 2 + slots * (width + LABEL_COLUMNS) * 2,
     )
+    if tiled:
+        shape = (devices, capacity * width // LABEL_COLUMNS + TILE, LABEL_COLUMNS)
+    else:
+        shape = (slots, width + LABEL_COLUMNS)
     return pl.pallas_call(
         functools.partial(
-            place_kernel, loop_count=loop_count, capacity=capacity, devices=devices
+            place_kernel, loop_count=loop_count, capacity=capacity, devices=devices, tiled=tiled
         ),
         out_shape=(
-            jax.ShapeDtypeStruct((slots, width + LABEL_COLUMNS), jnp.bfloat16),
+            jax.ShapeDtypeStruct(shape, jnp.bfloat16),
             jax.ShapeDtypeStruct((1, rows), jnp.int32),
         ),
         in_specs=[vmem] * 3,
@@ -90,15 +117,25 @@
     local_blocks = rows // BLOCK
     axes = ("owner", "loop")
 
-    send, slot_of_row = place(emb, row_owner, row_sub, loop_count, capacity, devices)
+    width = emb.shape[1]
+    tiled = capacity % TILE == 0 and width % LABEL_COLUMNS == 0
+    send, slot_of_row = place(emb, row_owner, row_sub, loop_count, capacity, devices, tiled)
     slot_of_row = slot_of_row[0]
     placing = (jnp.arange(slots, dtype=jnp.int32)[:, None] == slot_of_row[None, :]).astype(
         jnp.bfloat16
     )
-    width = emb.shape[1]
     held = lax.all_to_all(send, axes, split_axis=0, concat_axis=0, tiled=True)
-    held_emb = held[:, :width]
-    held_labels = held[:, width : width + 2].astype(jnp.int32)
+    if tiled:
+        row_tiles = capacity // TILE
+        col_tiles = width // LABEL_COLUMNS
+        body_rows = row_tiles * col_tiles * TILE
+        held_emb = held[:, :body_rows].reshape(devices, row_tiles, col_tiles, TILE, LABEL_COLUMNS)
+        held_emb = held_emb.transpose(0, 1, 3, 2, 4).reshape(slots, width)
+        held_labels = held[:, body_rows:, : 2 * row_tiles].reshape(devices, TILE, row_tiles, 2)
+        held_labels = held_labels.transpose(0, 2, 1, 3).reshape(slots, 2).astype(jnp.int32)
+    else:
+        held_emb = held[:, :width]
+        held_labels = held[:, width : width + 2].astype(jnp.int32)
 
     index = jnp.arange(slots, dtype=jnp.int32)
     present = held_labels[:, 0] > 0

time: 74.4 us -> 73.3 us (0.985)
  blocking collectives: 66.4 us -> 65 us
    all_to_all x1, blocking collectives: 36.7 us -> 35.5 us  [body(): held = lax.all_to_all(send, axes, split_axis=0, concat_axis=0, tiled=True)]
where the time goes in v9:
time: 73.3 us; the launch traced here: 72.3 us
  blocking collectives  65 us (89%)
  matrix products  3.5 us (5%)
  Pallas kernels  2.74 us (4%)
    all_to_all x1, blocking collectives, body(): held = lax.all_to_all(send, axes, split_axis=0, concat_axis=0, tiled=True)  35.5 us
    all_to_all x1, blocking collectives, body(): lax.all_to_all(averaged, axes, split_axis=0, concat_axis=0, tiled=True)  29.5 us
    pallas_call x1, Pallas kernels, place(): pl.pallas_call(functools.partial(place_kernel, loop_count=loop_count, cap...  2.74 us

profile of v9, /device:TPU:1, one launch (start us, length us, event | category | flops | bytes accessed | tf_op | source)
XLA Modules:
  0.0 72.3 jit_solution(4360805992733618616)
XLA Ops:
  0.0 2.7 %shard_map.46 = (bf16[16,272,128]{2,1,0:T(8,128)(2,1)}, s32[1,256]{1,0:T(1,128)}) custom-call(bf16[256,1024]{1,0:T(8,128)(2,1)} %emb_ref.1, s32[1,256]{1,0:T(1,128)} %bitcast.33, s32[1,256]{1,0:T(1,128)} %bitcast.34), custom_call_target="tpu_custom_call" | custom-call | flops 304087040 | bytes 1703936 | tf_op jit(solution)/shard_map/pallas_call | solution.py:79
  2.7 35.5 %all_to_all.17 = bf16[16,272,128]{2,1,0:T(8,128)(2,1)S(1)} all-to-all(bf16[16,272,128]{2,1,0:T(8,128)(2,1)} %get-tuple-element.8), channel_id=1, replica_groups=mesh['groups'=2,'owner'=4,'loop'=4] {'owner','loop'}, dimensions={0} | all-to-all | bytes 2228224 | tf_op jit(solution)/shard_map/all_to_all | solution.py:127
  38.3 0.2 copy.8
  38.5 0.1 reshape.81
  38.6 0.1 slice.20
  38.7 0.3 copy.10
  39.0 0.0 copy-start.1
  39.0 0.7 %convolution_multiply_fusion = f32[512,512]{0,1:T(8,128)S(1)} fusion(bf16[64,8,8,128]{3,2,1,0:T(8,128)(2,1)S(1)} %bitcast.25), kind=kOutput, calls=%fused_computation.1 | convolution fusion | flops 537133056 | bytes 2097152 | tf_op jit(solution)/shard_map/dot_general | solution.py:96
  39.8 0.0 copy-done.1
  39.8 0.7 select_reduce_fusion
  40.5 0.3 fusion.6
  40.8 0.8 %divide_convert_fusion = bf16[512,1024]{1,0:T(8,128)(2,1)S(1)} fusion(f32[512]{0:T(512)S(1)} %fusion.6, bf16[64,8,8,128]{3,2,1,0:T(8,128)(2,1)S(1)} %bitcast.26, pred[512,512]{0,1:T(32,128)(4,1)S(1)} %get-tuple-element.13, f32[512,512]{0,1:T(8,128)S(1)} %convolution_multiply_fusion, f32[512]{0:T(512)S(1)} %get-tuple-element.12), kind=kOutput, calls=%fused_computation | convolution fusion | flops 538705920 | bytes 3411968 | tf_op jit(solution)/shard_map/dot_general | solution.py:106
  41.6 0.0 copy-start
  41.6 29.5 %all_to_all.18 = bf16[16,32,1024]{2,1,0:T(8,128)(2,1)S(1)} all-to-all(bf16[16,32,1024]{2,1,0:T(8,128)(2,1)S(1)} %bitcast.27), channel_id=1, replica_groups=mesh['groups'=2,'owner'=4,'loop'=4] {'owner','loop'}, dimensions={0} | all-to-all | bytes 2097152 | tf_op jit(solution)/shard_map/all_to_all | solution.py:161
  71.0 0.0 copy-done
  71.0 1.3 %convolution_convert_fusion = bf16[256,1024]{1,0:T(8,128)(2,1)} fusion(bf16[512,1024]{1,0:T(8,128)(2,1)S(1)} %bitcast.23, s32[256]{0:T(256)S(1)} %bitcast.32), kind=kOutput, calls=%fused_computation.2 | convolution fusion | flops 268828672 | bytes 1573888 | tf_op jit(solution)/shard_map/dot_general | solution.py:162
  (5 shorter events, 0.1 us)
Async XLA Ops:
  39.0 0.8 %copy-start.1 = (s32[32,32]{1,0:T(8,128)S(1)}, s32[32,32]{1,0:T(8,128)}, u32[]{:S(2)}) copy-start(s32[32,32]{1,0:T(8,128)} %param.7) | copy-start | bytes 12292
  41.6 29.5 %copy-start = (s32[1,256]{1,0:T(1,128)S(1)}, s32[1,256]{1,0:T(1,128)}, u32[]{:S(2)}) copy-start(s32[1,256]{1,0:T(1,128)} %get-tuple-element.7) | copy-start | bytes 3076

commit v10 on v9

--- a/solution.py
+++ b/solution.py
@@ -11,6 +11,70 @@
 SUB = 16
 LABEL_COLUMNS = 128
 TILE = 16
+PLACE_GROUPS = 4
+
+
+def place_tiled_kernel(
+    emb_hbm, owner_ref, sub_ref, send_hbm, slot_ref, emb_vmem, stage, sems, *, loop_count, capacity, devices
+):
+    rows, width = emb_vmem.shape
+    slots = devices * capacity
+    groups = stage.shape[0]
+    group_chunks = devices // groups
+    load = pltpu.make_async_copy(emb_hbm, emb_vmem, sems.at[0])
+    load.start()
+    owner = owner_ref[...]
+    sub = sub_ref[...]
+    dest = owner * loop_count + sub % loop_count
+    onehot_t = (lax.broadcasted_iota(jnp.int32, (devices, rows), 0) == dest).astype(jnp.bfloat16)
+    upper = (
+        lax.broadcasted_iota(jnp.int32, (rows, rows), 0)
+        < lax.broadcasted_iota(jnp.int32, (rows, rows), 1)
+    ).astype(jnp.bfloat16)
+    earlier_t = jnp.dot(onehot_t, upper, preferred_element_type=jnp.float32)
+    within = jnp.sum(earlier_t * onehot_t.astype(jnp.float32), axis=0, keepdims=True)
+    slot = dest * capacity + within.astype(jnp.int32)
+    slot_ref[...] = slot
+    placing = (lax.broadcasted_iota(jnp.int32, (slots, rows), 0) == slot).astype(jnp.bfloat16)
+    which = lax.broadcasted_iota(jnp.int32, (LABEL_COLUMNS, rows), 0)
+    block = lax.broadcasted_iota(jnp.int32, (LABEL_COLUMNS, rows), 1) // BLOCK
+    column = slot % capacity // TILE * 2
+    labels_t = jnp.where(which == column, block + 1, jnp.where(which == column + 1, sub + 1, 0))
+    labels = labels_t.astype(jnp.float32).T.astype(jnp.bfloat16)
+    placed_labels = jnp.dot(placing, labels, preferred_element_type=jnp.float32).astype(
+        stage.dtype
+    )
+    row_tiles = capacity // TILE
+    col_tiles = width // LABEL_COLUMNS
+    load.wait()
+    stores = []
+    for g in range(groups):
+        first = g * group_chunks * capacity
+        placed = jnp.dot(
+            placing[first : first + group_chunks * capacity],
+            emb_vmem[...],
+            preferred_element_type=jnp.float32,
+        ).astype(stage.dtype)
+        for c in range(group_chunks):
+            base = c * capacity
+            for a in range(row_tiles):
+                for e in range(col_tiles):
+                    t = a * col_tiles + e
+                    stage[g, c, t * TILE : (t + 1) * TILE, :] = placed[
+                        base + a * TILE : base + (a + 1) * TILE,
+                        e * LABEL_COLUMNS : (e + 1) * LABEL_COLUMNS,
+                    ]
+            tile = placed_labels[first + base : first + base + TILE]
+            for a in range(1, row_tiles):
+                tile = tile + placed_labels[first + base + a * TILE : first + base + (a + 1) * TILE]
+            stage[g, c, row_tiles * col_tiles * TILE :, :] = tile
+        store = pltpu.make_async_copy(
+            stage.at[g], send_hbm.at[g * group_chunks : (g + 1) * group_chunks], sems.at[1 + g]
+        )
+        store.start()
+        stores.append(store)
+    for store in stores:
+        store.wait()
 
 
 def place_kernel(
@@ -73,9 +137,26 @@
         bytes_accessed=rows * width * 2 + slots * (width + LABEL_COLUMNS) * 2,
     )
     if tiled:
-        shape = (devices, capacity * width // LABEL_COLUMNS + TILE, LABEL_COLUMNS)
-    else:
-        shape = (slots, width + LABEL_COLUMNS)
+        chunk_rows = capacity * width // LABEL_COLUMNS + TILE
+        groups = PLACE_GROUPS if devices % PLACE_GROUPS == 0 else 1
+        return pl.pallas_call(
+            functools.partial(
+                place_tiled_kernel, loop_count=loop_count, capacity=capacity, devices=devices
+            ),
+            out_shape=(
+                jax.ShapeDtypeStruct((devices, chunk_rows, LABEL_COLUMNS), jnp.bfloat16),
+                jax.ShapeDtypeStruct((1, rows), jnp.int32),
+            ),
+            in_specs=[pl.BlockSpec(memory_space=pl.ANY), vmem, vmem],
+            out_specs=(pl.BlockSpec(memory_space=pl.ANY), vmem),
+            scratch_shapes=[
+                pltpu.VMEM((rows, width), jnp.bfloat16),
+                pltpu.VMEM((groups, devices // groups, chunk_rows, LABEL_COLUMNS), jnp.bfloat16),
+                pltpu.SemaphoreType.DMA((1 + groups,)),
+            ],
+            cost_estimate=cost,
+        )(emb, row_owner[None, :], row_sub[None, :])
+    shape = (slots, width + LABEL_COLUMNS)
     return pl.pallas_call(
         functools.partial(
             place_kernel, loop_count=loop_count, capacity=capacity, devices=devices, tiled=tiled

time: 73.3 us -> 74.2 us (1.012)
  Pallas kernels: 2.74 us -> 3.64 us
    pallas_call x1, Pallas kernels: 2.74 us -> 3.64 us  [place(): pl.pallas_call(functools.partial(place_tiled_kernel, loop_count=loop_coun...]
where the time goes in v10:
time: 74.2 us; the launch traced here: 73.2 us
  blocking collectives  65 us (88%)
  Pallas kernels  3.64 us (5%)
  matrix products  3.51 us (5%)
    all_to_all x1, blocking collectives, body(): held = lax.all_to_all(send, axes, split_axis=0, concat_axis=0, tiled=True)  35.5 us
    all_to_all x1, blocking collectives, body(): lax.all_to_all(averaged, axes, split_axis=0, concat_axis=0, tiled=True)  29.5 us
    pallas_call x1, Pallas kernels, place(): pl.pallas_call(functools.partial(place_tiled_kernel, loop_count=loop_coun...  3.64 us

profile of v10, /device:TPU:1, one launch (start us, length us, event | category | flops | bytes accessed | tf_op | source)
XLA Modules:
  0.0 73.2 jit_solution(3610508308166045559)
XLA Ops:
  0.0 3.6 %shard_map.46 = (bf16[16,272,128]{2,1,0:T(8,128)(2,1)}, s32[1,256]{1,0:T(1,128)}) custom-call(bf16[256,1024]{1,0:T(8,128)(2,1)} %emb_hbm.1, s32[1,256]{1,0:T(1,128)} %bitcast.33, s32[1,256]{1,0:T(1,128)} %bitcast.34), custom_call_target="tpu_custom_call" | custom-call | flops 304087040 | bytes 1703936 | tf_op jit(solution)/shard_map/pallas_call | solution.py:142
  3.7 35.5 %all_to_all.17 = bf16[16,272,128]{2,1,0:T(8,128)(2,1)S(1)} all-to-all(bf16[16,272,128]{2,1,0:T(8,128)(2,1)} %get-tuple-element.8), channel_id=1, replica_groups=mesh['groups'=2,'owner'=4,'loop'=4] {'owner','loop'}, dimensions={0} | all-to-all | bytes 2228224 | tf_op jit(solution)/shard_map/all_to_all | solution.py:208
  39.2 0.2 copy.8
  39.4 0.1 reshape.81
  39.6 0.1 slice.20
  39.7 0.3 copy.10
  39.9 0.0 copy-start.1
  40.0 0.8 %convolution_multiply_fusion = f32[512,512]{0,1:T(8,128)S(1)} fusion(bf16[64,8,8,128]{3,2,1,0:T(8,128)(2,1)S(1)} %bitcast.25), kind=kOutput, calls=%fused_computation.1 | convolution fusion | flops 537133056 | bytes 2097152 | tf_op jit(solution)/shard_map/dot_general | solution.py:177
  40.7 0.0 copy-done.1
  40.7 0.7 select_reduce_fusion
  41.4 0.3 fusion.6
  41.7 0.8 %divide_convert_fusion = bf16[512,1024]{1,0:T(8,128)(2,1)S(1)} fusion(f32[512]{0:T(512)S(1)} %fusion.6, bf16[64,8,8,128]{3,2,1,0:T(8,128)(2,1)S(1)} %bitcast.26, pred[512,512]{0,1:T(32,128)(4,1)S(1)} %get-tuple-element.13, f32[512,512]{0,1:T(8,128)S(1)} %convolution_multiply_fusion, f32[512]{0:T(512)S(1)} %get-tuple-element.12), kind=kOutput, calls=%fused_computation | convolution fusion | flops 538705920 | bytes 3411968 | tf_op jit(solution)/shard_map/dot_general | solution.py:187
  42.5 0.0 copy-start
  42.5 29.5 %all_to_all.18 = bf16[16,32,1024]{2,1,0:T(8,128)(2,1)S(1)} all-to-all(bf16[16,32,1024]{2,1,0:T(8,128)(2,1)S(1)} %bitcast.27), channel_id=1, replica_groups=mesh['groups'=2,'owner'=4,'loop'=4] {'owner','loop'}, dimensions={0} | all-to-all | bytes 2097152 | tf_op jit(solution)/shard_map/all_to_all | solution.py:242
  72.0 0.0 copy-done
  72.0 1.3 %convolution_convert_fusion = bf16[256,1024]{1,0:T(8,128)(2,1)} fusion(bf16[512,1024]{1,0:T(8,128)(2,1)S(1)} %bitcast.23, s32[256]{0:T(256)S(1)} %bitcast.32), kind=kOutput, calls=%fused_computation.2 | convolution fusion | flops 268828672 | bytes 1573888 | tf_op jit(solution)/shard_map/dot_general | solution.py:243
  (5 shorter events, 0.1 us)
Async XLA Ops:
  39.9 0.8 %copy-start.1 = (s32[32,32]{1,0:T(8,128)S(1)}, s32[32,32]{1,0:T(8,128)}, u32[]{:S(2)}) copy-start(s32[32,32]{1,0:T(8,128)} %param.7) | copy-start | bytes 12292
  42.5 29.5 %copy-start = (s32[1,256]{1,0:T(1,128)S(1)}, s32[1,256]{1,0:T(1,128)}, u32[]{:S(2)}) copy-start(s32[1,256]{1,0:T(1,128)} %get-tuple-element.7) | copy-start | bytes 3076

commit v11 on v9

--- a/solution.py
+++ b/solution.py
@@ -20,7 +20,7 @@
     slots = devices * capacity
     owner = owner_ref[...]
     sub = sub_ref[...]
-    dest = owner * loop_count + sub % loop_count
+    dest = sub % loop_count * (devices // loop_count) + owner
     onehot_t = (lax.broadcasted_iota(jnp.int32, (devices, rows), 0) == dest).astype(jnp.bfloat16)
     upper = (
         lax.broadcasted_iota(jnp.int32, (rows, rows), 0)
@@ -115,7 +115,7 @@
     capacity = 2 * rows // owner_count // loop_count
     slots = devices * capacity
     local_blocks = rows // BLOCK
-    axes = ("owner", "loop")
+    axes = ("loop", "owner")
 
     width = emb.shape[1]
     tiled = capacity % TILE == 0 and width % LABEL_COLUMNS == 0
@@ -140,6 +140,7 @@
     index = jnp.arange(slots, dtype=jnp.int32)
     present = held_labels[:, 0] > 0
     source = index // capacity
+    source = source % owner_count * loop_count + source // owner_count
     global_block = source * local_blocks + held_labels[:, 0] - 1
     global_block = jnp.where(present, global_block, 0)
     sub = jnp.where(present, held_labels[:, 1] - 1, -1 - index)

time: 73.3 us -> 71.5 us (0.975)
  blocking collectives: 65 us -> 63.9 us
    all_to_all x1, blocking collectives: 29.5 us -> 28.4 us  [body(): lax.all_to_all(averaged, axes, split_axis=0, concat_axis=0, tiled=True)]
where the time goes in v11:
time: 71.5 us; the launch traced here: 71.2 us
  blocking collectives  63.9 us (89%)
  matrix products  3.5 us (5%)
  Pallas kernels  2.74 us (4%)
    all_to_all x1, blocking collectives, body(): held = lax.all_to_all(send, axes, split_axis=0, concat_axis=0, tiled=True)  35.5 us
    all_to_all x1, blocking collectives, body(): lax.all_to_all(averaged, axes, split_axis=0, concat_axis=0, tiled=True)  28.4 us
    pallas_call x1, Pallas kernels, place(): pl.pallas_call(functools.partial(place_kernel, loop_count=loop_count, cap...  2.74 us

profile of v11, /device:TPU:1, one launch (start us, length us, event | category | flops | bytes accessed | tf_op | source)
XLA Modules:
  0.0 71.2 jit_solution(14722464378409524099)
XLA Ops:
  0.0 2.7 %shard_map.46 = (bf16[16,272,128]{2,1,0:T(8,128)(2,1)}, s32[1,256]{1,0:T(1,128)}) custom-call(bf16[256,1024]{1,0:T(8,128)(2,1)} %emb_ref.1, s32[1,256]{1,0:T(1,128)} %bitcast.33, s32[1,256]{1,0:T(1,128)} %bitcast.34), custom_call_target="tpu_custom_call" | custom-call | flops 304087040 | bytes 1703936 | tf_op jit(solution)/shard_map/pallas_call | solution.py:79
  2.7 35.5 %all_to_all.17 = bf16[16,272,128]{2,1,0:T(8,128)(2,1)S(1)} all-to-all(bf16[16,272,128]{2,1,0:T(8,128)(2,1)} %get-tuple-element.8), channel_id=1, replica_groups=mesh['groups'=2,'owner'=4,'loop'=4] {'loop','owner'}, dimensions={0} | all-to-all | bytes 2228224 | tf_op jit(solution)/shard_map/all_to_all | solution.py:127
  38.2 0.2 copy.8
  38.4 0.1 reshape.151
  38.6 0.1 slice.20
  38.7 0.3 copy.10
  39.0 0.0 copy-start.1
  39.0 0.7 %convolution_multiply_fusion = f32[512,512]{0,1:T(8,128)S(1)} fusion(bf16[64,8,8,128]{3,2,1,0:T(8,128)(2,1)S(1)} %bitcast.25), kind=kOutput, calls=%fused_computation.1 | convolution fusion | flops 537133056 | bytes 2097152 | tf_op jit(solution)/shard_map/dot_general | solution.py:96
  39.8 0.0 copy-done.1
  39.8 0.7 select_reduce_fusion
  40.5 0.3 fusion.6
  40.7 0.8 %divide_convert_fusion = bf16[512,1024]{1,0:T(8,128)(2,1)S(1)} fusion(f32[512]{0:T(512)S(1)} %fusion.6, bf16[64,8,8,128]{3,2,1,0:T(8,128)(2,1)S(1)} %bitcast.26, pred[512,512]{0,1:T(32,128)(4,1)S(1)} %get-tuple-element.13, f32[512,512]{0,1:T(8,128)S(1)} %convolution_multiply_fusion, f32[512]{0:T(512)S(1)} %get-tuple-element.12), kind=kOutput, calls=%fused_computation | convolution fusion | flops 538705920 | bytes 3411968 | tf_op jit(solution)/shard_map/dot_general | solution.py:106
  41.5 0.0 copy-start
  41.5 28.4 %all_to_all.18 = bf16[16,32,1024]{2,1,0:T(8,128)(2,1)S(1)} all-to-all(bf16[16,32,1024]{2,1,0:T(8,128)(2,1)S(1)} %bitcast.27), channel_id=1, replica_groups=mesh['groups'=2,'owner'=4,'loop'=4] {'loop','owner'}, dimensions={0} | all-to-all | bytes 2097152 | tf_op jit(solution)/shard_map/all_to_all | solution.py:162
  69.9 0.0 copy-done
  69.9 1.3 %convolution_convert_fusion = bf16[256,1024]{1,0:T(8,128)(2,1)} fusion(bf16[512,1024]{1,0:T(8,128)(2,1)S(1)} %bitcast.23, s32[256]{0:T(256)S(1)} %bitcast.32), kind=kOutput, calls=%fused_computation.2 | convolution fusion | flops 268828672 | bytes 1573888 | tf_op jit(solution)/shard_map/dot_general | solution.py:163
  (5 shorter events, 0.1 us)
Async XLA Ops:
  39.0 0.8 %copy-start.1 = (s32[32,32]{1,0:T(8,128)S(1)}, s32[32,32]{1,0:T(8,128)}, u32[]{:S(2)}) copy-start(s32[32,32]{1,0:T(8,128)} %param.7) | copy-start | bytes 12292
  41.5 28.4 %copy-start = (s32[1,256]{1,0:T(1,128)S(1)}, s32[1,256]{1,0:T(1,128)}, u32[]{:S(2)}) copy-start(s32[1,256]{1,0:T(1,128)} %get-tuple-element.7) | copy-start | bytes 3076

commit v12 on v11

--- a/solution.py
+++ b/solution.py
@@ -31,9 +31,6 @@
     slot = dest * capacity + within.astype(jnp.int32)
     slot_ref[...] = slot
     placing = (lax.broadcasted_iota(jnp.int32, (slots, rows), 0) == slot).astype(jnp.bfloat16)
-    placed = jnp.dot(placing, emb_ref[...], preferred_element_type=jnp.float32).astype(
-        send_ref.dtype
-    )
     which = lax.broadcasted_iota(jnp.int32, (LABEL_COLUMNS, rows), 0)
     block = lax.broadcasted_iota(jnp.int32, (LABEL_COLUMNS, rows), 1) // BLOCK
     column = 0
@@ -45,18 +42,28 @@
         send_ref.dtype
     )
     if not tiled:
-        send_ref[:, :width] = placed
+        send_ref[:, :width] = jnp.dot(
+            placing, emb_ref[...], preferred_element_type=jnp.float32
+        ).astype(send_ref.dtype)
         send_ref[:, width:] = placed_labels
         return
     row_tiles = capacity // TILE
     col_tiles = width // LABEL_COLUMNS
+    for e in range(col_tiles):
+        stripe = jnp.dot(
+            placing,
+            emb_ref[:, e * LABEL_COLUMNS : (e + 1) * LABEL_COLUMNS],
+            preferred_element_type=jnp.float32,
+        ).astype(send_ref.dtype)
+        for chunk in range(devices):
+            base = chunk * capacity
+            for a in range(row_tiles):
+                t = a * col_tiles + e
+                send_ref[chunk, t * TILE : (t + 1) * TILE, :] = stripe[
+                    base + a * TILE : base + (a + 1) * TILE
+                ]
     for chunk in range(devices):
         base = chunk * capacity
-        for a in range(row_tiles):
-            for e in range(col_tiles):
-                send_ref[chunk, (a * col_tiles + e) * TILE : (a * col_tiles + e + 1) * TILE, :] = placed[
-                    base + a * TILE : base + (a + 1) * TILE, e * LABEL_COLUMNS : (e + 1) * LABEL_COLUMNS
-                ]
         tile = placed_labels[base : base + TILE]
         for a in range(1, row_tiles):
             tile = tile + placed_labels[base + a * TILE : base + (a + 1) * TILE]

time: 71.5 us -> 71.8 us (level)
  no operation moved by 1% of the time
where the time goes in v12:
time: 71.8 us; the launch traced here: 71.6 us
  blocking collectives  63.8 us (89%)
  matrix products  3.5 us (5%)
  Pallas kernels  3.13 us (4%)
    all_to_all x1, blocking collectives, body(): held = lax.all_to_all(send, axes, split_axis=0, concat_axis=0, tiled=True)  35.5 us
    all_to_all x1, blocking collectives, body(): lax.all_to_all(averaged, axes, split_axis=0, concat_axis=0, tiled=True)  28.4 us
    pallas_call x1, Pallas kernels, place(): pl.pallas_call(functools.partial(place_kernel, loop_count=loop_count, cap...  3.13 us

profile of v12, /device:TPU:1, one launch (start us, length us, event | category | flops | bytes accessed | tf_op | source)
XLA Modules:
  0.0 71.6 jit_solution(6298127827930253589)
XLA Ops:
  0.0 3.1 %shard_map.46 = (bf16[16,272,128]{2,1,0:T(8,128)(2,1)}, s32[1,256]{1,0:T(1,128)}) custom-call(bf16[256,1024]{1,0:T(8,128)(2,1)} %emb_ref.1, s32[1,256]{1,0:T(1,128)} %bitcast.33, s32[1,256]{1,0:T(1,128)} %bitcast.34), custom_call_target="tpu_custom_call" | custom-call | flops 304087040 | bytes 1703936 | tf_op jit(solution)/shard_map/pallas_call | solution.py:86
  3.1 35.5 %all_to_all.17 = bf16[16,272,128]{2,1,0:T(8,128)(2,1)S(1)} all-to-all(bf16[16,272,128]{2,1,0:T(8,128)(2,1)} %get-tuple-element.8), channel_id=1, replica_groups=mesh['groups'=2,'owner'=4,'loop'=4] {'loop','owner'}, dimensions={0} | all-to-all | bytes 2228224 | tf_op jit(solution)/shard_map/all_to_all | solution.py:134
  38.6 0.2 copy.8
  38.8 0.1 reshape.151
  39.0 0.1 slice.20
  39.1 0.3 copy.10
  39.4 0.0 copy-start.1
  39.4 0.7 %convolution_multiply_fusion = f32[512,512]{0,1:T(8,128)S(1)} fusion(bf16[64,8,8,128]{3,2,1,0:T(8,128)(2,1)S(1)} %bitcast.25), kind=kOutput, calls=%fused_computation.1 | convolution fusion | flops 537133056 | bytes 2097152 | tf_op jit(solution)/shard_map/dot_general | solution.py:103
  40.1 0.0 copy-done.1
  40.2 0.7 select_reduce_fusion
  40.9 0.3 fusion.6
  41.1 0.8 %divide_convert_fusion = bf16[512,1024]{1,0:T(8,128)(2,1)S(1)} fusion(f32[512]{0:T(512)S(1)} %fusion.6, bf16[64,8,8,128]{3,2,1,0:T(8,128)(2,1)S(1)} %bitcast.26, pred[512,512]{0,1:T(32,128)(4,1)S(1)} %get-tuple-element.13, f32[512,512]{0,1:T(8,128)S(1)} %convolution_multiply_fusion, f32[512]{0:T(512)S(1)} %get-tuple-element.12), kind=kOutput, calls=%fused_computation | convolution fusion | flops 538705920 | bytes 3411968 | tf_op jit(solution)/shard_map/dot_general | solution.py:113
  41.9 0.0 copy-start
  41.9 28.4 %all_to_all.18 = bf16[16,32,1024]{2,1,0:T(8,128)(2,1)S(1)} all-to-all(bf16[16,32,1024]{2,1,0:T(8,128)(2,1)S(1)} %bitcast.27), channel_id=1, replica_groups=mesh['groups'=2,'owner'=4,'loop'=4] {'loop','owner'}, dimensions={0} | all-to-all | bytes 2097152 | tf_op jit(solution)/shard_map/all_to_all | solution.py:169
  70.3 0.0 copy-done
  70.3 1.3 %convolution_convert_fusion = bf16[256,1024]{1,0:T(8,128)(2,1)} fusion(bf16[512,1024]{1,0:T(8,128)(2,1)S(1)} %bitcast.23, s32[256]{0:T(256)S(1)} %bitcast.32), kind=kOutput, calls=%fused_computation.2 | convolution fusion | flops 268828672 | bytes 1573888 | tf_op jit(solution)/shard_map/dot_general | solution.py:170
  (5 shorter events, 0.1 us)
Async XLA Ops:
  39.4 0.8 %copy-start.1 = (s32[32,32]{1,0:T(8,128)S(1)}, s32[32,32]{1,0:T(8,128)}, u32[]{:S(2)}) copy-start(s32[32,32]{1,0:T(8,128)} %param.7) | copy-start | bytes 12292
  41.9 28.4 %copy-start = (s32[1,256]{1,0:T(1,128)S(1)}, s32[1,256]{1,0:T(1,128)}, u32[]{:S(2)}) copy-start(s32[1,256]{1,0:T(1,128)} %get-tuple-element.7) | copy-start | bytes 3076

commit v13 on v11

--- a/solution.py
+++ b/solution.py
@@ -118,7 +118,7 @@
     axes = ("loop", "owner")
 
     width = emb.shape[1]
-    tiled = capacity % TILE == 0 and width % LABEL_COLUMNS == 0
+    tiled = False
     send, slot_of_row = place(emb, row_owner, row_sub, loop_count, capacity, devices, tiled)
     slot_of_row = slot_of_row[0]
     placing = (jnp.arange(slots, dtype=jnp.int32)[:, None] == slot_of_row[None, :]).astype(

time: 71.5 us -> 72.4 us (1.013)
  blocking collectives: 63.9 us -> 65.1 us
    all_to_all x1, blocking collectives: 35.5 us -> 36.6 us  [body(): held = lax.all_to_all(send, axes, split_axis=0, concat_axis=0, tiled=True)]
where the time goes in v13:
time: 72.4 us; the launch traced here: 72.2 us
  blocking collectives  65.1 us (90%)
  matrix products  3.47 us (5%)
  Pallas kernels  2.73 us (4%)
  other arithmetic  0.85 us (1%)
    all_to_all x1, blocking collectives, body(): held = lax.all_to_all(send, axes, split_axis=0, concat_axis=0, tiled=True)  36.6 us
    all_to_all x1, blocking collectives, body(): lax.all_to_all(averaged, axes, split_axis=0, concat_axis=0, tiled=True)  28.5 us
    pallas_call x1, Pallas kernels, place(): pl.pallas_call(functools.partial(place_kernel, loop_count=loop_count, cap...  2.73 us

profile of v13, /device:TPU:1, one launch (start us, length us, event | category | flops | bytes accessed | tf_op | source)
XLA Modules:
  0.0 72.2 jit_solution(15728996422745215213)
XLA Ops:
  0.0 2.7 %shard_map.46 = (bf16[512,1152]{1,0:T(8,128)(2,1)}, s32[1,256]{1,0:T(1,128)}) custom-call(bf16[256,1024]{1,0:T(8,128)(2,1)} %emb_ref.1, s32[1,256]{1,0:T(1,128)} %bitcast.15, s32[1,256]{1,0:T(1,128)} %bitcast.16), custom_call_target="tpu_custom_call" | custom-call | flops 304087040 | bytes 1703936 | tf_op jit(solution)/shard_map/pallas_call | solution.py:79
  2.7 36.6 %all_to_all.24 = bf16[16,32,1152]{2,1,0:T(8,128)(2,1)S(1)} all-to-all(bf16[16,32,1152]{2,1,0:T(8,128)(2,1)} %bitcast.12), channel_id=1, replica_groups=mesh['groups'=2,'owner'=4,'loop'=4] {'loop','owner'}, dimensions={0} | all-to-all | bytes 2359296 | tf_op jit(solution)/shard_map/all_to_all | solution.py:127
  39.4 0.0 copy-start.1
  39.4 0.7 %convolution_multiply_fusion = f32[512,512]{0,1:T(8,128)S(1)} fusion(bf16[512,1152]{1,0:T(8,128)(2,1)S(1)} %bitcast.10), kind=kOutput, calls=%fused_computation.1 | convolution fusion | flops 537133056 | bytes 2097152 | tf_op jit(solution)/shard_map/dot_general | solution.py:96
  40.1 0.1 fusion.33
  40.3 0.4 fusion.15
  40.7 0.0 copy-done.1
  40.7 0.7 select_reduce_fusion
  41.4 0.3 fusion.4
  41.7 0.8 %divide_convert_fusion = bf16[512,1024]{1,0:T(8,128)(2,1)S(1)} fusion(f32[512]{0:T(512)S(1)} %fusion.4, bf16[512,1152]{1,0:T(8,128)(2,1)S(1)} %bitcast.11, pred[512,512]{0,1:T(32,128)(4,1)S(1)} %get-tuple-element.15, f32[512,512]{0,1:T(8,128)S(1)} %convolution_multiply_fusion, f32[512]{0:T(512)S(1)} %get-tuple-element.14), kind=kOutput, calls=%fused_computation | convolution fusion | flops 538705920 | bytes 3411968 | tf_op jit(solution)/shard_map/dot_general | solution.py:106
  42.4 0.0 copy-start
  42.4 28.5 %all_to_all.25 = bf16[16,32,1024]{2,1,0:T(8,128)(2,1)S(1)} all-to-all(bf16[16,32,1024]{2,1,0:T(8,128)(2,1)S(1)} %bitcast.13), channel_id=1, replica_groups=mesh['groups'=2,'owner'=4,'loop'=4] {'loop','owner'}, dimensions={0} | all-to-all | bytes 2097152 | tf_op jit(solution)/shard_map/all_to_all | solution.py:162
  70.9 0.0 copy-done
  70.9 1.3 %convolution_convert_fusion = bf16[256,1024]{1,0:T(8,128)(2,1)} fusion(bf16[512,1024]{1,0:T(8,128)(2,1)S(1)} %bitcast.8, s32[256]{0:T(256)S(1)} %bitcast.14), kind=kOutput, calls=%fused_computation.2 | convolution fusion | flops 268828672 | bytes 1573888 | tf_op jit(solution)/shard_map/dot_general | solution.py:163
  (2 shorter events, 0.0 us)
Async XLA Ops:
  39.4 1.3 %copy-start.1 = (s32[32,32]{1,0:T(8,128)S(1)}, s32[32,32]{1,0:T(8,128)}, u32[]{:S(2)}) copy-start(s32[32,32]{1,0:T(8,128)} %param.7) | copy-start | bytes 12292
  42.4 28.5 %copy-start = (s32[1,256]{1,0:T(1,128)S(1)}, s32[1,256]{1,0:T(1,128)}, u32[]{:S(2)}) copy-start(s32[1,256]{1,0:T(1,128)} %get-tuple-element.7) | copy-start | bytes 3076

commit v14 on v13

--- a/solution.py
+++ b/solution.py
@@ -34,22 +34,30 @@
     placed = jnp.dot(placing, emb_ref[...], preferred_element_type=jnp.float32).astype(
         send_ref.dtype
     )
-    which = lax.broadcasted_iota(jnp.int32, (LABEL_COLUMNS, rows), 0)
-    block = lax.broadcasted_iota(jnp.int32, (LABEL_COLUMNS, rows), 1) // BLOCK
-    column = 0
-    if tiled:
-        column = slot % capacity // TILE * 2
-    labels_t = jnp.where(which == column, block + 1, jnp.where(which == column + 1, sub + 1, 0))
-    labels = labels_t.astype(jnp.float32).T.astype(jnp.bfloat16)
-    placed_labels = jnp.dot(placing, labels, preferred_element_type=jnp.float32).astype(
-        send_ref.dtype
-    )
     if not tiled:
+        which = lax.broadcasted_iota(jnp.int32, (LABEL_COLUMNS, rows), 0)
+        block = lax.broadcasted_iota(jnp.int32, (LABEL_COLUMNS, rows), 1) // BLOCK
+        labels_t = jnp.where(which == 0, block + 1, jnp.where(which == 1, sub + 1, 0))
+        labels = labels_t.astype(jnp.float32).T.astype(jnp.bfloat16)
+        placed_labels = jnp.dot(placing, labels, preferred_element_type=jnp.float32).astype(
+            send_ref.dtype
+        )
         send_ref[:, :width] = placed
         send_ref[:, width:] = placed_labels
         return
     row_tiles = capacity // TILE
     col_tiles = width // LABEL_COLUMNS
+    which = lax.broadcasted_iota(jnp.int32, (8, rows), 0)
+    block = lax.broadcasted_iota(jnp.int32, (8, rows), 1) // BLOCK
+    labels_rows = jnp.where(which == 0, block + 1, jnp.where(which == 1, sub + 1, 0))
+    placed_rows = lax.dot_general(
+        labels_rows.astype(jnp.float32).astype(jnp.bfloat16),
+        placing,
+        (((1,), (1,)), ((), ())),
+        preferred_element_type=jnp.float32,
+    ).astype(send_ref.dtype)
+    body_rows = row_tiles * col_tiles * TILE
+    per_lanes = LABEL_COLUMNS // capacity
     for chunk in range(devices):
         base = chunk * capacity
         for a in range(row_tiles):
@@ -57,10 +65,9 @@
                 send_ref[chunk, (a * col_tiles + e) * TILE : (a * col_tiles + e + 1) * TILE, :] = placed[
                     base + a * TILE : base + (a + 1) * TILE, e * LABEL_COLUMNS : (e + 1) * LABEL_COLUMNS
                 ]
-        tile = placed_labels[base : base + TILE]
-        for a in range(1, row_tiles):
-            tile = tile + placed_labels[base + a * TILE : base + (a + 1) * TILE]
-        send_ref[chunk, row_tiles * col_tiles * TILE :, :] = tile
+        lanes = chunk // per_lanes * LABEL_COLUMNS
+        send_ref[chunk, body_rows : body_rows + 8, :] = placed_rows[:, lanes : lanes + LABEL_COLUMNS]
+        send_ref[chunk, body_rows + 8 :, :] = jnp.zeros((TILE - 8, LABEL_COLUMNS), send_ref.dtype)
 
 
 def place(emb, row_owner, row_sub, loop_count, capacity, devices, tiled):
@@ -118,7 +125,7 @@
     axes = ("loop", "owner")
 
     width = emb.shape[1]
-    tiled = False
+    tiled = capacity % TILE == 0 and width % LABEL_COLUMNS == 0 and LABEL_COLUMNS % capacity == 0
     send, slot_of_row = place(emb, row_owner, row_sub, loop_count, capacity, devices, tiled)
     slot_of_row = slot_of_row[0]
     placing = (jnp.arange(slots, dtype=jnp.int32)[:, None] == slot_of_row[None, :]).astype(
@@ -131,8 +138,11 @@
         body_rows = row_tiles * col_tiles * TILE
         held_emb = held[:, :body_rows].reshape(devices, row_tiles, col_tiles, TILE, LABEL_COLUMNS)
         held_emb = held_emb.transpose(0, 1, 3, 2, 4).reshape(slots, width)
-        held_labels = held[:, body_rows:, : 2 * row_tiles].reshape(devices, TILE, row_tiles, 2)
-        held_labels = held_labels.transpose(0, 2, 1, 3).reshape(slots, 2).astype(jnp.int32)
+        per_lanes = LABEL_COLUMNS // capacity
+        lanes = held[:, body_rows : body_rows + 2, :].reshape(devices, 2, per_lanes, capacity)
+        me = lax.axis_index("loop") * owner_count + lax.axis_index("owner")
+        held_labels = lax.dynamic_index_in_dim(lanes, me % per_lanes, axis=2, keepdims=False)
+        held_labels = held_labels.astype(jnp.int32).transpose(0, 2, 1).reshape(slots, 2)
     else:
         held_emb = held[:, :width]
         held_labels = held[:, width : width + 2].astype(jnp.int32)

time: 72.4 us -> 70.8 us (0.978)
  blocking collectives: 65.1 us -> 31.8 us
  waiting for transfers between devices: 0 us -> 24.3 us
  starting transfers between devices: 0 us -> 7.31 us
    all_to_all x1 -> x0, blocking collectives: 36.6 us -> none  [body(): held = lax.all_to_all(send, axes, split_axis=0, concat_axis=0, tiled=True)]
    all_to_all x0 -> x1, waiting for transfers between devices: none -> 24.3 us  [body(): held = lax.all_to_all(send, axes, split_axis=0, concat_axis=0, tiled=True)]
    all_to_all x0 -> x1, starting transfers between devices: none -> 7.31 us  [body(): held = lax.all_to_all(send, axes, split_axis=0, concat_axis=0, tiled=True)]
    all_to_all x1, blocking collectives: 28.5 us -> 31.8 us  [body(): lax.all_to_all(averaged, axes, split_axis=0, concat_axis=0, tiled=True)]
  transfers between devices with their start and end apart: 0 -> 1, of which waited for: 0 -> 1; matrix products, arithmetic and copies ran while one was open for 0% -> 0% of each run, Pallas kernels for 0% -> 0%
where the time goes in v14:
time: 70.8 us; the launch traced here: 70.6 us
  blocking collectives  31.8 us (45%)
  waiting for transfers between devices  24.3 us (34%)
  starting transfers between devices  7.31 us (10%)
  matrix products  3.49 us (5%)
  Pallas kernels  2.63 us (4%)
    all_to_all x1, blocking collectives, body(): lax.all_to_all(averaged, axes, split_axis=0, concat_axis=0, tiled=True)  31.8 us
    all_to_all x1, waiting for transfers between devices, body(): held = lax.all_to_all(send, axes, split_axis=0, concat_axis=0, tiled=True)  24.3 us
    all_to_all x1, starting transfers between devices, body(): held = lax.all_to_all(send, axes, split_axis=0, concat_axis=0, tiled=True)  7.31 us
    pallas_call x1, Pallas kernels, place(): pl.pallas_call(functools.partial(place_kernel, loop_count=loop_count, cap...  2.63 us
  transfers between devices with their start and end apart: 1, of which 1 were waited for; matrix products, arithmetic and copies ran while one was open for 0% of the time, Pallas kernels for 0%

profile of v14, /device:TPU:1, one launch (start us, length us, event | category | flops | bytes accessed | tf_op | source)
XLA Modules:
  0.0 70.6 jit_solution(1688370818519432767)
XLA Ops:
  0.0 2.6 %shard_map.46 = (bf16[16,272,128]{2,1,0:T(8,128)(2,1)}, s32[1,256]{1,0:T(1,128)}) custom-call(bf16[256,1024]{1,0:T(8,128)(2,1)} %emb_ref.1, s32[1,256]{1,0:T(1,128)} %bitcast.36, s32[1,256]{1,0:T(1,128)} %bitcast.37), custom_call_target="tpu_custom_call" | custom-call | flops 304087040 | bytes 1703936 | tf_op jit(solution)/shard_map/pallas_call | solution.py:86
  2.6 7.3 %all-to-all-start = ((bf16[16,272,128]{2,1,0:T(8,128)(2,1)}), bf16[16,272,128]{2,1,0:T(8,128)(2,1)S(1)}, u32[]{:S(2)}, u32[]{:S(2)}) async-start(bf16[16,272,128]{2,1,0:T(8,128)(2,1)} %get-tuple-element.8), calls=%async_computation | async-start | bytes 2228224 | tf_op jit(solution)/shard_map/all_to_all | solution.py:134
  9.9 24.3 %all-to-all-done = bf16[16,272,128]{2,1,0:T(8,128)(2,1)S(1)} async-done(((bf16[16,272,128]{2,1,0:T(8,128)(2,1)}), bf16[16,272,128]{2,1,0:T(8,128)(2,1)S(1)}, u32[]{:S(2)}, u32[]{:S(2)}) %all-to-all-start) | async-done | bytes 1114144 | tf_op jit(solution)/shard_map/all_to_all | solution.py:134
  34.3 0.1 reshape.154
  34.4 0.1 reshape.160
  34.6 0.1 slice.20
  34.7 0.3 copy.6
  34.9 0.0 copy-start.1
  34.9 0.8 %convolution_multiply_fusion = f32[512,512]{0,1:T(8,128)S(1)} fusion(bf16[64,8,8,128]{3,2,1,0:T(8,128)(2,1)S(1)} %bitcast.29), kind=kOutput, calls=%fused_computation.1 | convolution fusion | flops 537133056 | bytes 2097152 | tf_op jit(solution)/shard_map/dot_general | solution.py:103
  35.7 0.0 copy-done.1
  35.7 0.7 select_reduce_fusion
  36.4 0.3 fusion.6
  36.7 0.8 %divide_convert_fusion = bf16[512,1024]{1,0:T(8,128)(2,1)S(1)} fusion(f32[512]{0:T(512)S(1)} %fusion.6, bf16[64,8,8,128]{3,2,1,0:T(8,128)(2,1)S(1)} %bitcast.30, pred[512,512]{0,1:T(32,128)(4,1)S(1)} %get-tuple-element.13, f32[512,512]{0,1:T(8,128)S(1)} %convolution_multiply_fusion, f32[512]{0:T(512)S(1)} %get-tuple-element.12), kind=kOutput, calls=%fused_computation | convolution fusion | flops 538705920 | bytes 3411968 | tf_op jit(solution)/shard_map/dot_general | solution.py:113
  37.5 0.0 copy-start
  37.5 31.8 %all_to_all.17 = bf16[16,32,1024]{2,1,0:T(8,128)(2,1)S(1)} all-to-all(bf16[16,32,1024]{2,1,0:T(8,128)(2,1)S(1)} %bitcast.31), channel_id=1, replica_groups=mesh['groups'=2,'owner'=4,'loop'=4] {'loop','owner'}, dimensions={0} | all-to-all | bytes 2097152 | tf_op jit(solution)/shard_map/all_to_all | solution.py:172
  69.3 0.0 copy-done
  69.3 1.3 %convolution_convert_fusion = bf16[256,1024]{1,0:T(8,128)(2,1)} fusion(bf16[512,1024]{1,0:T(8,128)(2,1)S(1)} %bitcast.27, s32[256]{0:T(256)S(1)} %bitcast.35), kind=kOutput, calls=%fused_computation.2 | convolution fusion | flops 268828672 | bytes 1573888 | tf_op jit(solution)/shard_map/dot_general | solution.py:173
  (6 shorter events, 0.1 us)
Async XLA Ops:
  2.6 31.6 %all-to-all-start = ((bf16[16,272,128]{2,1,0:T(8,128)(2,1)}), bf16[16,272,128]{2,1,0:T(8,128)(2,1)S(1)}, u32[]{:S(2)}, u32[]{:S(2)}) async-start(bf16[16,272,128]{2,1,0:T(8,128)(2,1)} %get-tuple-element.8), calls=%async_computation | async-start | bytes 2228224 | tf_op jit(solution)/shard_map/all_to_all | solution.py:134
  34.9 0.8 %copy-start.1 = (s32[32,32]{1,0:T(8,128)S(1)}, s32[32,32]{1,0:T(8,128)}, u32[]{:S(2)}) copy-start(s32[32,32]{1,0:T(8,128)} %param.7) | copy-start | bytes 12292
  37.5 31.8 %copy-start = (s32[1,256]{1,0:T(1,128)S(1)}, s32[1,256]{1,0:T(1,128)}, u32[]{:S(2)}) copy-start(s32[1,256]{1,0:T(1,128)} %get-tuple-element.7) | copy-start | bytes 3076

commit v15 on v14

--- a/solution.py
+++ b/solution.py
@@ -131,6 +131,7 @@
     placing = (jnp.arange(slots, dtype=jnp.int32)[:, None] == slot_of_row[None, :]).astype(
         jnp.bfloat16
     )
+    placing = lax.optimization_barrier(placing)
     held = lax.all_to_all(send, axes, split_axis=0, concat_axis=0, tiled=True)
     if tiled:
         row_tiles = capacity // TILE

time: 70.8 us -> 71.1 us (level); the launches traced: 70.6 us -> 69.8 us
  blocking collectives: 31.8 us -> 0 us
  waiting for transfers between devices: 24.3 us -> 47.4 us
  starting transfers between devices: 7.31 us -> 14.2 us
  matrix products: 3.49 us -> 4.46 us
    all_to_all x1 -> x0, blocking collectives: 31.8 us -> none  [body(): lax.all_to_all(averaged, axes, split_axis=0, concat_axis=0, tiled=True)]
    all_to_all x0 -> x1, waiting for transfers between devices: none -> 23.1 us  [body(): lax.all_to_all(averaged, axes, split_axis=0, concat_axis=0, tiled=True)]
    all_to_all x0 -> x1, starting transfers between devices: none -> 6.89 us  [body(): lax.all_to_all(averaged, axes, split_axis=0, concat_axis=0, tiled=True)]
    dot_general x1, matrix products: 0.78 us -> 1.77 us  [attend(): jnp.dot(weights.astype(jnp.bfloat16), keys, preferred_element_type=jnp.fl...]
  transfers between devices with their start and end apart: 1 -> 2, of which waited for: 1 -> 2; matrix products, arithmetic and copies ran while one was open for 0% -> 0% of each run, Pallas kernels for 0% -> 0%
where the time goes in v15:
time: 71.1 us; the launch traced here: 69.8 us
  waiting for transfers between devices  47.4 us (67%)
  starting transfers between devices  14.2 us (20%)
  matrix products  4.46 us (6%)
  Pallas kernels  2.63 us (4%)
    all_to_all x1, waiting for transfers between devices, body(): held = lax.all_to_all(send, axes, split_axis=0, concat_axis=0, tiled=True)  24.3 us
    all_to_all x1, waiting for transfers between devices, body(): lax.all_to_all(averaged, axes, split_axis=0, concat_axis=0, tiled=True)  23.1 us
    all_to_all x1, starting transfers between devices, body(): held = lax.all_to_all(send, axes, split_axis=0, concat_axis=0, tiled=True)  7.31 us
    all_to_all x1, starting transfers between devices, body(): lax.all_to_all(averaged, axes, split_axis=0, concat_axis=0, tiled=True)  6.89 us
    pallas_call x1, Pallas kernels, place(): pl.pallas_call(functools.partial(place_kernel, loop_count=loop_count, cap...  2.63 us
    dot_general x1, matrix products, attend(): jnp.dot(weights.astype(jnp.bfloat16), keys, preferred_element_type=jnp.fl...  1.77 us
  transfers between devices with their start and end apart: 2, of which 2 were waited for; matrix products, arithmetic and copies ran while one was open for 0% of the time, Pallas kernels for 0%

profile of v15, /device:TPU:1, one launch (start us, length us, event | category | flops | bytes accessed | tf_op | source)
XLA Modules:
  0.0 69.8 jit_solution(7606784960019325298)
XLA Ops:
  0.0 2.6 %shard_map.46 = (bf16[16,272,128]{2,1,0:T(8,128)(2,1)}, s32[1,256]{1,0:T(1,128)}) custom-call(bf16[256,1024]{1,0:T(8,128)(2,1)} %emb_ref.1, s32[1,256]{1,0:T(1,128)} %bitcast.36, s32[1,256]{1,0:T(1,128)} %bitcast.37), custom_call_target="tpu_custom_call" | custom-call | flops 304087040 | bytes 1703936 | tf_op jit(solution)/shard_map/pallas_call | solution.py:86
  2.6 7.3 %all-to-all-start = ((bf16[16,272,128]{2,1,0:T(8,128)(2,1)}), bf16[16,272,128]{2,1,0:T(8,128)(2,1)S(1)}, u32[]{:S(2)}, u32[]{:S(2)}) async-start(bf16[16,272,128]{2,1,0:T(8,128)(2,1)} %get-tuple-element.8), calls=%async_computation | async-start | bytes 2228224 | tf_op jit(solution)/shard_map/all_to_all | solution.py:135
  9.9 24.3 %all-to-all-done = bf16[16,272,128]{2,1,0:T(8,128)(2,1)S(1)} async-done(((bf16[16,272,128]{2,1,0:T(8,128)(2,1)}), bf16[16,272,128]{2,1,0:T(8,128)(2,1)S(1)}, u32[]{:S(2)}, u32[]{:S(2)}) %all-to-all-start) | async-done | bytes 1114144 | tf_op jit(solution)/shard_map/all_to_all | solution.py:135
  34.3 0.1 reshape.154
  34.4 0.1 reshape.160
  34.6 0.1 slice.20
  34.7 0.3 copy.6
  34.9 0.0 copy-start.1
  34.9 0.7 %convolution_multiply_fusion = f32[512,512]{0,1:T(8,128)S(1)} fusion(bf16[64,8,8,128]{3,2,1,0:T(8,128)(2,1)S(1)} %bitcast.30), kind=kOutput, calls=%fused_computation.1 | convolution fusion | flops 537133056 | bytes 2097152 | tf_op jit(solution)/shard_map/dot_general | solution.py:103
  35.7 0.0 copy-done.1
  35.7 0.7 select_reduce_fusion
  36.4 0.3 fusion.6
  36.7 1.8 %divide_convert_fusion = bf16[512,1024]{1,0:T(8,128)(2,1)} fusion(f32[512]{0:T(512)S(1)} %fusion.6, bf16[64,8,8,128]{3,2,1,0:T(8,128)(2,1)S(1)} %bitcast.31, pred[512,512]{0,1:T(32,128)(4,1)S(1)} %get-tuple-element.13, f32[512,512]{0,1:T(8,128)S(1)} %convolution_multiply_fusion, f32[512]{0:T(512)S(1)} %get-tuple-element.12), kind=kOutput, calls=%fused_computation | convolution fusion | flops 538705920 | bytes 3411968 | tf_op jit(solution)/shard_map/dot_general | solution.py:113
  38.4 0.0 copy-start
  38.4 6.9 %all-to-all-start.1 = ((bf16[16,32,1024]{2,1,0:T(8,128)(2,1)}), bf16[16,32,1024]{2,1,0:T(8,128)(2,1)S(1)}, u32[]{:S(2)}, u32[]{:S(2)}) async-start(bf16[16,32,1024]{2,1,0:T(8,128)(2,1)} %bitcast.10), calls=%async_computation.1 | async-start | bytes 2097152 | tf_op jit(solution)/shard_map/all_to_all | solution.py:173
  45.3 0.0 copy-done
  45.3 0.1 fusion.11
  45.4 23.1 %all-to-all-done.1 = bf16[16,32,1024]{2,1,0:T(8,128)(2,1)S(1)} async-done(((bf16[16,32,1024]{2,1,0:T(8,128)(2,1)}), bf16[16,32,1024]{2,1,0:T(8,128)(2,1)S(1)}, u32[]{:S(2)}, u32[]{:S(2)}) %all-to-all-start.1) | async-done | bytes 1048608 | tf_op jit(solution)/shard_map/all_to_all | solution.py:173
  68.5 1.3 %convolution_convert_fusion = bf16[256,1024]{1,0:T(8,128)(2,1)} fusion(bf16[512,256]{1,0:T(8,128)(2,1)S(1)} %fusion.11, bf16[512,1024]{1,0:T(8,128)(2,1)S(1)} %bitcast.28), kind=kOutput, calls=%fused_computation.2 | convolution fusion | flops 268697600 | bytes 1835008 | tf_op jit(solution)/shard_map/dot_general | solution.py:174
  (6 shorter events, 0.1 us)
Async XLA Ops:
  2.6 31.6 %all-to-all-start = ((bf16[16,272,128]{2,1,0:T(8,128)(2,1)}), bf16[16,272,128]{2,1,0:T(8,128)(2,1)S(1)}, u32[]{:S(2)}, u32[]{:S(2)}) async-start(bf16[16,272,128]{2,1,0:T(8,128)(2,1)} %get-tuple-element.8), calls=%async_computation | async-start | bytes 2228224 | tf_op jit(solution)/shard_map/all_to_all | solution.py:135
  34.9 0.8 %copy-start.1 = (s32[32,32]{1,0:T(8,128)S(1)}, s32[32,32]{1,0:T(8,128)}, u32[]{:S(2)}) copy-start(s32[32,32]{1,0:T(8,128)} %param.7) | copy-start | bytes 12292
  38.4 6.9 %copy-start = (s32[1,256]{1,0:T(1,128)S(1)}, s32[1,256]{1,0:T(1,128)}, u32[]{:S(2)}) copy-start(s32[1,256]{1,0:T(1,128)} %get-tuple-element.7) | copy-start | bytes 3076
  38.4 30.1 %all-to-all-start.1 = ((bf16[16,32,1024]{2,1,0:T(8,128)(2,1)}), bf16[16,32,1024]{2,1,0:T(8,128)(2,1)S(1)}, u32[]{:S(2)}, u32[]{:S(2)}) async-start(bf16[16,32,1024]{2,1,0:T(8,128)(2,1)} %bitcast.10), calls=%async_computation.1 | async-start | bytes 2097152 | tf_op jit(solution)/shard_map/all_to_all | solution.py:173

commit v16 on v14

--- a/solution.py
+++ b/solution.py
@@ -128,7 +128,7 @@
     tiled = capacity % TILE == 0 and width % LABEL_COLUMNS == 0 and LABEL_COLUMNS % capacity == 0
     send, slot_of_row = place(emb, row_owner, row_sub, loop_count, capacity, devices, tiled)
     slot_of_row = slot_of_row[0]
-    placing = (jnp.arange(slots, dtype=jnp.int32)[:, None] == slot_of_row[None, :]).astype(
+    gathering = (slot_of_row[:, None] == jnp.arange(slots, dtype=jnp.int32)[None, :]).astype(
         jnp.bfloat16
     )
     held = lax.all_to_all(send, axes, split_axis=0, concat_axis=0, tiled=True)
@@ -170,9 +170,7 @@
     )
     averaged = attend(held_emb, near, sub)
     returned = lax.all_to_all(averaged, axes, split_axis=0, concat_axis=0, tiled=True)
-    result = lax.dot_general(
-        placing, returned, (((0,), (0,)), ((), ())), preferred_element_type=jnp.float32
-    )
+    result = jnp.dot(gathering, returned, preferred_element_type=jnp.float32)
     return result.astype(jnp.bfloat16)
 
 

time: 70.8 us -> 70.8 us (level)
  no operation moved by 1% of the time
where the time goes in v16:
time: 70.8 us; the launch traced here: 70.6 us
  blocking collectives  31.8 us (45%)
  waiting for transfers between devices  24.3 us (34%)
  starting transfers between devices  7.31 us (10%)
  matrix products  3.49 us (5%)
  Pallas kernels  2.63 us (4%)
    all_to_all x1, blocking collectives, body(): lax.all_to_all(averaged, axes, split_axis=0, concat_axis=0, tiled=True)  31.8 us
    all_to_all x1, waiting for transfers between devices, body(): held = lax.all_to_all(send, axes, split_axis=0, concat_axis=0, tiled=True)  24.3 us
    all_to_all x1, starting transfers between devices, body(): held = lax.all_to_all(send, axes, split_axis=0, concat_axis=0, tiled=True)  7.31 us
    pallas_call x1, Pallas kernels, place(): pl.pallas_call(functools.partial(place_kernel, loop_count=loop_count, cap...  2.63 us
  transfers between devices with their start and end apart: 1, of which 1 were waited for; matrix products, arithmetic and copies ran while one was open for 0% of the time, Pallas kernels for 0%

profile of v16, /device:TPU:1, one launch (start us, length us, event | category | flops | bytes accessed | tf_op | source)
XLA Modules:
  0.0 70.6 jit_solution(4181531842242659215)
XLA Ops:
  0.0 2.6 %shard_map.46 = (bf16[16,272,128]{2,1,0:T(8,128)(2,1)}, s32[1,256]{1,0:T(1,128)}) custom-call(bf16[256,1024]{1,0:T(8,128)(2,1)} %emb_ref.1, s32[1,256]{1,0:T(1,128)} %bitcast.36, s32[1,256]{1,0:T(1,128)} %bitcast.37), custom_call_target="tpu_custom_call" | custom-call | flops 304087040 | bytes 1703936 | tf_op jit(solution)/shard_map/pallas_call | solution.py:86
  2.6 7.3 %all-to-all-start = ((bf16[16,272,128]{2,1,0:T(8,128)(2,1)}), bf16[16,272,128]{2,1,0:T(8,128)(2,1)S(1)}, u32[]{:S(2)}, u32[]{:S(2)}) async-start(bf16[16,272,128]{2,1,0:T(8,128)(2,1)} %get-tuple-element.8), calls=%async_computation | async-start | bytes 2228224 | tf_op jit(solution)/shard_map/all_to_all | solution.py:134
  9.9 24.3 %all-to-all-done = bf16[16,272,128]{2,1,0:T(8,128)(2,1)S(1)} async-done(((bf16[16,272,128]{2,1,0:T(8,128)(2,1)}), bf16[16,272,128]{2,1,0:T(8,128)(2,1)S(1)}, u32[]{:S(2)}, u32[]{:S(2)}) %all-to-all-start) | async-done | bytes 1114144 | tf_op jit(solution)/shard_map/all_to_all | solution.py:134
  34.3 0.1 reshape.155
  34.4 0.1 reshape.161
  34.6 0.1 slice.20
  34.7 0.3 copy.6
  34.9 0.0 copy-start.1
  34.9 0.8 %convolution_multiply_fusion = f32[512,512]{0,1:T(8,128)S(1)} fusion(bf16[64,8,8,128]{3,2,1,0:T(8,128)(2,1)S(1)} %bitcast.29), kind=kOutput, calls=%fused_computation.1 | convolution fusion | flops 537133056 | bytes 2097152 | tf_op jit(solution)/shard_map/dot_general | solution.py:103
  35.7 0.0 copy-done.1
  35.7 0.7 select_reduce_fusion
  36.4 0.3 fusion.6
  36.7 0.8 %divide_convert_fusion = bf16[512,1024]{1,0:T(8,128)(2,1)S(1)} fusion(f32[512]{0:T(512)S(1)} %fusion.6, bf16[64,8,8,128]{3,2,1,0:T(8,128)(2,1)S(1)} %bitcast.30, pred[512,512]{0,1:T(32,128)(4,1)S(1)} %get-tuple-element.13, f32[512,512]{0,1:T(8,128)S(1)} %convolution_multiply_fusion, f32[512]{0:T(512)S(1)} %get-tuple-element.12), kind=kOutput, calls=%fused_computation | convolution fusion | flops 538705920 | bytes 3411968 | tf_op jit(solution)/shard_map/dot_general | solution.py:113
  37.5 0.0 copy-start
  37.5 31.8 %all_to_all.17 = bf16[16,32,1024]{2,1,0:T(8,128)(2,1)S(1)} all-to-all(bf16[16,32,1024]{2,1,0:T(8,128)(2,1)S(1)} %bitcast.31), channel_id=1, replica_groups=mesh['groups'=2,'owner'=4,'loop'=4] {'loop','owner'}, dimensions={0} | all-to-all | bytes 2097152 | tf_op jit(solution)/shard_map/all_to_all | solution.py:172
  69.3 0.0 copy-done
  69.3 1.3 %convolution_convert_fusion = bf16[256,1024]{1,0:T(8,128)(2,1)} fusion(bf16[512,1024]{1,0:T(8,128)(2,1)S(1)} %bitcast.27, s32[256]{0:T(256)S(1)} %bitcast.35), kind=kOutput, calls=%fused_computation.2 | convolution fusion | flops 268828672 | bytes 1573888 | tf_op jit(solution)/shard_map/dot_general | solution.py:173
  (6 shorter events, 0.1 us)
Async XLA Ops:
  2.6 31.6 %all-to-all-start = ((bf16[16,272,128]{2,1,0:T(8,128)(2,1)}), bf16[16,272,128]{2,1,0:T(8,128)(2,1)S(1)}, u32[]{:S(2)}, u32[]{:S(2)}) async-start(bf16[16,272,128]{2,1,0:T(8,128)(2,1)} %get-tuple-element.8), calls=%async_computation | async-start | bytes 2228224 | tf_op jit(solution)/shard_map/all_to_all | solution.py:134
  34.9 0.8 %copy-start.1 = (s32[32,32]{1,0:T(8,128)S(1)}, s32[32,32]{1,0:T(8,128)}, u32[]{:S(2)}) copy-start(s32[32,32]{1,0:T(8,128)} %param.7) | copy-start | bytes 12292
  37.5 31.8 %copy-start = (s32[1,256]{1,0:T(1,128)S(1)}, s32[1,256]{1,0:T(1,128)}, u32[]{:S(2)}) copy-start(s32[1,256]{1,0:T(1,128)} %get-tuple-element.7) | copy-start | bytes 3076

commit v17 on v16

--- a/solution.py
+++ b/solution.py
@@ -111,7 +111,7 @@
     weights = jnp.where(same, jnp.exp(scores - top[:, None]), jnp.float32(0.0))
     total = jnp.sum(weights, axis=1)
     summed = jnp.dot(weights.astype(jnp.bfloat16), keys, preferred_element_type=jnp.float32)
-    return (summed / total[:, None]).astype(jnp.bfloat16)
+    return (summed * (1.0 / total)[:, None]).astype(jnp.bfloat16)
 
 
 def body(emb, row_owner, row_sub, cand):

time: 70.8 us -> 70.8 us (level)
  no operation moved by 1% of the time
where the time goes in v17:
time: 70.8 us; the launch traced here: 70.6 us
  blocking collectives  31.8 us (45%)
  waiting for transfers between devices  24.3 us (34%)
  starting transfers between devices  7.31 us (10%)
  matrix products  3.5 us (5%)
  Pallas kernels  2.63 us (4%)
    all_to_all x1, blocking collectives, body(): lax.all_to_all(averaged, axes, split_axis=0, concat_axis=0, tiled=True)  31.8 us
    all_to_all x1, waiting for transfers between devices, body(): held = lax.all_to_all(send, axes, split_axis=0, concat_axis=0, tiled=True)  24.3 us
    all_to_all x1, starting transfers between devices, body(): held = lax.all_to_all(send, axes, split_axis=0, concat_axis=0, tiled=True)  7.31 us
    pallas_call x1, Pallas kernels, place(): pl.pallas_call(functools.partial(place_kernel, loop_count=loop_count, cap...  2.63 us
  transfers between devices with their start and end apart: 1, of which 1 were waited for; matrix products, arithmetic and copies ran while one was open for 0% of the time, Pallas kernels for 0%

profile of v17, /device:TPU:1, one launch (start us, length us, event | category | flops | bytes accessed | tf_op | source)
XLA Modules:
  0.0 70.6 jit_solution(12743647035181679962)
XLA Ops:
  0.0 2.6 %shard_map.46 = (bf16[16,272,128]{2,1,0:T(8,128)(2,1)}, s32[1,256]{1,0:T(1,128)}) custom-call(bf16[256,1024]{1,0:T(8,128)(2,1)} %emb_ref.1, s32[1,256]{1,0:T(1,128)} %bitcast.36, s32[1,256]{1,0:T(1,128)} %bitcast.37), custom_call_target="tpu_custom_call" | custom-call | flops 304087040 | bytes 1703936 | tf_op jit(solution)/shard_map/pallas_call | solution.py:86
  2.6 7.3 %all-to-all-start = ((bf16[16,272,128]{2,1,0:T(8,128)(2,1)}), bf16[16,272,128]{2,1,0:T(8,128)(2,1)S(1)}, u32[]{:S(2)}, u32[]{:S(2)}) async-start(bf16[16,272,128]{2,1,0:T(8,128)(2,1)} %get-tuple-element.8), calls=%async_computation | async-start | bytes 2228224 | tf_op jit(solution)/shard_map/all_to_all | solution.py:134
  9.9 24.3 %all-to-all-done = bf16[16,272,128]{2,1,0:T(8,128)(2,1)S(1)} async-done(((bf16[16,272,128]{2,1,0:T(8,128)(2,1)}), bf16[16,272,128]{2,1,0:T(8,128)(2,1)S(1)}, u32[]{:S(2)}, u32[]{:S(2)}) %all-to-all-start) | async-done | bytes 1114144 | tf_op jit(solution)/shard_map/all_to_all | solution.py:134
  34.3 0.1 reshape.157
  34.4 0.1 reshape.163
  34.6 0.1 slice.20
  34.7 0.3 copy.6
  34.9 0.0 copy-start.1
  34.9 0.8 %convolution_multiply_fusion = f32[512,512]{0,1:T(8,128)S(1)} fusion(bf16[64,8,8,128]{3,2,1,0:T(8,128)(2,1)S(1)} %bitcast.29), kind=kOutput, calls=%fused_computation.1 | convolution fusion | flops 537133056 | bytes 2097152 | tf_op jit(solution)/shard_map/dot_general | solution.py:103
  35.7 0.0 copy-done.1
  35.7 0.7 select_reduce_fusion
  36.4 0.3 fusion.6
  36.7 0.8 %multiply_convert_fusion = bf16[512,1024]{1,0:T(8,128)(2,1)S(1)} fusion(f32[512]{0:T(512)S(1)} %broadcast_divide_fusion, bf16[64,8,8,128]{3,2,1,0:T(8,128)(2,1)S(1)} %bitcast.30, pred[512,512]{0,1:T(32,128)(4,1)S(1)} %get-tuple-element.13, f32[512,512]{0,1:T(8,128)S(1)} %convolution_multiply_fusion, f32[512]{0:T(512)S(1)} %get-tuple-element.12), kind=kOutput, calls=%fused_computation | convolution fusion | flops 538705920 | bytes 3411968 | tf_op jit(solution)/shard_map/dot_general | solution.py:113
  37.5 0.0 copy-start
  37.5 31.8 %all_to_all.17 = bf16[16,32,1024]{2,1,0:T(8,128)(2,1)S(1)} all-to-all(bf16[16,32,1024]{2,1,0:T(8,128)(2,1)S(1)} %bitcast.31), channel_id=1, replica_groups=mesh['groups'=2,'owner'=4,'loop'=4] {'loop','owner'}, dimensions={0} | all-to-all | bytes 2097152 | tf_op jit(solution)/shard_map/all_to_all | solution.py:172
  69.3 0.0 copy-done
  69.3 1.3 %convolution_convert_fusion = bf16[256,1024]{1,0:T(8,128)(2,1)} fusion(bf16[512,1024]{1,0:T(8,128)(2,1)S(1)} %bitcast.27, s32[256]{0:T(256)S(1)} %bitcast.35), kind=kOutput, calls=%fused_computation.2 | convolution fusion | flops 268828672 | bytes 1573888 | tf_op jit(solution)/shard_map/dot_general | solution.py:173
  (7 shorter events, 0.1 us)
Async XLA Ops:
  2.6 31.6 %all-to-all-start = ((bf16[16,272,128]{2,1,0:T(8,128)(2,1)}), bf16[16,272,128]{2,1,0:T(8,128)(2,1)S(1)}, u32[]{:S(2)}, u32[]{:S(2)}) async-start(bf16[16,272,128]{2,1,0:T(8,128)(2,1)} %get-tuple-element.8), calls=%async_computation | async-start | bytes 2228224 | tf_op jit(solution)/shard_map/all_to_all | solution.py:134
  34.9 0.8 %copy-start.1 = (s32[32,32]{1,0:T(8,128)S(1)}, s32[32,32]{1,0:T(8,128)}, u32[]{:S(2)}) copy-start(s32[32,32]{1,0:T(8,128)} %param.7) | copy-start | bytes 12292
  37.5 31.8 %copy-start = (s32[1,256]{1,0:T(1,128)S(1)}, s32[1,256]{1,0:T(1,128)}, u32[]{:S(2)}) copy-start(s32[1,256]{1,0:T(1,128)} %get-tuple-element.7) | copy-start | bytes 3076

commit v18 on v16

--- a/solution.py
+++ b/solution.py
@@ -128,7 +128,8 @@
     tiled = capacity % TILE == 0 and width % LABEL_COLUMNS == 0 and LABEL_COLUMNS % capacity == 0
     send, slot_of_row = place(emb, row_owner, row_sub, loop_count, capacity, devices, tiled)
     slot_of_row = slot_of_row[0]
-    gathering = (slot_of_row[:, None] == jnp.arange(slots, dtype=jnp.int32)[None, :]).astype(
+    pair_slot = slot_of_row[::2] // 2
+    gathering = (pair_slot[:, None] == jnp.arange(slots // 2, dtype=jnp.int32)[None, :]).astype(
         jnp.bfloat16
     )
     held = lax.all_to_all(send, axes, split_axis=0, concat_axis=0, tiled=True)
@@ -170,7 +171,9 @@
     )
     averaged = attend(held_emb, near, sub)
     returned = lax.all_to_all(averaged, axes, split_axis=0, concat_axis=0, tiled=True)
-    result = jnp.dot(gathering, returned, preferred_element_type=jnp.float32)
+    result = jnp.dot(
+        gathering, returned.reshape(slots // 2, 2 * width), preferred_element_type=jnp.float32
+    ).reshape(rows, width)
     return result.astype(jnp.bfloat16)
 
 

time: 70.8 us -> 71.5 us (level); the launches traced: 70.6 us -> 70.2 us
  blocking collectives: 31.8 us -> 0 us
  waiting for transfers between devices: 24.3 us -> 47.3 us
  starting transfers between devices: 7.31 us -> 14.2 us
  local copies, waits for them, and re-layouts: 0.58 us -> 2.14 us
    all_to_all x1 -> x0, blocking collectives: 31.8 us -> none  [body(): lax.all_to_all(averaged, axes, split_axis=0, concat_axis=0, tiled=True)]
    all_to_all x0 -> x1, waiting for transfers between devices: none -> 22.9 us  [body(): lax.all_to_all(averaged, axes, split_axis=0, concat_axis=0, tiled=True)]
    all_to_all x0 -> x1, starting transfers between devices: none -> 6.89 us  [body(): lax.all_to_all(averaged, axes, split_axis=0, concat_axis=0, tiled=True)]
    dot_general x1, matrix products: 0.78 us -> 1.77 us  [attend(): jnp.dot(weights.astype(jnp.bfloat16), keys, preferred_element_type=jnp.fl...]
    convert_element_type x0 -> x1, local copies, waits for them, and re-layouts: none -> 0.97 us  [body(): return result.astype(jnp.bfloat16)]
    dot_general x1, matrix products: 1.28 us -> 0.35 us  [body(): jnp.dot(gathering, returned.reshape(slots // 2, 2 * width), preferred_ele...]
  transfers between devices with their start and end apart: 1 -> 2, of which waited for: 1 -> 2; matrix products, arithmetic and copies ran while one was open for 0% -> 0% of each run, Pallas kernels for 0% -> 0%
where the time goes in v18:
time: 71.5 us; the launch traced here: 70.2 us
  waiting for transfers between devices  47.3 us (66%)
  starting transfers between devices  14.2 us (20%)
  matrix products  3.54 us (5%)
  Pallas kernels  2.63 us (4%)
  local copies, waits for them, and re-layouts  2.14 us (3%)
    all_to_all x1, waiting for transfers between devices, body(): held = lax.all_to_all(send, axes, split_axis=0, concat_axis=0, tiled=True)  24.3 us
    all_to_all x1, waiting for transfers between devices, body(): lax.all_to_all(averaged, axes, split_axis=0, concat_axis=0, tiled=True)  22.9 us
    all_to_all x1, starting transfers between devices, body(): held = lax.all_to_all(send, axes, split_axis=0, concat_axis=0, tiled=True)  7.31 us
    all_to_all x1, starting transfers between devices, body(): lax.all_to_all(averaged, axes, split_axis=0, concat_axis=0, tiled=True)  6.89 us
    pallas_call x1, Pallas kernels, place(): pl.pallas_call(functools.partial(place_kernel, loop_count=loop_count, cap...  2.63 us
    dot_general x1, matrix products, attend(): jnp.dot(weights.astype(jnp.bfloat16), keys, preferred_element_type=jnp.fl...  1.77 us
  transfers between devices with their start and end apart: 2, of which 2 were waited for; matrix products, arithmetic and copies ran while one was open for 0% of the time, Pallas kernels for 0%

profile of v18, /device:TPU:1, one launch (start us, length us, event | category | flops | bytes accessed | tf_op | source)
XLA Modules:
  0.0 70.2 jit_solution(4290263345175349475)
XLA Ops:
  0.0 2.6 %shard_map.46 = (bf16[16,272,128]{2,1,0:T(8,128)(2,1)}, s32[1,256]{1,0:T(1,128)}) custom-call(bf16[256,1024]{1,0:T(8,128)(2,1)} %emb_ref.1, s32[1,256]{1,0:T(1,128)} %bitcast.32, s32[1,256]{1,0:T(1,128)} %bitcast.33), custom_call_target="tpu_custom_call" | custom-call | flops 304087040 | bytes 1703936 | tf_op jit(solution)/shard_map/pallas_call | solution.py:86
  2.6 7.3 %all-to-all-start = ((bf16[16,272,128]{2,1,0:T(8,128)(2,1)}), bf16[16,272,128]{2,1,0:T(8,128)(2,1)S(1)}, u32[]{:S(2)}, u32[]{:S(2)}) async-start(bf16[16,272,128]{2,1,0:T(8,128)(2,1)} %get-tuple-element.8), calls=%async_computation | async-start | bytes 2228224 | tf_op jit(solution)/shard_map/all_to_all | solution.py:135
  9.9 24.3 %all-to-all-done = bf16[16,272,128]{2,1,0:T(8,128)(2,1)S(1)} async-done(((bf16[16,272,128]{2,1,0:T(8,128)(2,1)}), bf16[16,272,128]{2,1,0:T(8,128)(2,1)S(1)}, u32[]{:S(2)}, u32[]{:S(2)}) %all-to-all-start) | async-done | bytes 1114144 | tf_op jit(solution)/shard_map/all_to_all | solution.py:135
  34.3 0.1 reshape.161
  34.4 0.1 reshape.168
  34.6 0.1 slice.24
  34.7 0.3 copy.6
  34.9 0.0 copy-start
  34.9 0.7 %convolution_multiply_fusion = f32[512,512]{0,1:T(8,128)S(1)} fusion(bf16[64,8,8,128]{3,2,1,0:T(8,128)(2,1)S(1)} %bitcast.27), kind=kOutput, calls=%fused_computation.2 | convolution fusion | flops 537133056 | bytes 2097152 | tf_op jit(solution)/shard_map/dot_general | solution.py:103
  35.7 0.0 copy-done
  35.7 0.7 select_reduce_fusion
  36.4 0.3 fusion.6
  36.7 1.8 %divide_convert_fusion = bf16[512,1024]{1,0:T(8,128)(2,1)} fusion(f32[512]{0:T(512)S(1)} %fusion.6, bf16[64,8,8,128]{3,2,1,0:T(8,128)(2,1)S(1)} %bitcast.28, pred[512,512]{0,1:T(32,128)(4,1)S(1)} %get-tuple-element.13, f32[512,512]{0,1:T(8,128)S(1)} %convolution_multiply_fusion, f32[512]{0:T(512)S(1)} %get-tuple-element.12), kind=kOutput, calls=%fused_computation.1 | convolution fusion | flops 538705920 | bytes 3411968 | tf_op jit(solution)/shard_map/dot_general | solution.py:113
  38.4 0.0 copy-start.1
  38.4 6.9 %all-to-all-start.1 = ((bf16[16,32,1024]{2,1,0:T(8,128)(2,1)}), bf16[16,32,1024]{2,1,0:T(8,128)(2,1)S(1)}, u32[]{:S(2)}, u32[]{:S(2)}) async-start(bf16[16,32,1024]{2,1,0:T(8,128)(2,1)} %bitcast.10), calls=%async_computation.1 | async-start | bytes 2097152 | tf_op jit(solution)/shard_map/all_to_all | solution.py:173
  45.3 0.0 copy-done.1
  45.3 0.2 slice.16
  45.6 22.9 %all-to-all-done.1 = bf16[16,32,1024]{2,1,0:T(8,128)(2,1)S(1)} async-done(((bf16[16,32,1024]{2,1,0:T(8,128)(2,1)}), bf16[16,32,1024]{2,1,0:T(8,128)(2,1)S(1)}, u32[]{:S(2)}, u32[]{:S(2)}) %all-to-all-start.1) | async-done | bytes 1048608 | tf_op jit(solution)/shard_map/all_to_all | solution.py:173
  68.5 0.4 reshape.166
  68.9 0.3 convolution_convert_fusion
  69.3 1.0 %convert_element_type.30 = bf16[256,1024]{1,0:T(8,128)(2,1)} reshape(bf16[128,2048]{1,0:T(8,128)(2,1)S(1)} %convolution_convert_fusion) | data formatting | bytes 1048576 | tf_op jit(solution)/shard_map/convert_element_type | solution.py:177
  (7 shorter events, 0.1 us)
Async XLA Ops:
  2.6 31.6 %all-to-all-start = ((bf16[16,272,128]{2,1,0:T(8,128)(2,1)}), bf16[16,272,128]{2,1,0:T(8,128)(2,1)S(1)}, u32[]{:S(2)}, u32[]{:S(2)}) async-start(bf16[16,272,128]{2,1,0:T(8,128)(2,1)} %get-tuple-element.8), calls=%async_computation | async-start | bytes 2228224 | tf_op jit(solution)/shard_map/all_to_all | solution.py:135
  34.9 0.8 %copy-start = (s32[32,32]{1,0:T(8,128)S(1)}, s32[32,32]{1,0:T(8,128)}, u32[]{:S(2)}) copy-start(s32[32,32]{1,0:T(8,128)} %param.7) | copy-start | bytes 12292
  38.4 6.9 %copy-start.1 = (s32[1,256]{1,0:T(1,128)S(1)}, s32[1,256]{1,0:T(1,128)}, u32[]{:S(2)}) copy-start(s32[1,256]{1,0:T(1,128)} %get-tuple-element.7) | copy-start | bytes 3076
  38.4 30.1 %all-to-all-start.1 = ((bf16[16,32,1024]{2,1,0:T(8,128)(2,1)}), bf16[16,32,1024]{2,1,0:T(8,128)(2,1)S(1)}, u32[]{:S(2)}, u32[]{:S(2)}) async-start(bf16[16,32,1024]{2,1,0:T(8,128)(2,1)} %bitcast.10), calls=%async_computation.1 | async-start | bytes 2097152 | tf_op jit(solution)/shard_map/all_to_all | solution.py:173

commit v19 on v16

--- a/solution.py
+++ b/solution.py
@@ -159,13 +159,11 @@
         global_block[:, None] == jnp.arange(block_count, dtype=jnp.int32)[None, :]
     ).astype(jnp.bfloat16)
     cand_rows = jnp.dot(block_onehot, cand.astype(jnp.bfloat16), preferred_element_type=jnp.float32)
+    block_onehot_t = (
+        jnp.arange(block_count, dtype=jnp.int32)[:, None] == global_block[None, :]
+    ).astype(jnp.bfloat16)
     near = (
-        lax.dot_general(
-            cand_rows.astype(jnp.bfloat16),
-            block_onehot,
-            (((1,), (1,)), ((), ())),
-            preferred_element_type=jnp.float32,
-        )
+        jnp.dot(cand_rows.astype(jnp.bfloat16), block_onehot_t, preferred_element_type=jnp.float32)
         > 0.5
     )
     averaged = attend(held_emb, near, sub)

time: 70.8 us -> 70.8 us (level)
  no operation moved by 1% of the time
where the time goes in v19:
time: 70.8 us; the launch traced here: 70.5 us
  blocking collectives  31.8 us (45%)
  waiting for transfers between devices  24.3 us (34%)
  starting transfers between devices  7.31 us (10%)
  matrix products  3.49 us (5%)
  Pallas kernels  2.63 us (4%)
    all_to_all x1, blocking collectives, body(): lax.all_to_all(averaged, axes, split_axis=0, concat_axis=0, tiled=True)  31.8 us
    all_to_all x1, waiting for transfers between devices, body(): held = lax.all_to_all(send, axes, split_axis=0, concat_axis=0, tiled=True)  24.3 us
    all_to_all x1, starting transfers between devices, body(): held = lax.all_to_all(send, axes, split_axis=0, concat_axis=0, tiled=True)  7.31 us
    pallas_call x1, Pallas kernels, place(): pl.pallas_call(functools.partial(place_kernel, loop_count=loop_count, cap...  2.63 us
  transfers between devices with their start and end apart: 1, of which 1 were waited for; matrix products, arithmetic and copies ran while one was open for 0% of the time, Pallas kernels for 0%

profile of v19, /device:TPU:1, one launch (start us, length us, event | category | flops | bytes accessed | tf_op | source)
XLA Modules:
  0.0 70.5 jit_solution(16568702719411809250)
XLA Ops:
  0.0 2.6 %shard_map.46 = (bf16[16,272,128]{2,1,0:T(8,128)(2,1)}, s32[1,256]{1,0:T(1,128)}) custom-call(bf16[256,1024]{1,0:T(8,128)(2,1)} %emb_ref.1, s32[1,256]{1,0:T(1,128)} %bitcast.38, s32[1,256]{1,0:T(1,128)} %bitcast.39), custom_call_target="tpu_custom_call" | custom-call | flops 304087040 | bytes 1703936 | tf_op jit(solution)/shard_map/pallas_call | solution.py:86
  2.6 7.3 %all-to-all-start = ((bf16[16,272,128]{2,1,0:T(8,128)(2,1)}), bf16[16,272,128]{2,1,0:T(8,128)(2,1)S(1)}, u32[]{:S(2)}, u32[]{:S(2)}) async-start(bf16[16,272,128]{2,1,0:T(8,128)(2,1)} %get-tuple-element.8), calls=%async_computation | async-start | bytes 2228224 | tf_op jit(solution)/shard_map/all_to_all | solution.py:134
  9.9 24.3 %all-to-all-done = bf16[16,272,128]{2,1,0:T(8,128)(2,1)S(1)} async-done(((bf16[16,272,128]{2,1,0:T(8,128)(2,1)}), bf16[16,272,128]{2,1,0:T(8,128)(2,1)S(1)}, u32[]{:S(2)}, u32[]{:S(2)}) %all-to-all-start) | async-done | bytes 1114144 | tf_op jit(solution)/shard_map/all_to_all | solution.py:134
  34.3 0.1 slice.20
  34.4 0.3 copy.6
  34.7 0.1 reshape.204
  34.8 0.1 reshape.210
  34.9 0.0 copy-start.1
  34.9 0.8 %convolution_multiply_fusion = f32[512,512]{0,1:T(8,128)S(1)} fusion(bf16[64,8,8,128]{3,2,1,0:T(8,128)(2,1)S(1)} %bitcast.30), kind=kOutput, calls=%fused_computation.1 | convolution fusion | flops 537133056 | bytes 2097152 | tf_op jit(solution)/shard_map/dot_general | solution.py:103
  35.7 0.0 copy-done.1
  35.7 0.7 select_reduce_fusion
  36.4 0.3 fusion.6
  36.7 0.8 %divide_convert_fusion = bf16[512,1024]{1,0:T(8,128)(2,1)S(1)} fusion(f32[512]{0:T(512)S(1)} %fusion.6, bf16[64,8,8,128]{3,2,1,0:T(8,128)(2,1)S(1)} %bitcast.31, pred[512,512]{0,1:T(32,128)(4,1)S(1)} %get-tuple-element.16, f32[512,512]{0,1:T(8,128)S(1)} %convolution_multiply_fusion, f32[512]{0:T(512)S(1)} %get-tuple-element.15), kind=kOutput, calls=%fused_computation | convolution fusion | flops 538705920 | bytes 3411968 | tf_op jit(solution)/shard_map/dot_general | solution.py:113
  37.5 0.0 copy-start
  37.5 31.8 %all_to_all.17 = bf16[16,32,1024]{2,1,0:T(8,128)(2,1)S(1)} all-to-all(bf16[16,32,1024]{2,1,0:T(8,128)(2,1)S(1)} %bitcast.32), channel_id=1, replica_groups=mesh['groups'=2,'owner'=4,'loop'=4] {'loop','owner'}, dimensions={0} | all-to-all | bytes 2097152 | tf_op jit(solution)/shard_map/all_to_all | solution.py:170
  69.3 0.0 copy-done
  69.3 1.3 %convolution_convert_fusion = bf16[256,1024]{1,0:T(8,128)(2,1)} fusion(bf16[512,1024]{1,0:T(8,128)(2,1)S(1)} %bitcast.28, s32[256]{0:T(256)S(1)} %bitcast.37), kind=kOutput, calls=%fused_computation.2 | convolution fusion | flops 268828672 | bytes 1573888 | tf_op jit(solution)/shard_map/dot_general | solution.py:171
  (5 shorter events, 0.1 us)
Async XLA Ops:
  2.6 31.6 %all-to-all-start = ((bf16[16,272,128]{2,1,0:T(8,128)(2,1)}), bf16[16,272,128]{2,1,0:T(8,128)(2,1)S(1)}, u32[]{:S(2)}, u32[]{:S(2)}) async-start(bf16[16,272,128]{2,1,0:T(8,128)(2,1)} %get-tuple-element.8), calls=%async_computation | async-start | bytes 2228224 | tf_op jit(solution)/shard_map/all_to_all | solution.py:134
  34.9 0.8 %copy-start.1 = (s32[32,32]{1,0:T(8,128)S(1)}, s32[32,32]{1,0:T(8,128)}, u32[]{:S(2)}) copy-start(s32[32,32]{1,0:T(8,128)} %param.7) | copy-start | bytes 12292
  37.5 31.8 %copy-start = (s32[1,256]{1,0:T(1,128)S(1)}, s32[1,256]{1,0:T(1,128)}, u32[]{:S(2)}) copy-start(s32[1,256]{1,0:T(1,128)} %get-tuple-element.7) | copy-start | bytes 3076

commit v20 on v16

--- a/solution.py
+++ b/solution.py
@@ -55,9 +55,8 @@
         placing,
         (((1,), (1,)), ((), ())),
         preferred_element_type=jnp.float32,
-    ).astype(send_ref.dtype)
+    )
     body_rows = row_tiles * col_tiles * TILE
-    per_lanes = LABEL_COLUMNS // capacity
     for chunk in range(devices):
         base = chunk * capacity
         for a in range(row_tiles):
@@ -65,8 +64,12 @@
                 send_ref[chunk, (a * col_tiles + e) * TILE : (a * col_tiles + e + 1) * TILE, :] = placed[
                     base + a * TILE : base + (a + 1) * TILE, e * LABEL_COLUMNS : (e + 1) * LABEL_COLUMNS
                 ]
-        lanes = chunk // per_lanes * LABEL_COLUMNS
-        send_ref[chunk, body_rows : body_rows + 8, :] = placed_rows[:, lanes : lanes + LABEL_COLUMNS]
+        rolled = placed_rows
+        if chunk:
+            rolled = pltpu.roll(placed_rows, slots - base, 1)
+        send_ref[chunk, body_rows : body_rows + 8, :] = rolled[:, :LABEL_COLUMNS].astype(
+            send_ref.dtype
+        )
         send_ref[chunk, body_rows + 8 :, :] = jnp.zeros((TILE - 8, LABEL_COLUMNS), send_ref.dtype)
 
 
@@ -138,10 +141,7 @@
         body_rows = row_tiles * col_tiles * TILE
         held_emb = held[:, :body_rows].reshape(devices, row_tiles, col_tiles, TILE, LABEL_COLUMNS)
         held_emb = held_emb.transpose(0, 1, 3, 2, 4).reshape(slots, width)
-        per_lanes = LABEL_COLUMNS // capacity
-        lanes = held[:, body_rows : body_rows + 2, :].reshape(devices, 2, per_lanes, capacity)
-        me = lax.axis_index("loop") * owner_count + lax.axis_index("owner")
-        held_labels = lax.dynamic_index_in_dim(lanes, me % per_lanes, axis=2, keepdims=False)
+        held_labels = held[:, body_rows : body_rows + 2, :capacity]
         held_labels = held_labels.astype(jnp.int32).transpose(0, 2, 1).reshape(slots, 2)
     else:
         held_emb = held[:, :width]

time: 70.8 us -> 71.2 us (level)
  blocking collectives: 31.8 us -> 63.9 us
  waiting for transfers between devices: 24.3 us -> 0 us
  starting transfers between devices: 7.31 us -> 0 us
    all_to_all x0 -> x1, blocking collectives: none -> 35.5 us  [body(): held = lax.all_to_all(send, axes, split_axis=0, concat_axis=0, tiled=True)]
    all_to_all x1 -> x0, waiting for transfers between devices: 24.3 us -> none  [body(): held = lax.all_to_all(send, axes, split_axis=0, concat_axis=0, tiled=True)]
    all_to_all x1 -> x0, starting transfers between devices: 7.31 us -> none  [body(): held = lax.all_to_all(send, axes, split_axis=0, concat_axis=0, tiled=True)]
    all_to_all x1, blocking collectives: 31.8 us -> 28.4 us  [body(): lax.all_to_all(averaged, axes, split_axis=0, concat_axis=0, tiled=True)]
  transfers between devices with their start and end apart: 1 -> 0, of which waited for: 1 -> 0; matrix products, arithmetic and copies ran while one was open for 0% -> 0% of each run, Pallas kernels for 0% -> 0%
where the time goes in v20:
time: 71.2 us; the launch traced here: 70.9 us
  blocking collectives  63.9 us (90%)
  matrix products  3.49 us (5%)
  Pallas kernels  2.7 us (4%)
    all_to_all x1, blocking collectives, body(): held = lax.all_to_all(send, axes, split_axis=0, concat_axis=0, tiled=True)  35.5 us
    all_to_all x1, blocking collectives, body(): lax.all_to_all(averaged, axes, split_axis=0, concat_axis=0, tiled=True)  28.4 us
    pallas_call x1, Pallas kernels, place(): pl.pallas_call(functools.partial(place_kernel, loop_count=loop_count, cap...  2.7 us

profile of v20, /device:TPU:1, one launch (start us, length us, event | category | flops | bytes accessed | tf_op | source)
XLA Modules:
  0.0 70.9 jit_solution(262638566445665444)
XLA Ops:
  0.0 2.7 %shard_map.46 = (bf16[16,272,128]{2,1,0:T(8,128)(2,1)}, s32[1,256]{1,0:T(1,128)}) custom-call(bf16[256,1024]{1,0:T(8,128)(2,1)} %emb_ref.1, s32[1,256]{1,0:T(1,128)} %bitcast.31, s32[1,256]{1,0:T(1,128)} %bitcast.32), custom_call_target="tpu_custom_call" | custom-call | flops 304087040 | bytes 1703936 | tf_op jit(solution)/shard_map/pallas_call | solution.py:89
  2.7 35.5 %all_to_all.17 = bf16[16,272,128]{2,1,0:T(8,128)(2,1)S(1)} all-to-all(bf16[16,272,128]{2,1,0:T(8,128)(2,1)} %get-tuple-element.8), channel_id=1, replica_groups=mesh['groups'=2,'owner'=4,'loop'=4] {'loop','owner'}, dimensions={0} | all-to-all | bytes 2228224 | tf_op jit(solution)/shard_map/all_to_all | solution.py:137
  38.2 0.1 reshape.155
  38.3 0.1 slice.20
  38.4 0.3 copy.6
  38.7 0.0 copy-start.1
  38.7 0.7 %convolution_multiply_fusion = f32[512,512]{0,1:T(8,128)S(1)} fusion(bf16[64,8,8,128]{3,2,1,0:T(8,128)(2,1)S(1)} %bitcast.24), kind=kOutput, calls=%fused_computation.1 | convolution fusion | flops 537133056 | bytes 2097152 | tf_op jit(solution)/shard_map/dot_general | solution.py:106
  39.5 0.0 copy-done.1
  39.5 0.7 select_reduce_fusion
  40.2 0.3 fusion.6
  40.5 0.8 %divide_convert_fusion = bf16[512,1024]{1,0:T(8,128)(2,1)S(1)} fusion(f32[512]{0:T(512)S(1)} %fusion.6, bf16[64,8,8,128]{3,2,1,0:T(8,128)(2,1)S(1)} %bitcast.25, pred[512,512]{0,1:T(32,128)(4,1)S(1)} %get-tuple-element.13, f32[512,512]{0,1:T(8,128)S(1)} %convolution_multiply_fusion, f32[512]{0:T(512)S(1)} %get-tuple-element.12), kind=kOutput, calls=%fused_computation | convolution fusion | flops 538705920 | bytes 3411968 | tf_op jit(solution)/shard_map/dot_general | solution.py:116
  41.2 0.0 copy-start
  41.3 28.4 %all_to_all.18 = bf16[16,32,1024]{2,1,0:T(8,128)(2,1)S(1)} all-to-all(bf16[16,32,1024]{2,1,0:T(8,128)(2,1)S(1)} %bitcast.26), channel_id=1, replica_groups=mesh['groups'=2,'owner'=4,'loop'=4] {'loop','owner'}, dimensions={0} | all-to-all | bytes 2097152 | tf_op jit(solution)/shard_map/all_to_all | solution.py:172
  69.6 0.0 copy-done
  69.6 1.3 %convolution_convert_fusion = bf16[256,1024]{1,0:T(8,128)(2,1)} fusion(bf16[512,1024]{1,0:T(8,128)(2,1)S(1)} %bitcast.22, s32[256]{0:T(256)S(1)} %bitcast.30), kind=kOutput, calls=%fused_computation.2 | convolution fusion | flops 268828672 | bytes 1573888 | tf_op jit(solution)/shard_map/dot_general | solution.py:173
  (5 shorter events, 0.1 us)
Async XLA Ops:
  38.7 0.8 %copy-start.1 = (s32[32,32]{1,0:T(8,128)S(1)}, s32[32,32]{1,0:T(8,128)}, u32[]{:S(2)}) copy-start(s32[32,32]{1,0:T(8,128)} %param.7) | copy-start | bytes 12292
  41.2 28.4 %copy-start = (s32[1,256]{1,0:T(1,128)S(1)}, s32[1,256]{1,0:T(1,128)}, u32[]{:S(2)}) copy-start(s32[1,256]{1,0:T(1,128)} %get-tuple-element.7) | copy-start | bytes 3076
